TPU v7x, 128 devices: a whole 4x4x4 slice. The times are simulated.
128 devices in a mesh: req: 32 (over x, z, core), seq: 4 (over y).
Axes of the slice: x: 4, y: 4, z: 4, core: 2. Of those that a mesh axis runs over, the one named last changes fastest.
Arguments:
- xs: bfloat16 [16384, 8192], P(('req', 'seq')), may hold values from -6 to 6
- bc: bfloat16 [16384, 2048], P(('req', 'seq')), may hold values from -6 to 6
- zgate: bfloat16 [16384, 8192], P(('req', 'seq'))
- dt_raw: bfloat16 [16384, 128], P(('req', 'seq'))
- dt_bias: float32 [128], replicated
- a_log: float32 [128], replicated, may hold values from -0.5 to 1
- d_skip: float32 [128], replicated, may hold values from 0.5 to 1.5
- norm_gain: float32 [8192], replicated, may hold values from 0.1 to 1.9
- resid: bfloat16 [16384, 4096], P('req', 'seq')
- w_out: bfloat16 [8192, 4096], P('req'), may hold values from -0.0625 to 0.0625
- final_gain: float32 [4096], replicated, may hold values from 0.1 to 1.9
- head_weight: bfloat16 [4096, 32768], P(None, ('req', 'seq')), may hold values from -0.09375 to 0.09375
- lengths: int32 [32, 2], P('req'), may hold values from 1 to 511, as said below
Outputs:
- layer_out: bfloat16 [16384, 4096], P('req', 'seq')
- logits: float32 [64, 32768], P(None, ('req', 'seq'))
Inputs may be any that keep to these rules, and one draw needn't show every extreme that they name: Every request has at least one row; a group's lengths sum to at most 512, and to exactly 512 in at least two groups, where one request takes all but 2 - 1 rows.
All inputs are finite; a program needn't handle non-finite values.
Results may differ from a plain program's by a relative error of at most 0.013.
Values may be sent and summed in bfloat16 or wider, within the bound.
No kernel may reach another device: no remote copies, remote signals or barrier semaphores. Data moves between devices by JAX's collectives and lax.ppermute only.
A program may use at most 128 MiB of HBM per device.

v0:
```python
import jax
import jax.numpy as jnp
from jax import lax
from jax.sharding import PartitionSpec as P

SSM_CHANNEL_COUNT = 128
HEAD_DIM = 64
NGROUPS = 8
STATE = 128


def carried_in(value, axis, join, neutral):
    count, mine = (lax.axis_size(axis), lax.axis_index(axis))
    pieces = jax.tree.map(lambda part: lax.all_gather(part, axis), value)
    total = jax.tree.map(
        lambda part, zero: jnp.full_like(part, 0) + jnp.asarray(zero, part.dtype), value, neutral
    )

    def lap(position, total):
        longer = join(total, jax.tree.map(lambda part: part[position], pieces))
        return jax.tree.map(lambda new, old: jnp.where(position < mine, new, old), longer, total)

    return lax.fori_loop(0, count - 1, lap, total)


def split_halves(value):
    upper = value.astype(jnp.bfloat16)
    lower = (value - upper.astype(jnp.float32)).astype(jnp.bfloat16)
    return (upper, lower)


def group_inner(operands):
    cum_g, scores_g, inflow_g, x_g, allowed_mask = operands
    diff = cum_g[:, None, :] - cum_g[None, :, :]
    decay = jnp.where(allowed_mask[:, :, None], jnp.exp(jnp.minimum(diff, 0.0)), 0.0)
    weights = decay * scores_g[:, :, None] * inflow_g[None, :, :]
    upper, lower = split_halves(weights)
    first_part = jnp.einsum("tsk,skp->tkp", upper, x_g, preferred_element_type=jnp.float32)
    second_part = jnp.einsum("tsk,skp->tkp", lower, x_g, preferred_element_type=jnp.float32)
    return first_part + second_part


def block_terms(xb, bcb, dtb, segment, live, prev_seg, rate, d_skip):
    rows = xb.shape[0]
    per_group = SSM_CHANNEL_COUNT // NGROUPS
    x4 = xb.reshape(rows, NGROUPS, per_group, HEAD_DIM)
    bmat = bcb[:, : NGROUPS * STATE].reshape(rows, NGROUPS, STATE)
    cmat = bcb[:, NGROUPS * STATE :].reshape(rows, NGROUPS, STATE)
    livef = live.astype(jnp.float32)
    cum = jnp.cumsum(-rate[None, :] * dtb, axis=0)
    inflow = dtb * livef[:, None]
    index = jnp.arange(rows, dtype=jnp.int32)
    allowed_mask = (segment[:, None] == segment[None, :]) & (index[:, None] >= index[None, :])
    scores = jnp.einsum("tgn,sgn->gts", cmat, bmat, preferred_element_type=jnp.float32)
    cum_g = cum.reshape(rows, NGROUPS, per_group).transpose(1, 0, 2)
    inflow_g = inflow.reshape(rows, NGROUPS, per_group).transpose(1, 0, 2)
    x_g = x4.transpose(1, 0, 2, 3)
    allowed_all = jnp.broadcast_to(allowed_mask[None], (NGROUPS, rows, rows))
    y_groups = lax.map(group_inner, (cum_g, scores, inflow_g, x_g, allowed_all))
    y_inner = y_groups.transpose(1, 0, 2, 3)
    skip = d_skip.reshape(1, NGROUPS, per_group, 1) * x4.astype(jnp.float32)
    last_seg = segment[rows - 1]
    tail = (
        jnp.exp(cum[rows - 1][None, :] - cum)
        * (segment == last_seg).astype(jnp.float32)[:, None]
        * inflow
    )
    scaled = tail.reshape(rows, NGROUPS, per_group, 1) * x4.astype(jnp.float32)
    upper, lower = split_halves(scaled)
    state = jnp.einsum("sgkp,sgn->gkpn", upper, bmat, preferred_element_type=jnp.float32)
    state = state + jnp.einsum("sgkp,sgn->gkpn", lower, bmat, preferred_element_type=jnp.float32)
    keep = jnp.exp(cum[rows - 1]) * (last_seg == prev_seg).astype(jnp.float32)
    carry_w = jnp.exp(cum) * (segment == prev_seg).astype(jnp.float32)[:, None]
    return (y_inner + skip, keep, state.reshape(SSM_CHANNEL_COUNT, HEAD_DIM, STATE), carry_w, cmat)


def carry_term(arriving_vector, cmat, carry_w):
    rows = cmat.shape[0]
    per_group = SSM_CHANNEL_COUNT // NGROUPS
    state4 = arriving_vector.reshape(NGROUPS, per_group, HEAD_DIM, STATE)
    upper, lower = split_halves(state4)
    y_carry = jnp.einsum("tgn,gkpn->tgkp", cmat, upper, preferred_element_type=jnp.float32)
    y_carry = y_carry + jnp.einsum(
        "tgn,gkpn->tgkp", cmat, lower, preferred_element_type=jnp.float32
    )
    return y_carry * carry_w.reshape(rows, NGROUPS, per_group, 1)


def gate_norm(y, zgate, norm_gain):
    rows = y.shape[0]
    gated = y * jax.nn.silu(zgate.astype(jnp.float32))
    blocks = gated.reshape(rows, NGROUPS, -1)
    meansq = jnp.mean(blocks * blocks, axis=-1, keepdims=True)
    normed = (blocks * lax.rsqrt(meansq + 1e-05)).reshape(rows, -1) * norm_gain[None, :]
    return normed.astype(jnp.bfloat16)


def compose(earlier, later):
    keep_first, state_first = earlier
    keep_second, state_second = later
    return (keep_first * keep_second, keep_second[:, None, None] * state_first + state_second)


def on_device(
    xs,
    bc,
    zgate,
    dt_raw,
    dt_bias,
    a_log,
    d_skip,
    norm_gain,
    resid,
    w_out,
    final_gain,
    head_weight,
    lengths,
):
    rows = xs.shape[0]
    seq_count = lax.axis_size("seq")
    owner_count = lax.axis_size("req")
    place = lax.axis_index("seq")
    lens = lengths[0]
    slots = lens.shape[0]
    ends = jnp.cumsum(lens)
    first = place * rows
    positions = first + jnp.arange(rows, dtype=jnp.int32)
    segment = jnp.sum((positions[:, None] >= ends[None, :]).astype(jnp.int32), axis=1)
    live = segment < slots
    before = jnp.sum((first - 1 >= ends).astype(jnp.int32))
    prev_seg = jnp.where(place > 0, before, -1)
    rate = jnp.exp(a_log)
    steps_dt = jax.nn.softplus(dt_raw.astype(jnp.float32) + dt_bias[None, :])
    local, keep, state, carry_w, cmat = block_terms(
        xs, bc, steps_dt, segment, live, prev_seg, rate, d_skip
    )
    identity = (jnp.ones_like(keep), jnp.zeros_like(state))
    _, arriving_vector = carried_in((keep, state), "seq", compose, identity)
    y4 = (local + carry_term(arriving_vector, cmat, carry_w)) * live.astype(jnp.float32)[
        :, None, None, None
    ]
    gated = gate_norm(y4.reshape(rows, -1), zgate, norm_gain)
    group_rows = resid.shape[0]
    width = resid.shape[1]
    full_width = w_out.shape[1]
    share_rows = w_out.shape[0] // seq_count
    share = lax.dynamic_index_in_dim(
        w_out.reshape(seq_count, share_rows, full_width), place, 0, keepdims=False
    )
    split = gated.reshape(rows, owner_count, seq_count, share_rows)
    mine = lax.all_to_all(split, "seq", split_axis=2, concat_axis=0, tiled=True)
    mine = mine.reshape(seq_count * rows, owner_count * share_rows)
    partial_rows = jnp.dot(
        mine, lax.all_gather(share, "req", axis=0, tiled=True), preferred_element_type=jnp.float32
    )
    total = lax.psum_scatter(partial_rows, "seq", scatter_dimension=1, tiled=True)
    mixer = total.astype(jnp.bfloat16)
    layer_out = (resid.astype(jnp.float32) + mixer.astype(jnp.float32)).astype(jnp.bfloat16)
    group_pos = jnp.arange(group_rows, dtype=jnp.int32)
    picker = (group_pos[None, :] == (ends - 1)[:, None]).astype(jnp.bfloat16)
    picked_rows = jnp.dot(picker, layer_out, preferred_element_type=jnp.float32).astype(
        jnp.bfloat16
    )
    collected = lax.all_gather(picked_rows, ("req", "seq"), axis=0, tiled=True)
    owners_all = collected.shape[0] // (seq_count * slots)
    last_rows = collected.reshape(owners_all, seq_count, slots, width).transpose(0, 2, 1, 3)
    last_rows = last_rows.reshape(owners_all * slots, seq_count * width).astype(jnp.float32)
    meansq = jnp.mean(last_rows * last_rows, axis=-1, keepdims=True)
    normed = (last_rows * lax.rsqrt(meansq + 1e-05) * final_gain[None, :]).astype(jnp.bfloat16)
    logits = jnp.dot(normed, head_weight, preferred_element_type=jnp.float32)
    return (layer_out, logits)


def solution(mesh):
    placed = (
        P(("req", "seq"), None),
        P(("req", "seq"), None),
        P(("req", "seq"), None),
        P(("req", "seq"), None),
        P(),
        P(),
        P(),
        P(),
        P("req", "seq"),
        P("req", None),
        P(),
        P(None, ("req", "seq")),
        P("req", None),
    )
    return jax.shard_map(
        on_device,
        mesh=mesh,
        in_specs=placed,
        out_specs=(P("req", "seq"), P(None, ("req", "seq"))),
        check_vma=False,
    )
```

profile of v0, /device:TPU:1, one launch (start us, length us, event | category | flops | bytes accessed | tf_op | source)
XLA Modules:
  0.0 422.3 jit_solution(12641163578007681055)
XLA Ops:
  7.3 1.0 reduce-window.7
  8.3 0.6 broadcast_add_fusion
  9.0 0.6 slice.16
  10.2 0.7 compare_convert_fusion
  11.5 0.7 exponential_negate_fusion
  12.2 0.8 fusion.51
  13.0 0.2 reduce_window_sum.18
  13.2 0.5 slice_bitcast_fusion
  13.7 1.5 multiply_multiply_fusion.1
  15.2 0.1 copy.94
  15.3 4.1 copy.87
  19.4 0.2 copy.124
  19.6 2.5 fusion.40
  22.0 2.7 convolution_add_fusion.1
  24.9 0.8 constant_dynamic-slice_fusion
  25.8 0.1 copy.88
  25.9 0.2 copy.123
  26.1 0.1 copy.93
  26.2 4.2 copy.99
  30.4 8.8 %all-gather.1 = f32[4,1,128]{2,1,0:T(1,128)S(1)} all-gather(f32[1,1,128]{2,1,0:T(1,128)S(1)} %copy-done.13), channel_id=1, replica_groups=mesh['req'=32,'seq'=4] {'seq'}, dimensions={0}, use_global_device_ids=true | all-gather | bytes 2560 | tf_op jit(solution)/shard_map/all_gather | solution.py:14
  39.3 0.3 fusion.58
  39.6 15.7 %while.24 = (s32[]{:T(128)}, f32[8,128,16,64]{1,3,2,0:T(8,128)}, bf16[8,128,16,64]{1,3,2,0:T(8,128)(2,1)S(1)}, pred[8,128,128]{2,1,0:T(8,128)(4,1)S(1)}, f32[8,1...) while((s32[]{:T(128)}, f32[8,128,16,64]{1,3,2,0:T(8,128)}, ...), condition=%wide.region_4.5_spmd, body=%wide.region_3.4_spmd.sunk | while | flops 71172096 | bytes 2507877 | solution.py:59
  39.7 0.5 fusion.76
  40.2 1.4 fusion.77
  41.7 0.5 fusion.76
  42.2 1.4 fusion.77
  43.6 0.5 fusion.76
  44.2 1.4 fusion.77
  45.6 0.5 fusion.76
  46.2 1.4 fusion.77
  47.6 0.5 fusion.76
  48.1 1.4 fusion.77
  49.6 0.5 fusion.76
  50.1 1.4 fusion.77
  51.5 0.5 fusion.76
  52.1 1.4 fusion.77
  53.5 0.5 fusion.76
  54.0 1.4 fusion.77
  55.4 126.6 %all-gather.6.cloned.1.call-done = f32[4,128,64,128]{3,2,1,0:T(8,128)} async-done(((f32[1,128,64,128]{3,2,1,0:T(8,128)}), f32[4,128,64,128]{3,2,1,0:T(8,128)}) %all-gather.6.cloned.1.call-update) | async-done | bytes 16777232 | tf_op jit(solution)/shard_map/all_gather | solution.py:14
  182.0 17.4 %while.25 = (s32[]{:T(128)}, f32[128,64,128]{2,1,0:T(8,128)}, s32[]{:T(128)}, f32[4,128]{1,0:T(4,128)S(1)}, f32[4,128,64,128]{3,2,1,0:T(8,128)}, /*index=5*/s32[]{:T(128)}, s32[]{:T(128)}) while((s32[]{:T(128)}, f32[128,64,128]{2,1,0:T(8,128)}, s32[]{:T(128)}, f32[4,128]{1,0:T(4,128)S(1)}, f32[4,128,64,128]{3,2,1,0:T(8,128)}, ...), condition=%wide.region_7.8_spmd.clone, body=%wide.region_6.7_spmd.clone.sunk | while | flops 4194308 | bytes 12584553 | solution.py:23
  182.0 4.9 %fusion.78 = f32[128,64,128]{2,1,0:T(8,128)} fusion(f32[4,128,64,128]{3,2,1,0:T(8,128)} %get-tuple-element.310, s32[]{:T(128)} %get-tuple-element.299, f32[128,64,128]{2,1,0:T(8,128)} %get-tuple-element.300, f32[128]{0:T(128)S(1)} %dynamic-slice_bitcast_fusion.12, pred[]{:T(512)S(6)} %compare.3, pred[]{:T(512)S(6)} %lt.49), kind=kLoop, calls=%fused_computation.26.clone.1 | loop fusion | flops 4194304 | bytes 12583430 | tf_op jit(solution)/shard_map/while/body/eval_jaxpr/jit(_where)/select_n | solution.py:21
  186.9 6.1 %fusion.78 = f32[128,64,128]{2,1,0:T(8,128)} fusion(f32[4,128,64,128]{3,2,1,0:T(8,128)} %get-tuple-element.310, s32[]{:T(128)} %get-tuple-element.299, f32[128,64,128]{2,1,0:T(8,128)} %get-tuple-element.300, f32[128]{0:T(128)S(1)} %dynamic-slice_bitcast_fusion.12, pred[]{:T(512)S(6)} %compare.3, pred[]{:T(512)S(6)} %lt.49), kind=kLoop, calls=%fused_computation.26.clone.1 | loop fusion | flops 4194304 | bytes 12583430 | tf_op jit(solution)/shard_map/while/body/eval_jaxpr/jit(_where)/select_n | solution.py:21
  193.0 6.4 %fusion.78 = f32[128,64,128]{2,1,0:T(8,128)} fusion(f32[4,128,64,128]{3,2,1,0:T(8,128)} %get-tuple-element.310, s32[]{:T(128)} %get-tuple-element.299, f32[128,64,128]{2,1,0:T(8,128)} %get-tuple-element.300, f32[128]{0:T(128)S(1)} %dynamic-slice_bitcast_fusion.12, pred[]{:T(512)S(6)} %compare.3, pred[]{:T(512)S(6)} %lt.49), kind=kLoop, calls=%fused_computation.26.clone.1 | loop fusion | flops 4194304 | bytes 12583430 | tf_op jit(solution)/shard_map/while/body/eval_jaxpr/jit(_where)/select_n | solution.py:21
  199.4 3.0 fusion.44
  202.4 0.5 copy-done.2
  202.9 1.4 copy-done.7
  204.3 1.4 fusion.28
  205.7 0.2 copy-done.5
  205.9 1.5 bitcast_reduce_fusion
  207.4 1.9 fusion.34
  209.2 0.2 copy.100
  209.4 28.6 %all_to_all.15 = bf16[128,32,4,64]{0,3,1,2:T(8,128)(2,1)S(1)} all-to-all(bf16[128,32,4,64]{0,3,1,2:T(8,128)(2,1)S(1)} %copy.100), channel_id=1, replica_groups=mesh['req'=32,'seq'=4] {'seq'}, dimensions={2} | all-to-all | bytes 4194304 | tf_op jit(solution)/shard_map/all_to_all | solution.py:151
  238.0 3.3 copy.101
  241.3 17.8 %all-gather.8.cloned.1.call-done = bf16[1,2048,4096]{2,1,0:T(8,128)(2,1)} async-done(((bf16[1,64,4096]{2,1,0:T(8,128)(2,1)}), bf16[1,2048,4096]{2,1,0:T(8,128)(2,1)}) %all-gather.8.cloned.1.call-update) | async-done | bytes 16777232 | tf_op jit(solution)/shard_map/all_gather | solution.py:154
  259.1 15.1 %fusion.21 = f32[512,4096]{1,0:T(8,128)} fusion(bf16[1,2048,4096]{2,1,0:T(8,128)(2,1)} %all-gather.8.cloned.1.call-done, bf16[256,8,4,128]{3,2,1,0:T(4,128)(2,1)} %bitcast.146), kind=kOutput, calls=%fused_computation.28 | convolution fusion | flops 8589934592 | bytes 27262976 | tf_op jit(solution)/shard_map/dot_general | solution.py:153
  274.3 79.6 %reduce-scatter.2.cloned.1.call-done = f32[512,1024]{1,0:T(8,128)} async-done(((f32[512,4096]{1,0:T(8,128)}), f32[512,1024]{1,0:T(8,128)}) %reduce-scatter.2.cloned.1.call-update) | async-done | bytes 2097168 | tf_op jit(solution)/shard_map/reduce_scatter | solution.py:156
  353.9 1.9 add_convert_fusion
  355.9 0.3 fusion.42
  356.1 55.2 %all-gather.2 = bf16[128,2,1024]{2,1,0:T(2,128)(2,1)S(1)} all-gather(bf16[1,2,1024]{2,1,0:T(2,128)(2,1)S(1)} %fusion.42), channel_id=1, replica_groups=mesh['req'=32,'seq'=4] {'req','seq'}, dimensions={0}, use_global_device_ids=true | all-gather | bytes 528384 | tf_op jit(solution)/shard_map/all_gather | solution.py:164
  411.3 0.6 multiply_reduce_fusion
  412.0 0.3 copy.102
  412.3 0.6 copy.126
  413.0 0.1 rsqrt.21
  413.1 2.7 fusion.46
  (72 shorter events, 0.8 us)
Async XLA Ops:
  7.2 17.7 %copy-start = (bf16[256,4096]{1,0:T(8,128)(2,1)S(1)}, bf16[256,4096]{1,0:T(8,128)(2,1)}, u32[]{:S(2)}) copy-start(bf16[256,4096]{1,0:T(8,128)(2,1)} %param.26) | copy-start | bytes 6291460
  7.2 12.2 %copy-start.9 = (bf16[128,2048]{1,0:T(8,128)(2,1)S(1)}, bf16[128,2048]{1,0:T(8,128)(2,1)}, u32[]{:S(2)}) copy-start(bf16[128,2048]{1,0:T(8,128)(2,1)} %param.18) | copy-start | bytes 1572868
  7.2 174.8 %all-gather.6.cloned.1.call-start = ((), (), s32[]{:S(2)}) async-start(), calls=%async_computation.2 | async-start | bytes 20971520 | tf_op jit(solution)/shard_map/all_gather | solution.py:14
  19.6 2.5 copy-start.3
  24.8 1.3 copy-start.10
  24.8 1.4 copy-start.14
  24.8 5.6 %copy-start.13 = (f32[1,1,128]{2,1,0:T(1,128)S(1)}, f32[1,1,128]{2,1,0:T(1,128)}, u32[]{:S(2)}) copy-start(f32[1,1,128]{2,1,0:T(1,128)} %get-tuple-element.182) | copy-start | bytes 1540
  24.8 234.3 %all-gather.8.cloned.1.call-start = ((), (), s32[]{:S(2)}) async-start(), calls=%async_computation.4 | async-start | bytes 17301504 | tf_op jit(solution)/shard_map/all_gather | solution.py:154
  25.7 13.9 %copy-start.4 = (bf16[128,8192]{0,1:T(8,128)(2,1)S(1)}, bf16[128,8192]{0,1:T(8,128)(2,1)}, u32[]{:S(2)}) copy-start(bf16[128,8192]{0,1:T(8,128)(2,1)} %copy.87) | copy-start | bytes 6291460
  25.7 328.2 %reduce-scatter.2.cloned.1.call-start = ((), (), s32[]{:S(2)}) async-start(), calls=%async_computation.3 | async-start | bytes 10485760 | tf_op jit(solution)/shard_map/reduce_scatter | solution.py:156
  199.4 3.5 copy-start.2
  199.4 4.9 %copy-start.7 = (f32[8,128,16,64]{1,3,2,0:T(8,128)S(1)}, f32[8,128,16,64]{1,3,2,0:T(8,128)}, u32[]{:S(2)}) copy-start(f32[8,128,16,64]{1,3,2,0:T(8,128)} %get-tuple-element.133) | copy-start | bytes 12582916
  204.3 1.6 copy-start.5
  205.8 1.5 copy-start.11
  274.2 79.7 %copy-start.8 = (bf16[512,1024]{1,0:T(8,128)(2,1)S(1)}, bf16[512,1024]{1,0:T(8,128)(2,1)}, u32[]{:S(2)}) copy-start(bf16[512,1024]{1,0:T(8,128)(2,1)} %param.25) | copy-start | bytes 3145732
  274.2 138.8 %copy-start.12 = (f32[4096]{0:T(1024)S(1)}, f32[4096]{0:T(1024)}, u32[]{:S(2)}) copy-start(f32[4096]{0:T(1024)} %param.27) | copy-start | bytes 49156
  355.8 57.0 %copy-start.6 = (bf16[512,1024]{1,0:T(8,128)(2,1)}, bf16[512,1024]{1,0:T(8,128)(2,1)S(1)}, u32[]{:S(2)}) copy-start(bf16[512,1024]{1,0:T(8,128)(2,1)S(1)} %add_convert_fusion) | copy-start | bytes 3145732
  355.8 60.0 %copy-start.1 = (bf16[256,4096]{1,0:T(8,128)(2,1)S(1)}, bf16[256,4096]{1,0:T(8,128)(2,1)}, u32[]{:S(2)}) copy-start(bf16[256,4096]{1,0:T(8,128)(2,1)} %param.26) | copy-start | bytes 6291460
Sparse Core Ops, SparseCore 0:
  24.9 157.0 all-gather.5
  184.8 74.2 all-gather.7
  274.4 79.4 reduce-scatter.1
where the time goes:
time: 423 us; the launch traced here: 422 us
  waiting for transfers between devices  224 us (53%)
  blocking collectives  92.5 us (22%)
  matrix products  43.5 us (10%)
  other arithmetic  29.5 us (7%)
  local copies, waits for them, and re-layouts  17.1 us (4%)
  between operations  15.4 us (4%)
    all_gather x1, waiting for transfers between devices, carried_in(): pieces = jax.tree.map(lambda part: lax.all_gather(part, axis), value)  127 us
    reduce_scatter x1, waiting for transfers between devices, on_device(): lax.psum_scatter(partial_rows, 'seq', scatter_dimension=1, tiled=True)  79.6 us
    all_gather x1, blocking collectives, on_device(): collected = lax.all_gather(picked_rows, ('req', 'seq'), axis=0, tiled=True)  55.2 us
    all_to_all x1, blocking collectives, on_device(): mine = lax.all_to_all(split, 'seq', split_axis=2, concat_axis=0, tiled=True)  28.6 us
    all_gather x1, waiting for transfers between devices, on_device(): lax.all_gather(share, 'req', axis=0, tiled=True)  17.8 us
    select_n x3, other arithmetic, lap(): jnp.where(position < mine, new, old)  17.4 us
    dot_general x1, matrix products, on_device(): jnp.dot(mine, lax.all_gather(share, 'req', axis=0, tiled=True), preferred...  15.1 us
    unnamed x35, local copies, waits for them, and re-layouts  11.2 us
  transfers between devices with their start and end apart: 3, of which 3 were waited for; matrix products, arithmetic and copies ran while one was open for 12% of the time, Pallas kernels for 0%

commit v1 on v0

v1 whole, which is shorter than its diff:
```python
import jax
import jax.numpy as jnp
from jax import lax
from jax.sharding import PartitionSpec as P

SSM_CHANNEL_COUNT = 128
HEAD_DIM = 64
NGROUPS = 8
STATE = 128


def split_halves(value):
    upper = value.astype(jnp.bfloat16)
    lower = (value - upper.astype(jnp.float32)).astype(jnp.bfloat16)
    return (upper, lower)


def group_inner(operands):
    cum_g, scores_g, inflow_g, x_g, allowed_mask = operands
    diff = cum_g[:, None, :] - cum_g[None, :, :]
    decay = jnp.where(allowed_mask[:, :, None], jnp.exp(jnp.minimum(diff, 0.0)), 0.0)
    weights = decay * scores_g[:, :, None] * inflow_g[None, :, :]
    upper, lower = split_halves(weights)
    first_part = jnp.einsum("tsk,skp->tkp", upper, x_g, preferred_element_type=jnp.float32)
    second_part = jnp.einsum("tsk,skp->tkp", lower, x_g, preferred_element_type=jnp.float32)
    return first_part + second_part


def block_terms(xb, bb, cb, dtb, segment, live, prev_seg, rate, d_skip, groups):
    rows = xb.shape[0]
    heads = rate.shape[0]
    per_group = heads // groups
    x4 = xb.reshape(rows, groups, per_group, HEAD_DIM)
    bmat = bb.reshape(rows, groups, STATE)
    cmat = cb.reshape(rows, groups, STATE)
    livef = live.astype(jnp.float32)
    cum = jnp.cumsum(-rate[None, :] * dtb, axis=0)
    inflow = dtb * livef[:, None]
    index = jnp.arange(rows, dtype=jnp.int32)
    allowed_mask = (segment[:, None] == segment[None, :]) & (index[:, None] >= index[None, :])
    scores = jnp.einsum("tgn,sgn->gts", cmat, bmat, preferred_element_type=jnp.float32)
    cum_g = cum.reshape(rows, groups, per_group).transpose(1, 0, 2)
    inflow_g = inflow.reshape(rows, groups, per_group).transpose(1, 0, 2)
    x_g = x4.transpose(1, 0, 2, 3)
    allowed_all = jnp.broadcast_to(allowed_mask[None], (groups, rows, rows))
    y_groups = lax.map(group_inner, (cum_g, scores, inflow_g, x_g, allowed_all))
    y_inner = y_groups.transpose(1, 0, 2, 3)
    skip = d_skip.reshape(1, groups, per_group, 1) * x4.astype(jnp.float32)
    last_seg = segment[rows - 1]
    tail = (
        jnp.exp(cum[rows - 1][None, :] - cum)
        * (segment == last_seg).astype(jnp.float32)[:, None]
        * inflow
    )
    scaled = tail.reshape(rows, groups, per_group, 1) * x4.astype(jnp.float32)
    upper, lower = split_halves(scaled)
    state = jnp.einsum("sgkp,sgn->gkpn", upper, bmat, preferred_element_type=jnp.float32)
    state = state + jnp.einsum("sgkp,sgn->gkpn", lower, bmat, preferred_element_type=jnp.float32)
    keep = jnp.exp(cum[rows - 1]) * (last_seg == prev_seg).astype(jnp.float32)
    carry_w = jnp.exp(cum) * (segment == prev_seg).astype(jnp.float32)[:, None]
    return (y_inner + skip, keep, state.reshape(heads, HEAD_DIM, STATE), carry_w, cmat)


def carry_term(arriving_vector, cmat, carry_w, groups):
    rows = cmat.shape[0]
    heads = arriving_vector.shape[0]
    per_group = heads // groups
    state4 = arriving_vector.reshape(groups, per_group, HEAD_DIM, STATE)
    upper, lower = split_halves(state4)
    y_carry = jnp.einsum("tgn,gkpn->tgkp", cmat, upper, preferred_element_type=jnp.float32)
    y_carry = y_carry + jnp.einsum(
        "tgn,gkpn->tgkp", cmat, lower, preferred_element_type=jnp.float32
    )
    return y_carry * carry_w.reshape(rows, groups, per_group, 1)


def gate_norm(y, zgate, norm_gain, groups):
    rows = y.shape[0]
    gated = y * jax.nn.silu(zgate.astype(jnp.float32))
    blocks = gated.reshape(rows, groups, -1)
    meansq = jnp.mean(blocks * blocks, axis=-1, keepdims=True)
    normed = (blocks * lax.rsqrt(meansq + 1e-05)).reshape(rows, -1) * norm_gain[None, :]
    return normed.astype(jnp.bfloat16)


def on_device(
    xs,
    bc,
    zgate,
    dt_raw,
    dt_bias,
    a_log,
    d_skip,
    norm_gain,
    resid,
    w_out,
    final_gain,
    head_weight,
    lengths,
):
    rows = xs.shape[0]
    inner = xs.shape[1]
    seq_count = lax.axis_size("seq")
    place = lax.axis_index("seq")
    heads_all = a_log.shape[0]
    heads = heads_all // seq_count
    groups = NGROUPS // seq_count
    share = inner // seq_count
    bshare = groups * STATE
    group_rows = rows * seq_count

    bpart = bc[:, : NGROUPS * STATE].reshape(rows, seq_count, bshare)
    cpart = bc[:, NGROUPS * STATE :].reshape(rows, seq_count, bshare)
    packed = jnp.concatenate(
        [
            xs.reshape(rows, seq_count, share),
            zgate.reshape(rows, seq_count, share),
            bpart,
            cpart,
            dt_raw.reshape(rows, seq_count, heads),
        ],
        axis=2,
    )
    moved = lax.all_to_all(packed, "seq", split_axis=1, concat_axis=0, tiled=True)
    moved = moved.reshape(group_rows, -1)
    xg = moved[:, :share]
    zg = moved[:, share : 2 * share]
    bg = moved[:, 2 * share : 2 * share + bshare]
    cg = moved[:, 2 * share + bshare : 2 * share + 2 * bshare]
    dg = moved[:, 2 * share + 2 * bshare :]

    my_heads = lambda v: lax.dynamic_slice_in_dim(v, place * heads, heads)
    rate = jnp.exp(my_heads(a_log))
    skipw = my_heads(d_skip)
    steps_dt = jax.nn.softplus(dg.astype(jnp.float32) + my_heads(dt_bias)[None, :])

    lens = lengths[0]
    slots = lens.shape[0]
    ends = jnp.cumsum(lens)
    positions = jnp.arange(group_rows, dtype=jnp.int32)
    segment = jnp.sum((positions[:, None] >= ends[None, :]).astype(jnp.int32), axis=1)
    live = segment < slots

    state_in = jnp.zeros((heads, HEAD_DIM, STATE), jnp.float32)
    prev_seg = jnp.array(-1, jnp.int32)
    ys = []
    for chunk in range(seq_count):
        lo, hi = chunk * rows, (chunk + 1) * rows
        local, keep, state, carry_w, cmat = block_terms(
            xg[lo:hi], bg[lo:hi], cg[lo:hi], steps_dt[lo:hi], segment[lo:hi], live[lo:hi],
            prev_seg, rate, skipw, groups,
        )
        y4 = (local + carry_term(state_in, cmat, carry_w, groups)) * live[lo:hi].astype(
            jnp.float32
        )[:, None, None, None]
        ys.append(y4.reshape(rows, share))
        state_in = keep[:, None, None] * state_in + state
        prev_seg = segment[hi - 1]
    y = jnp.concatenate(ys, axis=0)
    gain = lax.dynamic_slice_in_dim(norm_gain, place * share, share)
    gated = gate_norm(y, zg, gain, groups)

    width = resid.shape[1]
    w_cols = lax.dynamic_slice_in_dim(w_out, place * width, width, axis=1)
    w_full = lax.all_gather(w_cols, "req", axis=0, tiled=True)
    gated_all = lax.all_gather(gated, "seq", axis=1, tiled=True)
    mixer = jnp.dot(gated_all, w_full, preferred_element_type=jnp.float32).astype(jnp.bfloat16)
    layer_out = (resid.astype(jnp.float32) + mixer.astype(jnp.float32)).astype(jnp.bfloat16)

    group_pos = jnp.arange(group_rows, dtype=jnp.int32)
    picker = (group_pos[None, :] == (ends - 1)[:, None]).astype(jnp.bfloat16)
    picked_rows = jnp.dot(picker, layer_out, preferred_element_type=jnp.float32).astype(
        jnp.bfloat16
    )
    collected = lax.all_gather(picked_rows, ("req", "seq"), axis=0, tiled=True)
    owners_all = collected.shape[0] // (seq_count * slots)
    last_rows = collected.reshape(owners_all, seq_count, slots, width).transpose(0, 2, 1, 3)
    last_rows = last_rows.reshape(owners_all * slots, seq_count * width).astype(jnp.float32)
    meansq = jnp.mean(last_rows * last_rows, axis=-1, keepdims=True)
    normed = (last_rows * lax.rsqrt(meansq + 1e-05) * final_gain[None, :]).astype(jnp.bfloat16)
    logits = jnp.dot(normed, head_weight, preferred_element_type=jnp.float32)
    return (layer_out, logits)


def solution(mesh):
    placed = (
        P(("req", "seq"), None),
        P(("req", "seq"), None),
        P(("req", "seq"), None),
        P(("req", "seq"), None),
        P(),
        P(),
        P(),
        P(),
        P("req", "seq"),
        P("req", None),
        P(),
        P(None, ("req", "seq")),
        P("req", None),
    )
    return jax.shard_map(
        on_device,
        mesh=mesh,
        in_specs=placed,
        out_specs=(P("req", "seq"), P(None, ("req", "seq"))),
        check_vma=False,
    )
```

time: 423 us -> 429 us (1.014)
  local copies, waits for them, and re-layouts: 17.1 us -> 71.9 us
  blocking collectives: 92.5 us -> 54.6 us
  waiting for transfers between devices: 224 us -> 206 us
  other arithmetic: 29.5 us -> 20.6 us
  matrix products: 43.5 us -> 50.2 us
  starting transfers between devices: 0.12 us -> 5.21 us
    reduce_scatter x1 -> x0, waiting for transfers between devices: 79.6 us -> none  [on_device(): lax.psum_scatter(partial_rows, 'seq', scatter_dimension=1, tiled=True)]
    all_to_all x0 -> x1, waiting for transfers between devices: none -> 45.6 us  [on_device(): lax.all_to_all(packed, 'seq', split_axis=1, concat_axis=0, tiled=True)]
    all_to_all x1 -> x0, blocking collectives: 28.6 us -> none  [on_device(): mine = lax.all_to_all(split, 'seq', split_axis=2, concat_axis=0, tiled=True)]
    select_n x3 -> x1, other arithmetic: 17.4 us -> 0.11 us  [on_device(): jax.nn.softplus(dg.astype(jnp.float32) + my_heads(dt_bias)[None, :])]
    all_gather x2, waiting for transfers between devices: 144 us -> 160 us  [the longest x1 83.4 us: on_device(): gated_all = lax.all_gather(gated, 'seq', axis=1, tiled=True)]
    all_to_all x1, local copies, waits for them, and re-layouts: 3.31 us -> 18.4 us  [on_device(): lax.all_to_all(packed, 'seq', split_axis=1, concat_axis=0, tiled=True)]
    all_gather x1 -> x0, blocking collectives: 8.76 us -> none  [carried_in(): pieces = jax.tree.map(lambda part: lax.all_gather(part, axis), value)]
    unnamed x35 -> x93, local copies, waits for them, and re-layouts: 11.2 us -> 18.8 us
  transfers between devices with their start and end apart: 3 -> 3, of which waited for: 3 -> 3; matrix products, arithmetic and copies ran while one was open for 12% -> 2% of each run, Pallas kernels for 0% -> 0%
where the time goes in v1:
time: 429 us; the launch traced here: 426 us
  waiting for transfers between devices  206 us (48%)
  local copies, waits for them, and re-layouts  71.9 us (17%)
  blocking collectives  54.6 us (13%)
  matrix products  50.2 us (12%)
  other arithmetic  20.6 us (5%)
  between operations  17.7 us (4%)
  starting transfers between devices  5.21 us (1%)
    all_gather x1, waiting for transfers between devices, on_device(): gated_all = lax.all_gather(gated, 'seq', axis=1, tiled=True)  83.4 us
    all_gather x1, waiting for transfers between devices, on_device(): w_full = lax.all_gather(w_cols, 'req', axis=0, tiled=True)  77.1 us
    all_gather x1, blocking collectives, on_device(): collected = lax.all_gather(picked_rows, ('req', 'seq'), axis=0, tiled=True)  54.6 us
    all_to_all x1, waiting for transfers between devices, on_device(): lax.all_to_all(packed, 'seq', split_axis=1, concat_axis=0, tiled=True)  45.6 us
    unnamed x93, local copies, waits for them, and re-layouts  18.8 us
    all_to_all x1, local copies, waits for them, and re-layouts, on_device(): lax.all_to_all(packed, 'seq', split_axis=1, concat_axis=0, tiled=True)  18.4 us
    dot_general x8, matrix products, group_inner(): jnp.einsum('tsk,skp->tkp', lower, x_g, preferred_element_type=jnp.float32)  14.9 us
    dot_general x1, matrix products, on_device(): jnp.dot(gated_all, w_full, preferred_element_type=jnp.float32)  14.8 us
  transfers between devices with their start and end apart: 3, of which 3 were waited for; matrix products, arithmetic and copies ran while one was open for 2% of the time, Pallas kernels for 0%

profile of v1, /device:TPU:1, one launch (start us, length us, event | category | flops | bytes accessed | tf_op | source)
XLA Modules:
  0.0 426.3 jit_solution(4121959781990282691)
XLA Ops:
  7.2 1.2 fusion.158
  8.6 4.1 copy.339
  12.6 3.3 constant_dynamic-update-slice_fusion.4
  16.0 4.1 copy.340
  20.3 3.3 constant_dynamic-update-slice_fusion.3
  23.6 0.8 constant_dynamic-update-slice_fusion.2
  24.4 0.7 constant_dynamic-update-slice_fusion.1
  25.7 5.1 %all-to-all-start = ((bf16[128,4,4640]{0,2,1:T(8,128)(2,1)}), bf16[128,4,4640]{0,2,1:T(8,128)(2,1)}, u32[]{:S(2)}, u32[]{:S(2)}) async-start(bf16[128,4,4640]{0,2,1:T(8,128)(2,1)} %constant_dynamic-update-slice_fusion), calls=%async_computation | async-start | bytes 9502720 | tf_op jit(solution)/shard_map/all_to_all | solution.py:124
  36.4 2.5 compare_convert_fusion.7
  40.3 45.6 %all-to-all-done = bf16[128,4,4640]{0,2,1:T(8,128)(2,1)} async-done(((bf16[128,4,4640]{0,2,1:T(8,128)(2,1)}), bf16[128,4,4640]{0,2,1:T(8,128)(2,1)}, u32[]{:S(2)}, u32[]{:S(2)}) %all-to-all-start) | async-done | bytes 4751392 | tf_op jit(solution)/shard_map/all_to_all | solution.py:124
  85.9 18.4 %copy.344 = bf16[4,128,1,4640]{1,0,3,2:T(4,128)(2,1)S(1)} copy(bf16[4,128,1,4640]{1,3,0,2:T(8,128)(2,1)} %bitcast.34) | data formatting | bytes 9502720 | tf_op jit(solution)/shard_map/all_to_all | solution.py:124
  104.3 0.8 copy.436
  105.2 0.9 fusion.156
  106.1 1.8 fusion.157
  109.4 0.7 copy.359
  110.8 1.0 reduce_window_sum.38
  111.9 1.0 multiply_reduce_fusion.3
  112.9 1.0 reduce_window_sum.39
  114.6 1.6 reduce_window_sum.40
  116.2 1.5 copy.360
  117.7 1.3 multiply_reduce_fusion.1
  119.0 1.1 fusion.162
  120.1 1.5 multiply_multiply_fusion.6
  121.6 1.3 broadcast_in_dim.69
  123.0 1.1 broadcast.234.clone.3
  124.1 6.7 %while.40 = (s32[]{:T(128)}, f32[2,128,16,64]{1,3,2,0:T(8,128)}, bf16[2,128,16,64]{1,3,2,0:T(8,128)(2,1)S(1)}, pred[2,128,128]{2,1,0:T(8,128)(4,1)}, f32[2,128,1...) while((s32[]{:T(128)}, f32[2,128,16,64]{1,3,2,0:T(8,128)}, ...), condition=%wide.region_4.5_spmd, body=%wide.region_3.4_spmd.sunk | while | flops 71172096 | bytes 2507877 | solution.py:46
  126.0 1.4 fusion.216
  129.4 1.4 fusion.216
  130.8 1.0 fusion.163
  131.8 0.7 broadcast_in_dim.70
  132.6 1.1 broadcast.234.clone.2
  133.7 9.1 %while.41 = (s32[]{:T(128)}, f32[2,128,16,64]{1,3,2,0:T(8,128)}, bf16[2,128,16,64]{1,3,2,0:T(8,128)(2,1)}, pred[2,128,128]{2,1,0:T(8,128)(4,1)S(1)}, f32[2,128,1...) while((s32[]{:T(128)}, f32[2,128,16,64]{1,3,2,0:T(8,128)}, ...), condition=%wide.region_7.8_spmd, body=%wide.region_6.7_spmd.sunk | while | flops 71172096 | bytes 2508385 | solution.py:46
  134.5 1.5 fusion.220
  136.0 2.3 fusion.221
  139.0 1.5 fusion.220
  140.5 2.3 fusion.221
  142.9 1.3 mul.497
  144.3 0.7 broadcast_in_dim.72
  145.1 1.1 broadcast.234.clone.1
  146.2 5.3 %while.42 = (s32[]{:T(128)}, f32[2,128,16,64]{1,3,2,0:T(8,128)}, bf16[2,128,16,64]{1,3,2,0:T(8,128)(2,1)S(1)}, pred[2,128,128]{2,1,0:T(8,128)(4,1)S(1)}, f32[2,1...) while((s32[]{:T(128)}, f32[2,128,16,64]{1,3,2,0:T(8,128)}, ...), condition=%wide.region_10.11_spmd, body=%wide.region_9.10_spmd.sunk | while | flops 71172096 | bytes 2507877 | solution.py:46
  147.4 1.4 fusion.226
  150.1 1.4 fusion.226
  153.0 1.0 fusion.165
  154.1 1.3 broadcast_in_dim.73
  155.4 1.1 broadcast.234.clone
  156.6 10.6 %while.43 = (s32[]{:T(128)}, f32[2,128,16,64]{1,3,2,0:T(8,128)}, bf16[2,128,16,64]{1,3,2,0:T(8,128)(2,1)}, pred[2,128,128]{2,1,0:T(8,128)(4,1)}, f32[2,128,16]{1...) while((s32[]{:T(128)}, f32[2,128,16,64]{1,3,2,0:T(8,128)}, ...), condition=%wide.region_13.14_spmd, body=%wide.region_12.13_spmd.sunk | while | flops 71172096 | bytes 2508385 | solution.py:46
  158.0 1.5 fusion.230
  159.5 2.3 fusion.231
  163.2 1.5 fusion.230
  164.7 2.4 fusion.231
  167.1 1.2 mul.538
  168.3 1.4 exponential_multiply_fusion
  169.8 1.6 copy.377
  171.4 0.7 exponential_multiply_fusion.3
  172.1 1.2 fusion.134
  173.3 1.2 fusion.104
  179.3 2.6 bitcast_reduce_fusion
  182.0 1.8 fusion.85
  183.9 0.8 constant_dynamic-slice_fusion
  184.8 83.4 %all-gather.4.cloned.1.call-done = bf16[512,8192]{0,1:T(8,128)(2,1)} async-done(((bf16[512,2048]{0,1:T(8,128)(2,1)}), bf16[512,8192]{0,1:T(8,128)(2,1)}) %all-gather.4.cloned.1.call-update) | async-done | bytes 8388624 | tf_op jit(solution)/shard_map/all_gather | solution.py:166
  268.2 77.1 %all-gather.6.cloned.1.call-done = bf16[8192,1024]{1,0:T(8,128)(2,1)} async-done(((bf16[256,1024]{1,0:T(8,128)(2,1)}), bf16[8192,1024]{1,0:T(8,128)(2,1)}) %all-gather.6.cloned.1.call-update) | async-done | bytes 16777232 | tf_op jit(solution)/shard_map/all_gather | solution.py:165
  345.2 14.8 %add_convert_fusion = bf16[512,1024]{1,0:T(8,128)(2,1)S(1)} fusion(bf16[512,1024]{1,0:T(8,128)(2,1)S(1)} %copy-done.37, bf16[512,8192]{0,1:T(8,128)(2,1)} %all-gather.4.cloned.1.call-done, bf16[8192,1024]{1,0:T(8,128)(2,1)} %all-gather.6.cloned.1.call-done), kind=kOutput, calls=%fused_computation.111 | convolution fusion | flops 8592556032 | bytes 27262976 | tf_op jit(solution)/shard_map/dot_general | solution.py:167
  360.4 54.6 %all-gather = bf16[128,2,1024]{2,1,0:T(2,128)(2,1)S(1)} all-gather(bf16[1,2,1024]{2,1,0:T(2,128)(2,1)S(1)} %fusion.111), channel_id=1, replica_groups=mesh['req'=32,'seq'=4] {'req','seq'}, dimensions={0}, use_global_device_ids=true | all-gather | bytes 528384 | tf_op jit(solution)/shard_map/all_gather | solution.py:175
  416.7 2.7 fusion.118
  (166 shorter events, 27.1 us)
Async XLA Ops:
  7.2 176.8 %copy-start = (bf16[256,4096]{1,0:T(8,128)(2,1)S(1)}, bf16[256,4096]{1,0:T(8,128)(2,1)}, u32[]{:S(2)}) copy-start(bf16[256,4096]{1,0:T(8,128)(2,1)} %param.30) | copy-start | bytes 6291460
  12.6 7.5 %copy-start.23 = (bf16[128,128]{1,0:T(8,128)(2,1)S(1)}, bf16[128,128]{1,0:T(8,128)(2,1)}, u32[]{:S(2)}) copy-start(bf16[128,128]{1,0:T(8,128)(2,1)} %param.24) | copy-start | bytes 98308
  25.7 5.2 %copy-start.38 = (s32[1,2]{1,0:T(1,128)S(1)}, s32[1,2]{1,0:T(1,128)}, u32[]{:S(2)}) copy-start(s32[1,2]{1,0:T(1,128)} %param.33) | copy-start | bytes 28
  25.7 9.1 %copy-start.39 = (f32[128]{0:T(128)S(1)}, f32[128]{0:T(128)}, u32[]{:S(2)}) copy-start(f32[128]{0:T(128)} %param.25) | copy-start | bytes 1540
  25.7 9.2 %copy-start.40 = (f32[128]{0:T(128)S(1)}, f32[128]{0:T(128)}, u32[]{:S(2)}) copy-start(f32[128]{0:T(128)} %param.27) | copy-start | bytes 1540
  25.7 10.0 %copy-start.41 = (f32[128]{0:T(128)S(1)}, f32[128]{0:T(128)}, u32[]{:S(2)}) copy-start(f32[128]{0:T(128)} %param.26) | copy-start | bytes 1540
  25.7 60.2 %all-to-all-start = ((bf16[128,4,4640]{0,2,1:T(8,128)(2,1)}), bf16[128,4,4640]{0,2,1:T(8,128)(2,1)}, u32[]{:S(2)}, u32[]{:S(2)}) async-start(bf16[128,4,4640]{0,2,1:T(8,128)(2,1)} %constant_dynamic-update-slice_fusion), calls=%async_computation | async-start | bytes 9502720 | tf_op jit(solution)/shard_map/all_to_all | solution.py:124
  30.9 237.3 %all-gather.4.cloned.1.call-start = ((), (), s32[]{:S(2)}) async-start(), calls=%async_computation.1 | async-start | bytes 10485760 | tf_op jit(solution)/shard_map/all_gather | solution.py:166
  31.1 73.2 %copy-start.34 = (s32[2,1]{0,1:T(1,128)}, s32[2,1]{0,1:T(1,128)S(1)}, u32[]{:S(2)}) copy-start(s32[2,1]{0,1:T(1,128)S(1)} %reduce-window.7) | copy-start | bytes 28
  105.2 2.7 copy-start.1
  106.1 24.7 %copy-start.8 = (bf16[128,256]{0,1:T(8,128)(2,1)}, bf16[128,256]{0,1:T(8,128)(2,1)S(1)}, u32[]{:S(2)}) copy-start(bf16[128,256]{0,1:T(8,128)(2,1)S(1)} %get-tuple-element.281) | copy-start | bytes 196612
  106.1 38.1 %copy-start.10 = (bf16[128,256]{0,1:T(8,128)(2,1)}, bf16[128,256]{0,1:T(8,128)(2,1)S(1)}, u32[]{:S(2)}) copy-start(bf16[128,256]{0,1:T(8,128)(2,1)S(1)} %get-tuple-element.278) | copy-start | bytes 196612
  108.0 11.0 %copy-start.15 = (f32[512,32]{0,1:T(8,128)}, f32[512,32]{0,1:T(8,128)S(1)}, u32[]{:S(2)}) copy-start(f32[512,32]{0,1:T(8,128)S(1)} %compare_select_fusion) | copy-start | bytes 196612
  133.7 12.4 %copy-start.17 = (f32[128,32]{0,1:T(8,128)S(1)}, f32[128,32]{0,1:T(8,128)}, u32[]{:S(2)}) copy-start(f32[128,32]{0,1:T(8,128)} %copy.360) | copy-start | bytes 49156
  146.2 5.3 %copy-start.36 = (f32[32]{0:T(128)S(1)}, f32[32]{0:T(128)}, u32[]{:S(2)}) copy-start(f32[32]{0:T(128)} %get-tuple-element.325) | copy-start | bytes 388
  146.2 5.9 %copy-start.22 = (f32[128,32]{0,1:T(8,128)S(1)}, f32[128,32]{0,1:T(8,128)}, u32[]{:S(2)}) copy-start(f32[128,32]{0,1:T(8,128)} %get-tuple-element.289) | copy-start | bytes 49156
  167.1 7.4 %copy-start.9 = (bf16[128,256]{0,1:T(8,128)(2,1)S(1)}, bf16[128,256]{0,1:T(8,128)(2,1)}, u32[]{:S(2)}) copy-start(bf16[128,256]{0,1:T(8,128)(2,1)} %copy-done.8) | copy-start | bytes 196612
  169.8 5.0 %copy-start.12 = (bf16[128,256]{0,1:T(8,128)(2,1)S(1)}, bf16[128,256]{0,1:T(8,128)(2,1)}, u32[]{:S(2)}) copy-start(bf16[128,256]{0,1:T(8,128)(2,1)} %get-tuple-element.280) | copy-start | bytes 196612
  169.8 5.0 %copy-start.20 = (f32[128,32]{0,1:T(8,128)S(1)}, f32[128,32]{0,1:T(8,128)}, u32[]{:S(2)}) copy-start(f32[128,32]{0,1:T(8,128)} %get-tuple-element.300) | copy-start | bytes 49156
  169.8 5.3 %copy-start.32 = (f32[2,16]{1,0:T(2,128)S(1)}, f32[2,16]{1,0:T(2,128)}, u32[]{:S(2)}) copy-start(f32[2,16]{1,0:T(2,128)} %mul.517) | copy-start | bytes 388
  171.4 3.4 copy-start.2
  174.8 1.0 copy-start.11
  174.8 1.0 copy-start.19
  175.1 1.0 copy-start.33
  175.8 1.2 copy-start.3
  175.8 1.2 copy-start.14
  175.8 1.2 copy-start.25
  175.8 1.2 copy-start.29
  176.1 1.2 copy-start.16
  176.2 1.2 copy-start.18
  176.2 1.2 copy-start.30
  176.2 1.2 copy-start.31
  176.2 1.3 copy-start.4
  176.2 1.3 copy-start.28
  176.8 1.4 copy-start.5
  176.8 1.3 copy-start.27
  177.5 1.3 copy-start.6
  177.5 1.4 copy-start.7
  177.5 1.4 copy-start.21
  177.5 1.4 copy-start.26
  179.3 2.7 dynamic-slice-start
  182.0 2.8 copy-start.35
  182.0 163.2 %copy-start.37 = (bf16[512,1024]{1,0:T(8,128)(2,1)S(1)}, bf16[512,1024]{1,0:T(8,128)(2,1)}, u32[]{:S(2)}) copy-start(bf16[512,1024]{1,0:T(8,128)(2,1)} %param.29) | copy-start | bytes 3145732
  183.9 161.4 %all-gather.6.cloned.1.call-start = ((), (), s32[]{:S(2)}) async-start(), calls=%async_computation.2 | async-start | bytes 17301504 | tf_op jit(solution)/shard_map/all_gather | solution.py:165
  360.1 56.5 %copy-start.13 = (bf16[512,1024]{1,0:T(8,128)(2,1)}, bf16[512,1024]{1,0:T(8,128)(2,1)S(1)}, u32[]{:S(2)}) copy-start(bf16[512,1024]{1,0:T(8,128)(2,1)S(1)} %add_convert_fusion) | copy-start | bytes 3145732
  360.1 56.6 %copy-start.24 = (f32[4096]{0:T(1024)S(1)}, f32[4096]{0:T(1024)}, u32[]{:S(2)}) copy-start(f32[4096]{0:T(1024)} %param.31) | copy-start | bytes 49156
Sparse Core Ops, SparseCore 0:
  184.0 84.1 all-gather.3
  271.0 74.1 all-gather.5

commit v2 on v1

--- a/solution.py
+++ b/solution.py
@@ -3,7 +3,6 @@
 from jax import lax
 from jax.sharding import PartitionSpec as P
 
-SSM_CHANNEL_COUNT = 128
 HEAD_DIM = 64
 NGROUPS = 8
 STATE = 128
@@ -83,7 +82,7 @@
     return normed.astype(jnp.bfloat16)
 
 
-def on_device(
+def mixer_layer(
     xs,
     bc,
     zgate,
@@ -109,19 +108,20 @@
     bshare = groups * STATE
     group_rows = rows * seq_count
 
-    bpart = bc[:, : NGROUPS * STATE].reshape(rows, seq_count, bshare)
-    cpart = bc[:, NGROUPS * STATE :].reshape(rows, seq_count, bshare)
+    def by_dest(part, width):
+        return part.reshape(rows, seq_count, width).transpose(1, 0, 2)
+
     packed = jnp.concatenate(
         [
-            xs.reshape(rows, seq_count, share),
-            zgate.reshape(rows, seq_count, share),
-            bpart,
-            cpart,
-            dt_raw.reshape(rows, seq_count, heads),
+            by_dest(xs, share),
+            by_dest(zgate, share),
+            by_dest(bc[:, : NGROUPS * STATE], bshare),
+            by_dest(bc[:, NGROUPS * STATE :], bshare),
+            by_dest(dt_raw, heads),
         ],
         axis=2,
     )
-    moved = lax.all_to_all(packed, "seq", split_axis=1, concat_axis=0, tiled=True)
+    moved = lax.all_to_all(packed, "seq", split_axis=0, concat_axis=0, tiled=True)
     moved = moved.reshape(group_rows, -1)
     xg = moved[:, :share]
     zg = moved[:, share : 2 * share]
@@ -172,10 +172,9 @@
     picked_rows = jnp.dot(picker, layer_out, preferred_element_type=jnp.float32).astype(
         jnp.bfloat16
     )
-    collected = lax.all_gather(picked_rows, ("req", "seq"), axis=0, tiled=True)
-    owners_all = collected.shape[0] // (seq_count * slots)
-    last_rows = collected.reshape(owners_all, seq_count, slots, width).transpose(0, 2, 1, 3)
-    last_rows = last_rows.reshape(owners_all * slots, seq_count * width).astype(jnp.float32)
+    row_pair = lax.all_gather(picked_rows, "seq", axis=1, tiled=True)
+    collected = lax.all_gather(row_pair, "req", axis=0, tiled=True)
+    last_rows = collected.astype(jnp.float32)
     meansq = jnp.mean(last_rows * last_rows, axis=-1, keepdims=True)
     normed = (last_rows * lax.rsqrt(meansq + 1e-05) * final_gain[None, :]).astype(jnp.bfloat16)
     logits = jnp.dot(normed, head_weight, preferred_element_type=jnp.float32)
@@ -199,7 +198,7 @@
         P("req", None),
     )
     return jax.shard_map(
-        on_device,
+        mixer_layer,
         mesh=mesh,
         in_specs=placed,
         out_specs=(P("req", "seq"), P(None, ("req", "seq"))),

time: 429 us -> 397 us (0.925)
  local copies, waits for them, and re-layouts: 71.9 us -> 55.9 us
  blocking collectives: 54.6 us -> 39.1 us
    all_to_all x1 -> x0, local copies, waits for them, and re-layouts: 18.4 us -> none  [on_device(): lax.all_to_all(packed, 'seq', split_axis=1, concat_axis=0, tiled=True)]
    all_gather x1 -> x2, blocking collectives: 54.6 us -> 39.1 us  [the longest x1 29.6 us: mixer_layer(): collected = lax.all_gather(row_pair, 'req', axis=0, tiled=True)]
    unnamed x93 -> x91, local copies, waits for them, and re-layouts: 18.8 us -> 17.4 us
where the time goes in v2:
time: 397 us; the launch traced here: 394 us
  waiting for transfers between devices  205 us (52%)
  local copies, waits for them, and re-layouts  55.9 us (14%)
  matrix products  50.2 us (13%)
  blocking collectives  39.1 us (10%)
  other arithmetic  20.2 us (5%)
  between operations  17.9 us (5%)
  starting transfers between devices  5.38 us (1%)
    all_gather x1, waiting for transfers between devices, mixer_layer(): gated_all = lax.all_gather(gated, 'seq', axis=1, tiled=True)  83.2 us
    all_gather x1, waiting for transfers between devices, mixer_layer(): w_full = lax.all_gather(w_cols, 'req', axis=0, tiled=True)  77.1 us
    all_to_all x1, waiting for transfers between devices, mixer_layer(): lax.all_to_all(packed, 'seq', split_axis=0, concat_axis=0, tiled=True)  45.2 us
    all_gather x1, blocking collectives, mixer_layer(): collected = lax.all_gather(row_pair, 'req', axis=0, tiled=True)  29.6 us
    unnamed x91, local copies, waits for them, and re-layouts  17.4 us
    dot_general x8, matrix products, group_inner(): jnp.einsum('tsk,skp->tkp', lower, x_g, preferred_element_type=jnp.float32)  14.9 us
    dot_general x1, matrix products, mixer_layer(): jnp.dot(gated_all, w_full, preferred_element_type=jnp.float32)  14.8 us
    all_gather x1, blocking collectives, mixer_layer(): row_pair = lax.all_gather(picked_rows, 'seq', axis=1, tiled=True)  9.46 us
  transfers between devices with their start and end apart: 3, of which 3 were waited for; matrix products, arithmetic and copies ran while one was open for 2% of the time, Pallas kernels for 0%

profile of v2, /device:TPU:1, one launch (start us, length us, event | category | flops | bytes accessed | tf_op | source)
XLA Modules:
  0.0 394.2 jit_solution(17153141175510089573)
XLA Ops:
  7.2 1.2 fusion.157
  8.6 4.1 %copy.214 = bf16[128,8192]{0,1:T(8,128)(2,1)} copy(bf16[128,8192]{1,0:T(8,128)(2,1)} %param.21) | data formatting | bytes 4194304 | tf_op args[0]
  12.7 3.3 constant_dynamic-update-slice_fusion.4
  15.9 4.1 %copy.215 = bf16[128,8192]{0,1:T(8,128)(2,1)} copy(bf16[128,8192]{1,0:T(8,128)(2,1)} %param.23) | data formatting | bytes 4194304 | tf_op args[2]
  20.3 3.3 constant_dynamic-update-slice_fusion.3
  23.6 0.8 constant_dynamic-update-slice_fusion.2
  24.4 0.8 constant_dynamic-update-slice_fusion.1
  25.8 5.1 %all-to-all-start = ((bf16[4,128,4640]{1,2,0:T(8,128)(2,1)}), bf16[4,128,4640]{1,2,0:T(8,128)(2,1)}, u32[]{:S(2)}, u32[]{:S(2)}) async-start(bf16[4,128,4640]{1,2,0:T(8,128)(2,1)} %constant_dynamic-update-slice_fusion), calls=%async_computation | async-start | bytes 9502720 | tf_op jit(solution)/shard_map/all_to_all | solution.py:124
  36.7 2.5 compare_convert_fusion.7
  40.7 45.2 %all-to-all-done = bf16[4,128,4640]{1,2,0:T(8,128)(2,1)} async-done(((bf16[4,128,4640]{1,2,0:T(8,128)(2,1)}), bf16[4,128,4640]{1,2,0:T(8,128)(2,1)}, u32[]{:S(2)}, u32[]{:S(2)}) %all-to-all-start) | async-done | bytes 4751392 | tf_op jit(solution)/shard_map/all_to_all | solution.py:124
  85.9 2.7 copy_bitcast_fusion
  88.7 0.9 fusion.155
  89.6 1.8 fusion.156
  92.2 0.7 copy.225
  94.4 1.0 reduce_window_sum.38
  95.5 1.1 multiply_reduce_fusion.3
  96.6 1.0 reduce_window_sum.39
  98.2 1.6 reduce_window_sum.40
  99.9 1.5 copy.235
  101.4 1.3 multiply_reduce_fusion.1
  102.7 1.1 fusion.161
  103.7 1.5 multiply_multiply_fusion.6
  105.3 1.3 broadcast_in_dim.69
  106.6 1.1 broadcast.230.clone.3
  107.7 6.7 %while.40 = (s32[]{:T(128)}, f32[2,128,16,64]{1,3,2,0:T(8,128)}, bf16[2,128,16,64]{1,3,2,0:T(8,128)(2,1)S(1)}, pred[2,128,128]{2,1,0:T(8,128)(4,1)}, f32[2,128,1...) while((s32[]{:T(128)}, f32[2,128,16,64]{1,3,2,0:T(8,128)}, ...), condition=%wide.region_4.5_spmd, body=%wide.region_3.4_spmd.sunk | while | flops 71172096 | bytes 2507877 | solution.py:45
  109.7 1.4 fusion.216
  113.0 1.4 fusion.216
  114.4 1.0 fusion.162
  115.5 0.7 broadcast_in_dim.70
  116.2 1.1 broadcast.230.clone.2
  117.3 9.2 %while.41 = (s32[]{:T(128)}, f32[2,128,16,64]{1,3,2,0:T(8,128)}, bf16[2,128,16,64]{1,3,2,0:T(8,128)(2,1)}, pred[2,128,128]{2,1,0:T(8,128)(4,1)S(1)}, f32[2,128,1...) while((s32[]{:T(128)}, f32[2,128,16,64]{1,3,2,0:T(8,128)}, ...), condition=%wide.region_7.8_spmd, body=%wide.region_6.7_spmd.sunk | while | flops 71172096 | bytes 2508385 | solution.py:45
  118.1 1.5 fusion.220
  119.6 2.4 fusion.221
  122.7 1.5 fusion.220
  124.2 2.3 fusion.221
  126.5 1.3 mul.494
  128.0 0.7 broadcast_in_dim.72
  128.8 1.1 broadcast.230.clone.1
  129.9 5.3 %while.42 = (s32[]{:T(128)}, f32[2,128,16,64]{1,3,2,0:T(8,128)}, bf16[2,128,16,64]{1,3,2,0:T(8,128)(2,1)S(1)}, pred[2,128,128]{2,1,0:T(8,128)(4,1)S(1)}, f32[2,1...) while((s32[]{:T(128)}, f32[2,128,16,64]{1,3,2,0:T(8,128)}, ...), condition=%wide.region_10.11_spmd, body=%wide.region_9.10_spmd.sunk | while | flops 71172096 | bytes 2507877 | solution.py:45
  131.2 1.4 fusion.226
  133.8 1.4 fusion.226
  136.8 1.0 fusion.164
  137.8 1.3 broadcast_in_dim.73
  139.2 1.1 broadcast.230.clone
  140.3 10.6 %while.43 = (s32[]{:T(128)}, f32[2,128,16,64]{1,3,2,0:T(8,128)}, bf16[2,128,16,64]{1,3,2,0:T(8,128)(2,1)}, pred[2,128,128]{2,1,0:T(8,128)(4,1)}, f32[2,128,16]{1...) while((s32[]{:T(128)}, f32[2,128,16,64]{1,3,2,0:T(8,128)}, ...), condition=%wide.region_13.14_spmd, body=%wide.region_12.13_spmd.sunk | while | flops 71172096 | bytes 2508385 | solution.py:45
  141.7 1.5 fusion.230
  143.2 2.3 fusion.231
  147.0 1.5 fusion.230
  148.5 2.4 fusion.231
  150.9 1.3 mul.535
  152.2 1.5 exponential_multiply_fusion
  153.6 1.6 copy.252
  155.9 1.2 fusion.133
  157.1 1.2 fusion.104
  163.1 2.6 bitcast_reduce_fusion
  165.8 1.8 fusion.85
  167.9 0.8 constant_dynamic-slice_fusion
  168.8 83.2 %all-gather.4.cloned.1.call-done = bf16[512,8192]{0,1:T(8,128)(2,1)} async-done(((bf16[512,2048]{0,1:T(8,128)(2,1)}), bf16[512,8192]{0,1:T(8,128)(2,1)}) %all-gather.4.cloned.1.call-update) | async-done | bytes 8388624 | tf_op jit(solution)/shard_map/all_gather | solution.py:166
  251.9 77.1 %all-gather.6.cloned.1.call-done = bf16[8192,1024]{1,0:T(8,128)(2,1)} async-done(((bf16[256,1024]{1,0:T(8,128)(2,1)}), bf16[8192,1024]{1,0:T(8,128)(2,1)}) %all-gather.6.cloned.1.call-update) | async-done | bytes 16777232 | tf_op jit(solution)/shard_map/all_gather | solution.py:165
  329.0 14.8 %add_convert_fusion = bf16[512,1024]{1,0:T(8,128)(2,1)S(1)} fusion(bf16[512,1024]{1,0:T(8,128)(2,1)S(1)} %copy-done.37, bf16[512,8192]{0,1:T(8,128)(2,1)} %all-gather.4.cloned.1.call-done, bf16[8192,1024]{1,0:T(8,128)(2,1)} %all-gather.6.cloned.1.call-done), kind=kOutput, calls=%fused_computation.111 | convolution fusion | flops 8592556032 | bytes 27262976 | tf_op jit(solution)/shard_map/dot_general | solution.py:167
  344.2 9.5 %all_gather.14 = bf16[2,4096]{1,0:T(2,128)(2,1)S(1)} all-gather(bf16[2,1024]{1,0:T(2,128)(2,1)S(1)} %convolution_convert_fusion.1), channel_id=1, replica_groups=mesh['req'=32,'seq'=4] {'seq'}, dimensions={1}, use_global_device_ids=true | all-gather | bytes 20480 | tf_op jit(solution)/shard_map/all_gather | solution.py:175
  353.6 29.6 %all-gather = bf16[32,2,4096]{2,1,0:T(2,128)(2,1)} all-gather(bf16[1,2,4096]{2,1,0:T(2,128)(2,1)S(1)} %bitcast.378), channel_id=1, replica_groups=mesh['req'=32,'seq'=4] {'req'}, dimensions={0}, use_global_device_ids=true | all-gather | bytes 540672 | tf_op jit(solution)/shard_map/all_gather | solution.py:176
  383.2 1.2 reshape.471
  384.6 2.7 fusion.117
  (163 shorter events, 26.6 us)
Async XLA Ops:
  7.2 160.7 %copy-start = (bf16[256,4096]{1,0:T(8,128)(2,1)S(1)}, bf16[256,4096]{1,0:T(8,128)(2,1)}, u32[]{:S(2)}) copy-start(bf16[256,4096]{1,0:T(8,128)(2,1)} %param.30) | copy-start | bytes 6291460
  12.7 7.5 %copy-start.23 = (bf16[128,128]{1,0:T(8,128)(2,1)S(1)}, bf16[128,128]{1,0:T(8,128)(2,1)}, u32[]{:S(2)}) copy-start(bf16[128,128]{1,0:T(8,128)(2,1)} %param.24) | copy-start | bytes 98308
  25.8 5.2 %copy-start.38 = (s32[1,2]{1,0:T(1,128)S(1)}, s32[1,2]{1,0:T(1,128)}, u32[]{:S(2)}) copy-start(s32[1,2]{1,0:T(1,128)} %param.33) | copy-start | bytes 28
  25.8 9.4 %copy-start.39 = (f32[128]{0:T(128)S(1)}, f32[128]{0:T(128)}, u32[]{:S(2)}) copy-start(f32[128]{0:T(128)} %param.25) | copy-start | bytes 1540
  25.8 9.5 %copy-start.40 = (f32[128]{0:T(128)S(1)}, f32[128]{0:T(128)}, u32[]{:S(2)}) copy-start(f32[128]{0:T(128)} %param.27) | copy-start | bytes 1540
  25.8 10.3 %copy-start.41 = (f32[128]{0:T(128)S(1)}, f32[128]{0:T(128)}, u32[]{:S(2)}) copy-start(f32[128]{0:T(128)} %param.26) | copy-start | bytes 1540
  25.8 60.2 %all-to-all-start = ((bf16[4,128,4640]{1,2,0:T(8,128)(2,1)}), bf16[4,128,4640]{1,2,0:T(8,128)(2,1)}, u32[]{:S(2)}, u32[]{:S(2)}) async-start(bf16[4,128,4640]{1,2,0:T(8,128)(2,1)} %constant_dynamic-update-slice_fusion), calls=%async_computation | async-start | bytes 9502720 | tf_op jit(solution)/shard_map/all_to_all | solution.py:124
  30.9 221.0 %all-gather.4.cloned.1.call-start = ((), (), s32[]{:S(2)}) async-start(), calls=%async_computation.1 | async-start | bytes 10485760 | tf_op jit(solution)/shard_map/all_gather | solution.py:166
  31.1 57.5 %copy-start.34 = (s32[2,1]{0,1:T(1,128)}, s32[2,1]{0,1:T(1,128)S(1)}, u32[]{:S(2)}) copy-start(s32[2,1]{0,1:T(1,128)S(1)} %reduce-window.7) | copy-start | bytes 28
  88.7 2.7 copy-start.1
  89.6 24.8 %copy-start.8 = (bf16[128,256]{0,1:T(8,128)(2,1)}, bf16[128,256]{0,1:T(8,128)(2,1)S(1)}, u32[]{:S(2)}) copy-start(bf16[128,256]{0,1:T(8,128)(2,1)S(1)} %get-tuple-element.267) | copy-start | bytes 196612
  89.6 38.3 %copy-start.10 = (bf16[128,256]{0,1:T(8,128)(2,1)}, bf16[128,256]{0,1:T(8,128)(2,1)S(1)}, u32[]{:S(2)}) copy-start(bf16[128,256]{0,1:T(8,128)(2,1)S(1)} %get-tuple-element.264) | copy-start | bytes 196612
  91.5 11.1 %copy-start.15 = (f32[512,32]{0,1:T(8,128)}, f32[512,32]{0,1:T(8,128)S(1)}, u32[]{:S(2)}) copy-start(f32[512,32]{0,1:T(8,128)S(1)} %compare_select_fusion) | copy-start | bytes 196612
  117.3 12.6 %copy-start.17 = (f32[128,32]{0,1:T(8,128)S(1)}, f32[128,32]{0,1:T(8,128)}, u32[]{:S(2)}) copy-start(f32[128,32]{0,1:T(8,128)} %copy.235) | copy-start | bytes 49156
  129.9 5.3 %copy-start.36 = (f32[32]{0:T(128)S(1)}, f32[32]{0:T(128)}, u32[]{:S(2)}) copy-start(f32[32]{0:T(128)} %get-tuple-element.311) | copy-start | bytes 388
  129.9 6.0 %copy-start.22 = (f32[128,32]{0,1:T(8,128)S(1)}, f32[128,32]{0,1:T(8,128)}, u32[]{:S(2)}) copy-start(f32[128,32]{0,1:T(8,128)} %get-tuple-element.275) | copy-start | bytes 49156
  150.9 7.4 %copy-start.9 = (bf16[128,256]{0,1:T(8,128)(2,1)S(1)}, bf16[128,256]{0,1:T(8,128)(2,1)}, u32[]{:S(2)}) copy-start(bf16[128,256]{0,1:T(8,128)(2,1)} %copy-done.8) | copy-start | bytes 196612
  153.6 4.9 %copy-start.12 = (bf16[128,256]{0,1:T(8,128)(2,1)S(1)}, bf16[128,256]{0,1:T(8,128)(2,1)}, u32[]{:S(2)}) copy-start(bf16[128,256]{0,1:T(8,128)(2,1)} %get-tuple-element.266) | copy-start | bytes 196612
  153.6 4.9 %copy-start.20 = (f32[128,32]{0,1:T(8,128)S(1)}, f32[128,32]{0,1:T(8,128)}, u32[]{:S(2)}) copy-start(f32[128,32]{0,1:T(8,128)} %get-tuple-element.286) | copy-start | bytes 49156
  153.6 5.3 %copy-start.32 = (f32[2,16]{1,0:T(2,128)S(1)}, f32[2,16]{1,0:T(2,128)}, u32[]{:S(2)}) copy-start(f32[2,16]{1,0:T(2,128)} %mul.514) | copy-start | bytes 388
  155.2 3.3 copy-start.2
  158.5 1.0 copy-start.11
  158.6 1.0 copy-start.19
  158.9 1.0 copy-start.33
  159.5 1.2 copy-start.3
  159.5 1.2 copy-start.14
  159.6 1.2 copy-start.25
  159.6 1.2 copy-start.29
  159.9 1.2 copy-start.16
  159.9 1.2 copy-start.18
  159.9 1.2 copy-start.30
  160.0 1.2 copy-start.31
  160.0 1.3 copy-start.5
  160.0 1.3 copy-start.28
  160.6 1.4 copy-start.6
  160.6 1.3 copy-start.27
  161.3 1.3 copy-start.4
  161.3 1.4 copy-start.7
  161.3 1.4 copy-start.21
  161.3 1.4 copy-start.26
  163.1 2.7 dynamic-slice-start
  165.8 3.0 copy-start.35
  165.8 163.2 %copy-start.37 = (bf16[512,1024]{1,0:T(8,128)(2,1)S(1)}, bf16[512,1024]{1,0:T(8,128)(2,1)}, u32[]{:S(2)}) copy-start(bf16[512,1024]{1,0:T(8,128)(2,1)} %param.29) | copy-start | bytes 3145732
  167.6 161.3 %all-gather.6.cloned.1.call-start = ((), (), s32[]{:S(2)}) async-start(), calls=%async_computation.2 | async-start | bytes 17301504 | tf_op jit(solution)/shard_map/all_gather | solution.py:165
  343.8 9.8 %copy-start.13 = (bf16[512,1024]{1,0:T(8,128)(2,1)}, bf16[512,1024]{1,0:T(8,128)(2,1)S(1)}, u32[]{:S(2)}) copy-start(bf16[512,1024]{1,0:T(8,128)(2,1)S(1)} %add_convert_fusion) | copy-start | bytes 3145732
  343.9 40.8 %copy-start.24 = (f32[4096]{0:T(1024)S(1)}, f32[4096]{0:T(1024)}, u32[]{:S(2)}) copy-start(f32[4096]{0:T(1024)} %param.31) | copy-start | bytes 49156
Sparse Core Ops, SparseCore 0:
  167.8 84.1 all-gather.3
  254.8 74.1 all-gather.5

commit v3 on v2

--- a/solution.py
+++ b/solution.py
@@ -111,23 +111,15 @@
     def by_dest(part, width):
         return part.reshape(rows, seq_count, width).transpose(1, 0, 2)
 
-    packed = jnp.concatenate(
-        [
-            by_dest(xs, share),
-            by_dest(zgate, share),
-            by_dest(bc[:, : NGROUPS * STATE], bshare),
-            by_dest(bc[:, NGROUPS * STATE :], bshare),
-            by_dest(dt_raw, heads),
-        ],
-        axis=2,
-    )
-    moved = lax.all_to_all(packed, "seq", split_axis=0, concat_axis=0, tiled=True)
-    moved = moved.reshape(group_rows, -1)
-    xg = moved[:, :share]
-    zg = moved[:, share : 2 * share]
-    bg = moved[:, 2 * share : 2 * share + bshare]
-    cg = moved[:, 2 * share + bshare : 2 * share + 2 * bshare]
-    dg = moved[:, 2 * share + 2 * bshare :]
+    def to_heads(part, width):
+        moved = lax.all_to_all(by_dest(part, width), "seq", split_axis=0, concat_axis=0, tiled=True)
+        return moved.reshape(group_rows, width)
+
+    xg = to_heads(xs, share)
+    bg = to_heads(bc[:, : NGROUPS * STATE], bshare)
+    cg = to_heads(bc[:, NGROUPS * STATE :], bshare)
+    dg = to_heads(dt_raw, heads)
+    zg = to_heads(zgate, share)
 
     my_heads = lambda v: lax.dynamic_slice_in_dim(v, place * heads, heads)
     rate = jnp.exp(my_heads(a_log))
@@ -141,30 +133,32 @@
     segment = jnp.sum((positions[:, None] >= ends[None, :]).astype(jnp.int32), axis=1)
     live = segment < slots
 
+    gain = lax.dynamic_slice_in_dim(norm_gain, place * share, share)
+    width = resid.shape[1]
+    w_cols = lax.dynamic_slice_in_dim(w_out, place * width, width, axis=1)
+    w_full = lax.all_gather(w_cols, "req", axis=0, tiled=True)
+
     state_in = jnp.zeros((heads, HEAD_DIM, STATE), jnp.float32)
     prev_seg = jnp.array(-1, jnp.int32)
-    ys = []
+    inputs = (xg, bg, cg, steps_dt)
+    mixers = []
     for chunk in range(seq_count):
         lo, hi = chunk * rows, (chunk + 1) * rows
+        xb, bb, cb, db = (part[lo:hi] for part in inputs)
+        if chunk > 0:
+            xb, bb, cb, db = lax.optimization_barrier((xb, bb, cb, db, gated))[:4]
         local, keep, state, carry_w, cmat = block_terms(
-            xg[lo:hi], bg[lo:hi], cg[lo:hi], steps_dt[lo:hi], segment[lo:hi], live[lo:hi],
-            prev_seg, rate, skipw, groups,
+            xb, bb, cb, db, segment[lo:hi], live[lo:hi], prev_seg, rate, skipw, groups,
         )
         y4 = (local + carry_term(state_in, cmat, carry_w, groups)) * live[lo:hi].astype(
             jnp.float32
         )[:, None, None, None]
-        ys.append(y4.reshape(rows, share))
         state_in = keep[:, None, None] * state_in + state
         prev_seg = segment[hi - 1]
-    y = jnp.concatenate(ys, axis=0)
-    gain = lax.dynamic_slice_in_dim(norm_gain, place * share, share)
-    gated = gate_norm(y, zg, gain, groups)
-
-    width = resid.shape[1]
-    w_cols = lax.dynamic_slice_in_dim(w_out, place * width, width, axis=1)
-    w_full = lax.all_gather(w_cols, "req", axis=0, tiled=True)
-    gated_all = lax.all_gather(gated, "seq", axis=1, tiled=True)
-    mixer = jnp.dot(gated_all, w_full, preferred_element_type=jnp.float32).astype(jnp.bfloat16)
+        gated = gate_norm(y4.reshape(rows, share), zg[lo:hi], gain, groups)
+        gated_all = lax.all_gather(gated, "seq", axis=1, tiled=True)
+        mixers.append(jnp.dot(gated_all, w_full, preferred_element_type=jnp.float32))
+    mixer = jnp.concatenate(mixers, axis=0).astype(jnp.bfloat16)
     layer_out = (resid.astype(jnp.float32) + mixer.astype(jnp.float32)).astype(jnp.bfloat16)
 
     group_pos = jnp.arange(group_rows, dtype=jnp.int32)

time: 397 us -> 445 us (1.12)
  matrix products: 50.2 us -> 73 us
  starting transfers between devices: 5.38 us -> 21.9 us
  waiting for transfers between devices: 205 us -> 219 us
  local copies, waits for them, and re-layouts: 55.9 us -> 45.1 us
  other arithmetic: 20.2 us -> 26.4 us
    dot_general x1 -> x4, matrix products: 14.8 us -> 35.1 us  [mixer_layer(): jnp.dot(gated_all, w_full, preferred_element_type=jnp.float32)]
    all_gather x1 -> x4, waiting for transfers between devices: 83.2 us -> 103 us  [mixer_layer(): gated_all = lax.all_gather(gated, 'seq', axis=1, tiled=True)]
    all_to_all x1 -> x5, starting transfers between devices: 5.14 us -> 21.6 us  [to_heads(): lax.all_to_all(by_dest(part, width), 'seq', split_axis=0, concat_axis=0,...]
    unnamed x91 -> x95, local copies, waits for them, and re-layouts: 17.4 us -> 3.12 us
    convert_element_type x1 -> x4, other arithmetic: 1.79 us -> 9.42 us  [gate_norm(): return normed.astype(jnp.bfloat16)]
    all_to_all x1 -> x5, waiting for transfers between devices: 45.2 us -> 39.1 us  [to_heads(): lax.all_to_all(by_dest(part, width), 'seq', split_axis=0, concat_axis=0,...]
    slice x5 -> x12, local copies, waits for them, and re-layouts: 4.26 us -> 9.87 us  [the longest x9 7.13 us: mixer_layer(): xb, bb, cb, db = (part[lo:hi] for part in inputs)]
    reshape x1 -> x2, local copies, waits for them, and re-layouts: 2.72 us -> 8.16 us  [by_dest(): return part.reshape(rows, seq_count, width).transpose(1, 0, 2)]
  transfers between devices with their start and end apart: 3 -> 10, of which waited for: 3 -> 9; matrix products, arithmetic and copies ran while one was open for 2% -> 14% of each run, Pallas kernels for 0% -> 0%
where the time goes in v3:
time: 445 us; the launch traced here: 443 us
  waiting for transfers between devices  219 us (49%)
  matrix products  73 us (16%)
  local copies, waits for them, and re-layouts  45.1 us (10%)
  blocking collectives  39.9 us (9%)
  other arithmetic  26.4 us (6%)
  starting transfers between devices  21.9 us (5%)
  between operations  17.7 us (4%)
    all_gather x4, waiting for transfers between devices, mixer_layer(): gated_all = lax.all_gather(gated, 'seq', axis=1, tiled=True)  103 us
    all_gather x1, waiting for transfers between devices, mixer_layer(): w_full = lax.all_gather(w_cols, 'req', axis=0, tiled=True)  75.5 us
    all_to_all x5, waiting for transfers between devices, to_heads(): lax.all_to_all(by_dest(part, width), 'seq', split_axis=0, concat_axis=0,...  39.1 us
    dot_general x4, matrix products, mixer_layer(): jnp.dot(gated_all, w_full, preferred_element_type=jnp.float32)  35.1 us
    all_gather x1, blocking collectives, mixer_layer(): collected = lax.all_gather(row_pair, 'req', axis=0, tiled=True)  30.8 us
    all_to_all x5, starting transfers between devices, to_heads(): lax.all_to_all(by_dest(part, width), 'seq', split_axis=0, concat_axis=0,...  21.6 us
    dot_general x8, matrix products, group_inner(): jnp.einsum('tsk,skp->tkp', lower, x_g, preferred_element_type=jnp.float32)  11.1 us
    convert_element_type x4, other arithmetic, gate_norm(): return normed.astype(jnp.bfloat16)  9.42 us
  transfers between devices with their start and end apart: 10, of which 9 were waited for; matrix products, arithmetic and copies ran while one was open for 14% of the time, Pallas kernels for 0%

profile of v3, /device:TPU:1, one launch (start us, length us, event | category | flops | bytes accessed | tf_op | source)
XLA Modules:
  0.0 443.3 jit_solution(16112066232506627821)
XLA Ops:
  7.2 1.6 copy.140
  8.8 5.0 %all-to-all-start.1 = ((bf16[4,128,32]{1,2,0:T(8,128)(2,1)}), bf16[4,128,32]{1,2,0:T(8,128)(2,1)S(1)}, u32[]{:S(2)}, u32[]{:S(2)}) async-start(bf16[4,128,32]{1,2,0:T(8,128)(2,1)} %bitcast.35), calls=%async_computation.1 | async-start | bytes 65536 | tf_op jit(solution)/shard_map/all_to_all | solution.py:115
  15.9 1.1 fusion.173
  19.0 2.4 compare_convert_fusion.1
  27.7 4.1 copy.213
  32.5 4.1 copy.216
  37.3 4.2 all-to-all-start.2
  41.5 5.5 %all-to-all-done.2 = bf16[4,128,256]{1,2,0:T(8,128)(2,1)S(1)} async-done(((bf16[4,128,256]{1,2,0:T(8,128)(2,1)}), bf16[4,128,256]{1,2,0:T(8,128)(2,1)S(1)}, u32[]{:S(2)}, u32[]{:S(2)}) %all-to-all-start.2) | async-done | bytes 262176 | tf_op jit(solution)/shard_map/all_to_all | solution.py:115
  47.0 3.4 all-to-all-start.3
  51.1 4.8 %all-to-all-done.3 = bf16[4,128,256]{1,2,0:T(8,128)(2,1)S(1)} async-done(((bf16[4,128,256]{1,2,0:T(8,128)(2,1)}), bf16[4,128,256]{1,2,0:T(8,128)(2,1)S(1)}, u32[]{:S(2)}, u32[]{:S(2)}) %all-to-all-start.3) | async-done | bytes 262176 | tf_op jit(solution)/shard_map/all_to_all | solution.py:115
  56.0 4.4 %all-to-all-start = ((bf16[4,128,2048]{1,2,0:T(8,128)(2,1)}), bf16[4,128,2048]{1,2,0:T(8,128)(2,1)}, u32[]{:S(2)}, u32[]{:S(2)}) async-start(bf16[4,128,2048]{1,2,0:T(8,128)(2,1)} %bitcast.427), calls=%async_computation | async-start | bytes 4194304 | tf_op jit(solution)/shard_map/all_to_all | solution.py:115
  68.2 14.9 %all-to-all-done = bf16[4,128,2048]{1,2,0:T(8,128)(2,1)} async-done(((bf16[4,128,2048]{1,2,0:T(8,128)(2,1)}), bf16[4,128,2048]{1,2,0:T(8,128)(2,1)}, u32[]{:S(2)}, u32[]{:S(2)}) %all-to-all-start) | async-done | bytes 2097184 | tf_op jit(solution)/shard_map/all_to_all | solution.py:115
  83.1 4.5 %all-to-all-start.4 = ((bf16[4,128,2048]{1,2,0:T(8,128)(2,1)}), bf16[4,128,2048]{1,2,0:T(8,128)(2,1)}, u32[]{:S(2)}, u32[]{:S(2)}) async-start(bf16[4,128,2048]{1,2,0:T(8,128)(2,1)} %bitcast.426), calls=%async_computation.4 | async-start | bytes 4194304 | tf_op jit(solution)/shard_map/all_to_all | solution.py:115
  87.8 2.7 fusion.172
  90.5 1.1 broadcast.299.clone
  91.6 3.9 while.40
  92.2 1.4 fusion.239
  94.1 1.4 fusion.239
  95.6 13.8 %all-to-all-done.4 = bf16[4,128,2048]{1,2,0:T(8,128)(2,1)} async-done(((bf16[4,128,2048]{1,2,0:T(8,128)(2,1)}), bf16[4,128,2048]{1,2,0:T(8,128)(2,1)}, u32[]{:S(2)}, u32[]{:S(2)}) %all-to-all-start.4) | async-done | bytes 2097184 | tf_op jit(solution)/shard_map/all_to_all | solution.py:115
  109.4 3.3 slice_convert_fusion
  112.6 1.9 multiply_reduce_fusion.4
  114.5 2.3 fusion.130
  117.7 1.4 multiply_multiply_fusion.5
  121.1 1.4 broadcast_in_dim.70
  122.5 1.1 broadcast.299.clone.1
  123.6 6.7 %while.41 = (s32[]{:T(128)}, f32[2,128,16,64]{1,3,2,0:T(8,128)}, bf16[2,128,16,64]{1,3,2,0:T(8,128)(2,1)S(1)}, pred[2,128,128]{2,1,0:T(8,128)(4,1)}, f32[2,128,1...) while((s32[]{:T(128)}, f32[2,128,16,64]{1,3,2,0:T(8,128)}, ...), condition=%wide.region_8.9_spmd, body=%wide.region_7.8_spmd.sunk | while | flops 71172096 | bytes 2507877 | solution.py:45
  125.6 1.4 fusion.244
  128.9 1.4 fusion.244
  132.2 1.5 fusion.98
  134.0 1.9 multiply_reduce_fusion.3
  136.0 2.3 fusion.124
  139.2 1.3 multiply_multiply_fusion.4
  140.6 1.5 copy.170
  143.3 1.1 broadcast.299.clone.2
  144.4 7.3 %while.42 = (s32[]{:T(128)}, f32[2,128,16,64]{1,3,2,0:T(8,128)}, bf16[2,128,16,64]{1,3,2,0:T(8,128)(2,1)}, pred[2,128,128]{2,1,0:T(8,128)(4,1)S(1)}, f32[2,128,1...) while((s32[]{:T(128)}, f32[2,128,16,64]{1,3,2,0:T(8,128)}, ...), condition=%wide.region_12.13_spmd, body=%wide.region_11.12_spmd.sunk | while | flops 71172096 | bytes 4605565 | solution.py:45
  145.2 1.5 fusion.248
  146.7 1.4 fusion.249
  148.8 1.5 fusion.248
  150.4 1.4 fusion.249
  152.7 1.4 fusion.147
  154.2 1.5 fusion.93
  156.0 1.9 multiply_reduce_fusion.2
  158.0 2.4 fusion.118
  161.5 1.1 broadcast.299
  162.6 4.0 while.43
  163.2 1.4 fusion.254
  165.2 1.4 fusion.254
  168.2 1.4 fusion.143
  169.6 1.5 fusion.88
  171.4 1.9 multiply_reduce_fusion.1
  173.3 2.3 fusion.112
  178.5 33.1 %all-gather.15.cloned.1.call-done = bf16[128,8192]{0,1:T(8,128)(2,1)} async-done(((bf16[128,2048]{0,1:T(8,128)(2,1)}), bf16[128,8192]{0,1:T(8,128)(2,1)}) %all-gather.15.cloned.1.call-update) | async-done | bytes 2097168 | tf_op jit(solution)/shard_map/all_gather | solution.py:159
  211.6 75.5 %all-gather.9.cloned.1.call-done = bf16[8192,1024]{1,0:T(8,128)(2,1)} async-done(((bf16[256,1024]{1,0:T(8,128)(2,1)}), bf16[8192,1024]{1,0:T(8,128)(2,1)}) %all-gather.9.cloned.1.call-update) | async-done | bytes 16777232 | tf_op jit(solution)/shard_map/all_gather | solution.py:139
  287.2 8.8 %convolution_convert_fusion = bf16[128,1024]{1,0:T(8,128)(2,1)S(1)} fusion(bf16[128,8192]{0,1:T(8,128)(2,1)} %all-gather.15.cloned.1.call-done, bf16[8192,1024]{1,0:T(8,128)(2,1)} %all-gather.9.cloned.1.call-done), kind=kOutput, calls=%fused_computation.139 | convolution fusion | flops 2147614720 | bytes 19136512 | tf_op jit(solution)/shard_map/dot_general | solution.py:160
  295.9 22.5 %all-gather.13.cloned.1.call-done = bf16[128,8192]{0,1:T(8,128)(2,1)} async-done(((bf16[128,2048]{0,1:T(8,128)(2,1)}), bf16[128,8192]{0,1:T(8,128)(2,1)}) %all-gather.13.cloned.1.call-update) | async-done | bytes 2097168 | tf_op jit(solution)/shard_map/all_gather | solution.py:159
  318.5 8.8 %convolution_convert_fusion.1 = bf16[128,1024]{1,0:T(8,128)(2,1)S(1)} fusion(bf16[128,8192]{0,1:T(8,128)(2,1)} %all-gather.13.cloned.1.call-done, bf16[8192,1024]{1,0:T(8,128)(2,1)} %all-gather.9.cloned.1.call-done), kind=kOutput, calls=%fused_computation.140 | convolution fusion | flops 2147614720 | bytes 19136512 | tf_op jit(solution)/shard_map/dot_general | solution.py:160
  327.2 23.6 %all-gather.11.cloned.1.call-done = bf16[128,8192]{0,1:T(8,128)(2,1)} async-done(((bf16[128,2048]{0,1:T(8,128)(2,1)}), bf16[128,8192]{0,1:T(8,128)(2,1)}) %all-gather.11.cloned.1.call-update) | async-done | bytes 2097168 | tf_op jit(solution)/shard_map/all_gather | solution.py:159
  350.8 8.8 %convolution_convert_fusion.2 = bf16[128,1024]{1,0:T(8,128)(2,1)S(1)} fusion(bf16[128,8192]{0,1:T(8,128)(2,1)} %all-gather.11.cloned.1.call-done, bf16[8192,1024]{1,0:T(8,128)(2,1)} %all-gather.9.cloned.1.call-done), kind=kOutput, calls=%fused_computation.141 | convolution fusion | flops 2147614720 | bytes 19136512 | tf_op jit(solution)/shard_map/dot_general | solution.py:160
  359.6 23.6 %all-gather.7.cloned.1.call-done = bf16[128,8192]{0,1:T(8,128)(2,1)} async-done(((bf16[128,2048]{0,1:T(8,128)(2,1)}), bf16[128,8192]{0,1:T(8,128)(2,1)}) %all-gather.7.cloned.1.call-update) | async-done | bytes 2097168 | tf_op jit(solution)/shard_map/all_gather | solution.py:159
  383.2 8.8 %convolution_convert_fusion.3 = bf16[128,1024]{1,0:T(8,128)(2,1)S(1)} fusion(bf16[128,8192]{0,1:T(8,128)(2,1)} %all-gather.7.cloned.1.call-done, bf16[8192,1024]{1,0:T(8,128)(2,1)} %all-gather.9.cloned.1.call-done), kind=kOutput, calls=%fused_computation.142 | convolution fusion | flops 2147614720 | bytes 19136512 | tf_op jit(solution)/shard_map/dot_general | solution.py:160
  392.8 9.1 %all_gather.26 = bf16[2,4096]{1,0:T(2,128)(2,1)S(1)} all-gather(bf16[2,1024]{1,0:T(2,128)(2,1)S(1)} %convolution_convert_fusion.4), channel_id=1, replica_groups=mesh['req'=32,'seq'=4] {'seq'}, dimensions={1}, use_global_device_ids=true | all-gather | bytes 20480 | tf_op jit(solution)/shard_map/all_gather | solution.py:169
  401.9 30.8 %all-gather = bf16[32,2,4096]{2,1,0:T(2,128)(2,1)} all-gather(bf16[1,2,4096]{2,1,0:T(2,128)(2,1)S(1)} %bitcast.491), channel_id=1, replica_groups=mesh['req'=32,'seq'=4] {'req'}, dimensions={0}, use_global_device_ids=true | all-gather | bytes 540672 | tf_op jit(solution)/shard_map/all_gather | solution.py:170
  432.7 1.2 reshape.570
  434.1 2.7 fusion.135
  (224 shorter events, 40.0 us)
Async XLA Ops:
  7.2 168.5 %copy-start = (bf16[256,4096]{1,0:T(8,128)(2,1)S(1)}, bf16[256,4096]{1,0:T(8,128)(2,1)}, u32[]{:S(2)}) copy-start(bf16[256,4096]{1,0:T(8,128)(2,1)} %param.30) | copy-start | bytes 6291460
  8.8 28.5 %all-to-all-start.1 = ((bf16[4,128,32]{1,2,0:T(8,128)(2,1)}), bf16[4,128,32]{1,2,0:T(8,128)(2,1)S(1)}, u32[]{:S(2)}, u32[]{:S(2)}) async-start(bf16[4,128,32]{1,2,0:T(8,128)(2,1)} %bitcast.35), calls=%async_computation.1 | async-start | bytes 65536 | tf_op jit(solution)/shard_map/all_to_all | solution.py:115
  14.6 0.6 copy-start.39
  22.2 94.7 %copy-start.30 = (f32[32]{0:T(128)}, f32[32]{0:T(128)S(1)}, u32[]{:S(2)}) copy-start(f32[32]{0:T(128)S(1)} %exponential_negate_fusion) | copy-start | bytes 388
  27.7 4.1 copy-start.43
  37.3 77.3 %copy-start.24 = (f32[2048]{0:T(1024)}, f32[2048]{0:T(1024)S(1)}, u32[]{:S(2)}) copy-start(f32[2048]{0:T(1024)S(1)} %dynamic_slice.82) | copy-start | bytes 24580
  37.3 9.8 %all-to-all-start.2 = ((bf16[4,128,256]{1,2,0:T(8,128)(2,1)}), bf16[4,128,256]{1,2,0:T(8,128)(2,1)S(1)}, u32[]{:S(2)}, u32[]{:S(2)}) async-start(bf16[4,128,256]{1,2,0:T(8,128)(2,1)} %bitcast.40), calls=%async_computation.2 | async-start | bytes 524288 | tf_op jit(solution)/shard_map/all_to_all | solution.py:115
  47.0 8.9 %all-to-all-start.3 = ((bf16[4,128,256]{1,2,0:T(8,128)(2,1)}), bf16[4,128,256]{1,2,0:T(8,128)(2,1)S(1)}, u32[]{:S(2)}, u32[]{:S(2)}) async-start(bf16[4,128,256]{1,2,0:T(8,128)(2,1)} %bitcast.43), calls=%async_computation.3 | async-start | bytes 524288 | tf_op jit(solution)/shard_map/all_to_all | solution.py:115
  56.0 27.1 %all-to-all-start = ((bf16[4,128,2048]{1,2,0:T(8,128)(2,1)}), bf16[4,128,2048]{1,2,0:T(8,128)(2,1)}, u32[]{:S(2)}, u32[]{:S(2)}) async-start(bf16[4,128,2048]{1,2,0:T(8,128)(2,1)} %bitcast.427), calls=%async_computation | async-start | bytes 4194304 | tf_op jit(solution)/shard_map/all_to_all | solution.py:115
  64.3 18.8 %copy-start.22 = (bf16[1,128,256]{1,2,0:T(8,128)(2,1)}, bf16[1,128,256]{1,2,0:T(8,128)(2,1)S(1)}, u32[]{:S(2)}) copy-start(bf16[1,128,256]{1,2,0:T(8,128)(2,1)S(1)} %get-tuple-element.293) | copy-start | bytes 196612
  83.1 26.3 %all-to-all-start.4 = ((bf16[4,128,2048]{1,2,0:T(8,128)(2,1)}), bf16[4,128,2048]{1,2,0:T(8,128)(2,1)}, u32[]{:S(2)}, u32[]{:S(2)}) async-start(bf16[4,128,2048]{1,2,0:T(8,128)(2,1)} %bitcast.426), calls=%async_computation.4 | async-start | bytes 4194304 | tf_op jit(solution)/shard_map/all_to_all | solution.py:115
  87.6 124.0 %all-gather.15.cloned.1.call-start = ((), (), s32[]{:S(2)}) async-start(), calls=%async_computation.9 | async-start | bytes 2621440 | tf_op jit(solution)/shard_map/all_gather | solution.py:159
  87.8 2.7 copy-start.27
  95.5 34.8 %copy-start.3 = (bf16[2,128,16,64]{1,3,2,0:T(8,128)(2,1)}, bf16[2,128,16,64]{1,3,2,0:T(8,128)(2,1)S(1)}, u32[]{:S(2)}) copy-start(bf16[2,128,16,64]{1,3,2,0:T(8,128)(2,1)S(1)} %get-tuple-element.627) | copy-start | bytes 1572868
  95.5 17.1 %copy-start.23 = (bf16[1,128,256]{1,2,0:T(8,128)(2,1)S(1)}, bf16[1,128,256]{1,2,0:T(8,128)(2,1)}, u32[]{:S(2)}) copy-start(bf16[1,128,256]{1,2,0:T(8,128)(2,1)} %copy-done.22) | copy-start | bytes 196612
  95.5 17.1 %copy-start.29 = (f32[128,2,16]{0,2,1:T(8,128)S(1)}, f32[128,2,16]{0,2,1:T(8,128)}, u32[]{:S(2)}) copy-start(f32[128,2,16]{0,2,1:T(8,128)} %exponential_multiply_fusion.3) | copy-start | bytes 49156
  95.5 17.1 %copy-start.44 = (f32[2,16]{1,0:T(2,128)S(1)}, f32[2,16]{1,0:T(2,128)}, u32[]{:S(2)}) copy-start(f32[2,16]{1,0:T(2,128)} %mul.597) | copy-start | bytes 388
  114.5 6.2 %copy-start.20 = (bf16[1,128,256]{2,1,0:T(8,128)(2,1)S(1)}, bf16[1,128,256]{2,1,0:T(8,128)(2,1)}, u32[]{:S(2)}) copy-start(bf16[1,128,256]{2,1,0:T(8,128)(2,1)} %copy.150) | copy-start | bytes 196612
  130.3 0.8 copy-start.6
  132.1 1.8 copy-start.35
  132.2 1.8 copy-start.7
  132.2 1.8 copy-start.12
  132.2 1.8 copy-start.38
  132.2 1.8 copy-start.45
  134.0 2.0 copy-start.25
  136.0 2.4 copy-start.31
  136.0 3.3 copy-start.34
  136.0 6.1 %copy-start.19 = (bf16[1,128,256]{2,1,0:T(8,128)(2,1)S(1)}, bf16[1,128,256]{2,1,0:T(8,128)(2,1)}, u32[]{:S(2)}) copy-start(bf16[1,128,256]{2,1,0:T(8,128)(2,1)} %copy.164) | copy-start | bytes 196612
  136.0 6.2 %copy-start.18 = (bf16[1,128,256]{2,1,0:T(8,128)(2,1)S(1)}, bf16[1,128,256]{2,1,0:T(8,128)(2,1)}, u32[]{:S(2)}) copy-start(bf16[1,128,256]{2,1,0:T(8,128)(2,1)} %copy.163) | copy-start | bytes 196612
  144.4 8.2 %copy-start.42 = (f32[32]{0:T(128)S(1)}, f32[32]{0:T(128)}, u32[]{:S(2)}) copy-start(f32[32]{0:T(128)} %get-tuple-element.301) | copy-start | bytes 388
  144.4 2.3 copy-start.4
  148.1 2.3 copy-start.4
  154.1 1.8 copy-start.33
  154.1 1.8 copy-start.5
  154.1 1.8 copy-start.11
  154.1 1.8 copy-start.37
  154.1 1.8 copy-start.46
  155.6 2.3 copy-start.1
  157.9 2.5 copy-start.17
  157.9 2.6 copy-start.16
  157.9 2.7 copy-start.15
  157.9 2.7 copy-start.36
  157.9 3.5 copy-start.26
  158.0 4.6 %copy-start.13 = (bf16[128,2048]{0,1:T(8,128)(2,1)S(1)}, bf16[128,2048]{0,1:T(8,128)(2,1)}, u32[]{:S(2)}) copy-start(bf16[128,2048]{0,1:T(8,128)(2,1)} %get-tuple-element.173) | copy-start | bytes 1572868
  162.6 4.0 copy-start.21
  162.6 4.7 %copy-start.41 = (f32[32]{0:T(128)S(1)}, f32[32]{0:T(128)}, u32[]{:S(2)}) copy-start(f32[32]{0:T(128)} %get-tuple-element.299) | copy-start | bytes 388
  162.6 5.3 %copy-start.32 = (f32[128]{0:T(128)S(1)}, f32[128]{0:T(128)}, u32[]{:S(2)}) copy-start(f32[128]{0:T(128)} %get-tuple-element.305) | copy-start | bytes 1540
  166.6 2.9 copy-start.2
  169.5 1.8 copy-start.10
  169.5 1.8 copy-start.14
  169.6 1.8 copy-start.47
  175.6 2.9 copy-start.40
  175.6 111.5 %all-gather.9.cloned.1.call-start = ((), (), s32[]{:S(2)}) async-start(), calls=%async_computation.6 | async-start | bytes 17301504 | tf_op jit(solution)/shard_map/all_gather | solution.py:139
  176.6 141.9 %all-gather.13.cloned.1.call-start = ((), (), s32[]{:S(2)}) async-start(), calls=%async_computation.8 | async-start | bytes 2621440 | tf_op jit(solution)/shard_map/all_gather | solution.py:159
  177.3 173.5 %all-gather.11.cloned.1.call-start = ((), (), s32[]{:S(2)}) async-start(), calls=%async_computation.7 | async-start | bytes 2621440 | tf_op jit(solution)/shard_map/all_gather | solution.py:159
  177.9 205.3 %all-gather.7.cloned.1.call-start = ((), (), s32[]{:S(2)}) async-start(), calls=%async_computation.5 | async-start | bytes 2621440 | tf_op jit(solution)/shard_map/all_gather | solution.py:159
  383.2 8.9 %copy-start.9 = (bf16[512,1024]{1,0:T(8,128)(2,1)S(1)}, bf16[512,1024]{1,0:T(8,128)(2,1)}, u32[]{:S(2)}) copy-start(bf16[512,1024]{1,0:T(8,128)(2,1)} %param.29) | copy-start | bytes 3145732
  392.5 9.4 %copy-start.8 = (bf16[512,1024]{1,0:T(8,128)(2,1)}, bf16[512,1024]{1,0:T(8,128)(2,1)S(1)}, u32[]{:S(2)}) copy-start(bf16[512,1024]{1,0:T(8,128)(2,1)S(1)} %add_convert_fusion) | copy-start | bytes 3145732
  392.5 41.6 %copy-start.28 = (f32[4096]{0:T(1024)S(1)}, f32[4096]{0:T(1024)}, u32[]{:S(2)}) copy-start(f32[4096]{0:T(1024)} %param.31) | copy-start | bytes 49156
Sparse Core Ops, SparseCore 0:
  175.8 35.7 all-gather.14
  213.9 73.2 all-gather.8
  288.8 29.5 all-gather.12
  320.0 30.7 all-gather.10
  352.3 30.7 all-gather.6

commit v4 on v2

--- a/solution.py
+++ b/solution.py
@@ -169,12 +169,18 @@
 
     group_pos = jnp.arange(group_rows, dtype=jnp.int32)
     picker = (group_pos[None, :] == (ends - 1)[:, None]).astype(jnp.bfloat16)
-    picked_rows = jnp.dot(picker, layer_out, preferred_element_type=jnp.float32).astype(
+    picked_gated = jnp.dot(picker, gated_all, preferred_element_type=jnp.float32).astype(jnp.bfloat16)
+    picked_resid = jnp.dot(picker, resid, preferred_element_type=jnp.float32)
+    picked_mixer = jnp.dot(picked_gated, w_full, preferred_element_type=jnp.float32)
+    picked_rows = (picked_resid + picked_mixer.astype(jnp.bfloat16).astype(jnp.float32)).astype(
         jnp.bfloat16
     )
-    row_pair = lax.all_gather(picked_rows, "seq", axis=1, tiled=True)
-    collected = lax.all_gather(row_pair, "req", axis=0, tiled=True)
-    last_rows = collected.astype(jnp.float32)
+    owner = lax.axis_index("req")
+    owners_all = lax.axis_size("req")
+    spread = jnp.zeros((owners_all, slots, seq_count, width), jnp.bfloat16)
+    spread = lax.dynamic_update_slice(spread, picked_rows[None, :, None, :], (owner, 0, place, 0))
+    collected = lax.psum(spread, ("req", "seq"))
+    last_rows = collected.reshape(owners_all * slots, seq_count * width).astype(jnp.float32)
     meansq = jnp.mean(last_rows * last_rows, axis=-1, keepdims=True)
     normed = (last_rows * lax.rsqrt(meansq + 1e-05) * final_gain[None, :]).astype(jnp.bfloat16)
     logits = jnp.dot(normed, head_weight, preferred_element_type=jnp.float32)

time: 397 us -> 498 us (1.25)
  waiting for transfers between devices: 205 us -> 335 us
  blocking collectives: 39.1 us -> 0 us
  matrix products: 50.2 us -> 63.7 us
    psum x0 -> x1, waiting for transfers between devices: none -> 130 us  [mixer_layer(): collected = lax.psum(spread, ('req', 'seq'))]
    all_gather x2 -> x0, blocking collectives: 39.1 us -> none  [the longest x1 29.6 us: mixer_layer(): collected = lax.all_gather(row_pair, 'req', axis=0, tiled=True)]
    dot_general x1 -> x2, matrix products: 0.28 us -> 12.9 us  [the longest x1 12.6 us: mixer_layer(): jnp.dot(picked_gated, w_full, preferred_element_type=jnp.float32)]
    unnamed x91 -> x88, local copies, waits for them, and re-layouts: 17.4 us -> 19.5 us
  transfers between devices with their start and end apart: 3 -> 4, of which waited for: 3 -> 4; matrix products, arithmetic and copies ran while one was open for 2% -> 5% of each run, Pallas kernels for 0% -> 0%
where the time goes in v4:
time: 498 us; the launch traced here: 495 us
  waiting for transfers between devices  335 us (67%)
  matrix products  63.7 us (13%)
  local copies, waits for them, and re-layouts  55.8 us (11%)
  between operations  17.7 us (4%)
  other arithmetic  17.3 us (3%)
  starting transfers between devices  5.42 us (1%)
    psum x1, waiting for transfers between devices, mixer_layer(): collected = lax.psum(spread, ('req', 'seq'))  130 us
    all_gather x1, waiting for transfers between devices, mixer_layer(): gated_all = lax.all_gather(gated, 'seq', axis=1, tiled=True)  83.1 us
    all_gather x1, waiting for transfers between devices, mixer_layer(): w_full = lax.all_gather(w_cols, 'req', axis=0, tiled=True)  77.1 us
    all_to_all x1, waiting for transfers between devices, mixer_layer(): lax.all_to_all(packed, 'seq', split_axis=0, concat_axis=0, tiled=True)  45.3 us
    unnamed x88, local copies, waits for them, and re-layouts  19.5 us
    dot_general x1, matrix products, mixer_layer(): jnp.dot(gated_all, w_full, preferred_element_type=jnp.float32)  15.8 us
    dot_general x8, matrix products, group_inner(): jnp.einsum('tsk,skp->tkp', lower, x_g, preferred_element_type=jnp.float32)  14.9 us
    dot_general x1, matrix products, mixer_layer(): jnp.dot(picked_gated, w_full, preferred_element_type=jnp.float32)  12.6 us
  transfers between devices with their start and end apart: 4, of which 4 were waited for; matrix products, arithmetic and copies ran while one was open for 5% of the time, Pallas kernels for 0%

profile of v4, /device:TPU:1, one launch (start us, length us, event | category | flops | bytes accessed | tf_op | source)
XLA Modules:
  0.0 495.2 jit_solution(2061553077661066185)
XLA Ops:
  7.2 4.2 copy.217
  11.4 3.4 constant_dynamic-update-slice_fusion.4
  14.8 4.1 copy.218
  19.4 3.3 constant_dynamic-update-slice_fusion.3
  22.7 0.8 constant_dynamic-update-slice_fusion.2
  23.4 0.7 constant_dynamic-update-slice_fusion.1
  24.8 5.1 %all-to-all-start = ((bf16[4,128,4640]{1,2,0:T(8,128)(2,1)}), bf16[4,128,4640]{1,2,0:T(8,128)(2,1)}, u32[]{:S(2)}, u32[]{:S(2)}) async-start(bf16[4,128,4640]{1,2,0:T(8,128)(2,1)} %constant_dynamic-update-slice_fusion), calls=%async_computation | async-start | bytes 9502720 | tf_op jit(solution)/shard_map/all_to_all | solution.py:124
  35.6 2.6 compare_convert_fusion.7
  38.2 0.7 fusion.148
  38.9 0.7 fusion.150
  39.7 45.3 %all-to-all-done = bf16[4,128,4640]{1,2,0:T(8,128)(2,1)} async-done(((bf16[4,128,4640]{1,2,0:T(8,128)(2,1)}), bf16[4,128,4640]{1,2,0:T(8,128)(2,1)}, u32[]{:S(2)}, u32[]{:S(2)}) %all-to-all-start) | async-done | bytes 4751392 | tf_op jit(solution)/shard_map/all_to_all | solution.py:124
  85.0 2.7 copy_bitcast_fusion
  87.7 0.9 fusion.158
  88.6 1.8 fusion.159
  91.6 1.1 multiply_reduce_fusion.3
  93.6 0.8 copy.237
  95.3 1.3 mul.495
  98.5 1.5 copy.246
  100.0 1.0 fusion.163
  101.7 1.0 fusion.167
  102.7 1.5 multiply_multiply_fusion.6
  104.3 1.3 broadcast_in_dim.77
  105.6 1.1 broadcast.234.clone
  106.7 10.6 %while.43 = (s32[]{:T(128)}, f32[2,128,16,64]{1,3,2,0:T(8,128)}, bf16[2,128,16,64]{1,3,2,0:T(8,128)(2,1)}, pred[2,128,128]{2,1,0:T(8,128)(4,1)}, f32[2,128,16]{1...) while((s32[]{:T(128)}, f32[2,128,16,64]{1,3,2,0:T(8,128)}, ...), condition=%wide.region_13.14_spmd, body=%wide.region_12.13_spmd.sunk | while | flops 71172096 | bytes 2507885 | solution.py:45
  108.2 1.5 fusion.235
  109.7 2.3 fusion.236
  113.4 1.5 fusion.235
  114.9 2.4 fusion.236
  117.3 0.8 exponential_multiply_fusion
  118.8 1.1 fusion.166
  119.9 0.7 broadcast_in_dim.76
  120.6 1.1 broadcast.234.clone.1
  121.7 9.1 %while.42 = (s32[]{:T(128)}, f32[2,128,16,64]{1,3,2,0:T(8,128)}, bf16[2,128,16,64]{1,3,2,0:T(8,128)(2,1)}, pred[2,128,128]{2,1,0:T(8,128)(4,1)S(1)}, f32[2,128,1...) while((s32[]{:T(128)}, f32[2,128,16,64]{1,3,2,0:T(8,128)}, ...), condition=%wide.region_10.11_spmd, body=%wide.region_9.10_spmd.sunk | while | flops 71172096 | bytes 2507885 | solution.py:45
  121.7 0.7 dynamic-slice_bitcast_fusion.34
  122.5 1.5 fusion.230
  124.0 2.3 fusion.231
  127.0 1.5 fusion.230
  128.5 2.3 fusion.231
  131.1 1.3 broadcast_in_dim.74
  132.4 1.1 broadcast.234.clone.2
  133.6 6.8 %while.41 = (s32[]{:T(128)}, f32[2,128,16,64]{1,3,2,0:T(8,128)}, bf16[2,128,16,64]{1,3,2,0:T(8,128)(2,1)S(1)}, pred[2,128,128]{2,1,0:T(8,128)(4,1)}, f32[2,128,1...) while((s32[]{:T(128)}, f32[2,128,16,64]{1,3,2,0:T(8,128)}, ...), condition=%wide.region_7.8_spmd, body=%wide.region_6.7_spmd.sunk | while | flops 71172096 | bytes 2507885 | solution.py:45
  133.6 0.7 dynamic-slice_bitcast_fusion.31
  135.6 1.4 fusion.226
  139.0 1.4 fusion.226
  140.4 1.0 fusion.164
  141.4 1.3 broadcast_in_dim.73
  142.7 1.1 broadcast.234.clone.3
  143.9 6.7 %while.40 = (s32[]{:T(128)}, f32[2,128,16,64]{1,3,2,0:T(8,128)}, bf16[2,128,16,64]{1,3,2,0:T(8,128)(2,1)S(1)}, pred[2,128,128]{2,1,0:T(8,128)(4,1)}, f32[2,128,1...) while((s32[]{:T(128)}, f32[2,128,16,64]{1,3,2,0:T(8,128)}, ...), condition=%wide.region_4.5_spmd, body=%wide.region_3.4_spmd.sunk | while | flops 71172096 | bytes 2507885 | solution.py:45
  145.8 1.4 fusion.221
  149.2 1.4 fusion.221
  150.6 1.0 fusion.136
  151.6 1.0 fusion.104
  157.6 2.6 bitcast_reduce_fusion
  160.3 1.8 fusion.85
  162.2 0.8 constant_dynamic-slice_fusion
  163.3 83.1 %all-gather.3.cloned.1.call-done = bf16[512,8192]{0,1:T(8,128)(2,1)} async-done(((bf16[512,2048]{0,1:T(8,128)(2,1)}), bf16[512,8192]{0,1:T(8,128)(2,1)}) %all-gather.3.cloned.1.call-update) | async-done | bytes 8388624 | tf_op jit(solution)/shard_map/all_gather | solution.py:166
  246.4 77.1 %all-gather.5.cloned.1.call-done = bf16[8192,1024]{1,0:T(8,128)(2,1)} async-done(((bf16[256,1024]{1,0:T(8,128)(2,1)}), bf16[8192,1024]{1,0:T(8,128)(2,1)}) %all-gather.5.cloned.1.call-update) | async-done | bytes 16777232 | tf_op jit(solution)/shard_map/all_gather | solution.py:165
  323.4 12.6 %fusion.111 = f32[2,1024]{1,0:T(2,128)S(1)} fusion(bf16[8192,1024]{1,0:T(8,128)(2,1)} %all-gather.5.cloned.1.call-done, bf16[512,8192]{0,1:T(8,128)(2,1)} %all-gather.3.cloned.1.call-done, s32[2]{0:T(128)S(1)} %broadcast_add_fusion), kind=kOutput, calls=%fused_computation.154 | convolution fusion | flops 50353152 | bytes 25174024 | tf_op jit(solution)/shard_map/dot_general | solution.py:174
  336.6 0.8 copy-done.7
  337.5 15.8 %add_convert_fusion = bf16[512,1024]{1,0:T(8,128)(2,1)} fusion(bf16[512,1024]{1,0:T(8,128)(2,1)} %param.29, bf16[512,8192]{0,1:T(8,128)(2,1)} %all-gather.3.cloned.1.call-done, bf16[8192,1024]{1,0:T(8,128)(2,1)} %all-gather.5.cloned.1.call-done), kind=kOutput, calls=%fused_computation.112 | convolution fusion | flops 8592556032 | bytes 27262976 | tf_op jit(solution)/shard_map/dot_general | solution.py:167
  353.3 129.8 %all-reduce.2.cloned.1.call-done = bf16[32,2,4,1024]{3,2,1,0:T(4,128)(2,1)} async-done(((bf16[32,2,4,1024]{3,2,1,0:T(4,128)(2,1)}), bf16[32,2,4,1024]{3,2,1,0:T(4,128)(2,1)}) %all-reduce.2.cloned.1.call-update) | async-done | bytes 524304 | tf_op jit(solution)/shard_map/psum | solution.py:182
  483.2 1.2 copy.305
  484.4 1.4 multiply_reduce_fusion
  486.0 2.7 fusion.120
  (165 shorter events, 26.4 us)
Async XLA Ops:
  7.2 155.0 %copy-start = (bf16[256,4096]{1,0:T(8,128)(2,1)S(1)}, bf16[256,4096]{1,0:T(8,128)(2,1)}, u32[]{:S(2)}) copy-start(bf16[256,4096]{1,0:T(8,128)(2,1)} %param.30) | copy-start | bytes 6291460
  11.4 7.4 %copy-start.16 = (bf16[128,2048]{1,0:T(8,128)(2,1)S(1)}, bf16[128,2048]{1,0:T(8,128)(2,1)}, u32[]{:S(2)}) copy-start(bf16[128,2048]{1,0:T(8,128)(2,1)} %param.22) | copy-start | bytes 1572868
  14.8 4.5 copy-start.22
  24.8 5.2 %copy-start.36 = (s32[1,2]{1,0:T(1,128)S(1)}, s32[1,2]{1,0:T(1,128)}, u32[]{:S(2)}) copy-start(s32[1,2]{1,0:T(1,128)} %param.33) | copy-start | bytes 28
  24.8 9.4 %copy-start.37 = (f32[128]{0:T(128)S(1)}, f32[128]{0:T(128)}, u32[]{:S(2)}) copy-start(f32[128]{0:T(128)} %param.25) | copy-start | bytes 1540
  24.8 9.5 %copy-start.38 = (f32[128]{0:T(128)S(1)}, f32[128]{0:T(128)}, u32[]{:S(2)}) copy-start(f32[128]{0:T(128)} %param.27) | copy-start | bytes 1540
  24.8 10.2 %copy-start.39 = (f32[128]{0:T(128)S(1)}, f32[128]{0:T(128)}, u32[]{:S(2)}) copy-start(f32[128]{0:T(128)} %param.26) | copy-start | bytes 1540
  24.8 60.2 %all-to-all-start = ((bf16[4,128,4640]{1,2,0:T(8,128)(2,1)}), bf16[4,128,4640]{1,2,0:T(8,128)(2,1)}, u32[]{:S(2)}, u32[]{:S(2)}) async-start(bf16[4,128,4640]{1,2,0:T(8,128)(2,1)} %constant_dynamic-update-slice_fusion), calls=%async_computation | async-start | bytes 9502720 | tf_op jit(solution)/shard_map/all_to_all | solution.py:124
  29.9 216.5 %all-gather.3.cloned.1.call-start = ((), (), s32[]{:S(2)}) async-start(), calls=%async_computation.1 | async-start | bytes 10485760 | tf_op jit(solution)/shard_map/all_gather | solution.py:166
  30.1 57.6 %copy-start.34 = (s32[2,1]{0,1:T(1,128)}, s32[2,1]{0,1:T(1,128)S(1)}, u32[]{:S(2)}) copy-start(s32[2,1]{0,1:T(1,128)S(1)} %reduce-window.7) | copy-start | bytes 28
  87.7 2.7 copy-start.1
  90.5 11.2 %copy-start.15 = (f32[512,32]{0,1:T(8,128)}, f32[512,32]{0,1:T(8,128)S(1)}, u32[]{:S(2)}) copy-start(f32[512,32]{0,1:T(8,128)S(1)} %compare_select_fusion) | copy-start | bytes 196612
  121.7 9.1 %copy-start.11 = (bf16[128,256]{0,1:T(8,128)(2,1)S(1)}, bf16[128,256]{0,1:T(8,128)(2,1)}, u32[]{:S(2)}) copy-start(bf16[128,256]{0,1:T(8,128)(2,1)} %get-tuple-element.266) | copy-start | bytes 196612
  133.6 6.8 %copy-start.12 = (bf16[128,256]{0,1:T(8,128)(2,1)S(1)}, bf16[128,256]{0,1:T(8,128)(2,1)}, u32[]{:S(2)}) copy-start(bf16[128,256]{0,1:T(8,128)(2,1)} %get-tuple-element.268) | copy-start | bytes 196612
  150.6 2.4 copy-start.20
  150.6 2.7 copy-start.33
  152.7 1.0 copy-start.9
  153.0 1.1 copy-start.2
  153.0 1.1 copy-start.10
  153.0 1.1 copy-start.19
  153.3 1.1 copy-start.32
  153.9 1.1 copy-start.31
  154.0 1.1 copy-start.17
  154.0 1.1 copy-start.18
  154.0 1.1 copy-start.29
  154.0 1.1 copy-start.30
  154.0 1.2 copy-start.5
  154.0 1.2 copy-start.24
  154.0 1.2 copy-start.27
  154.8 1.3 copy-start.6
  154.8 1.3 copy-start.26
  155.2 1.3 copy-start.3
  155.2 1.3 copy-start.14
  155.2 1.3 copy-start.28
  155.7 1.4 copy-start.4
  155.7 1.5 copy-start.8
  155.7 1.5 copy-start.21
  155.7 1.5 copy-start.25
  157.6 2.6 dynamic-slice-start
  160.3 3.0 copy-start.35
  162.1 161.3 %all-gather.5.cloned.1.call-start = ((), (), s32[]{:S(2)}) async-start(), calls=%async_computation.2 | async-start | bytes 17301504 | tf_op jit(solution)/shard_map/all_gather | solution.py:165
  163.0 320.1 %all-reduce.2.cloned.1.call-start = ((), (), s32[]{:S(2)}) async-start(), calls=%async_computation.3 | async-start | bytes 1048576 | tf_op jit(solution)/shard_map/psum | solution.py:182
  163.3 172.7 %copy-start.13 = (bf16[512,1024]{1,0:T(8,128)(2,1)S(1)}, bf16[512,1024]{1,0:T(8,128)(2,1)}, u32[]{:S(2)}) copy-start(bf16[512,1024]{1,0:T(8,128)(2,1)} %param.29) | copy-start | bytes 3145732
  336.6 0.8 copy-start.7
  337.4 148.5 %copy-start.23 = (f32[4096]{0:T(1024)S(1)}, f32[4096]{0:T(1024)}, u32[]{:S(2)}) copy-start(f32[4096]{0:T(1024)} %param.31) | copy-start | bytes 49156
Sparse Core Ops, SparseCore 0:
  162.2 84.0 all-gather.2
  249.2 74.1 all-gather.4
  337.6 145.5 all-reduce.1

commit v5 on v2

--- a/solution.py
+++ b/solution.py
@@ -164,20 +164,25 @@
     w_cols = lax.dynamic_slice_in_dim(w_out, place * width, width, axis=1)
     w_full = lax.all_gather(w_cols, "req", axis=0, tiled=True)
     gated_all = lax.all_gather(gated, "seq", axis=1, tiled=True)
-    mixer = jnp.dot(gated_all, w_full, preferred_element_type=jnp.float32).astype(jnp.bfloat16)
-    layer_out = (resid.astype(jnp.float32) + mixer.astype(jnp.float32)).astype(jnp.bfloat16)
 
     group_pos = jnp.arange(group_rows, dtype=jnp.int32)
     picker = (group_pos[None, :] == (ends - 1)[:, None]).astype(jnp.bfloat16)
-    picked_rows = jnp.dot(picker, layer_out, preferred_element_type=jnp.float32).astype(
-        jnp.bfloat16
-    )
+    picked_gated = jnp.dot(picker, gated, preferred_element_type=jnp.float32).astype(jnp.bfloat16)
+    picked_gated = lax.all_gather(picked_gated, "seq", axis=1, tiled=True)
+    picked_resid = jnp.dot(picker, resid, preferred_element_type=jnp.float32)
+    picked_mixer = jnp.dot(picked_gated, w_full, preferred_element_type=jnp.float32)
+    picked_rows = (
+        picked_resid + picked_mixer.astype(jnp.bfloat16).astype(jnp.float32)
+    ).astype(jnp.bfloat16)
     row_pair = lax.all_gather(picked_rows, "seq", axis=1, tiled=True)
     collected = lax.all_gather(row_pair, "req", axis=0, tiled=True)
     last_rows = collected.astype(jnp.float32)
     meansq = jnp.mean(last_rows * last_rows, axis=-1, keepdims=True)
     normed = (last_rows * lax.rsqrt(meansq + 1e-05) * final_gain[None, :]).astype(jnp.bfloat16)
     logits = jnp.dot(normed, head_weight, preferred_element_type=jnp.float32)
+
+    mixer = jnp.dot(gated_all, w_full, preferred_element_type=jnp.float32).astype(jnp.bfloat16)
+    layer_out = (resid.astype(jnp.float32) + mixer.astype(jnp.float32)).astype(jnp.bfloat16)
     return (layer_out, logits)
 
 

time: 397 us -> 275 us (0.69)
  waiting for transfers between devices: 205 us -> 65 us
  matrix products: 50.2 us -> 76.9 us
  blocking collectives: 39.1 us -> 50.6 us
  local copies, waits for them, and re-layouts: 55.9 us -> 46.2 us
  other arithmetic: 20.2 us -> 11.4 us
    all_gather x1, waiting for transfers between devices: 77.1 us -> 0.02 us  [mixer_layer(): w_full = lax.all_gather(w_cols, 'req', axis=0, tiled=True)]
    all_gather x1, waiting for transfers between devices: 83.2 us -> 18.6 us  [mixer_layer(): gated_all = lax.all_gather(gated, 'seq', axis=1, tiled=True)]
    dot_general x1 -> x3, matrix products: 0.28 us -> 12 us  [the longest x1 9.45 us: mixer_layer(): jnp.dot(picked_gated, w_full, preferred_element_type=jnp.float32)]
    all_gather x0 -> x1, blocking collectives: none -> 9.41 us  [mixer_layer(): picked_gated = lax.all_gather(picked_gated, 'seq', axis=1, tiled=True)]
    dot_general x3, matrix products: 1.19 us -> 7.36 us  [carry_term(): jnp.einsum('tgn,gkpn->tgkp', cmat, lower, preferred_element_type=jnp.floa...]
    dot_general x4, matrix products: 1.19 us -> 6.61 us  [carry_term(): jnp.einsum('tgn,gkpn->tgkp', cmat, upper, preferred_element_type=jnp.floa...]
    unnamed x91 -> x95, local copies, waits for them, and re-layouts: 17.4 us -> 19 us
  transfers between devices with their start and end apart: 3 -> 3, of which waited for: 3 -> 2; matrix products, arithmetic and copies ran while one was open for 2% -> 41% of each run, Pallas kernels for 0% -> 0%
where the time goes in v5:
time: 275 us; the launch traced here: 274 us
  matrix products  76.9 us (28%)
  waiting for transfers between devices  65 us (24%)
  blocking collectives  50.6 us (18%)
  local copies, waits for them, and re-layouts  46.2 us (17%)
  between operations  17.9 us (7%)
  other arithmetic  11.4 us (4%)
  starting transfers between devices  5.38 us (2%)
    all_to_all x1, waiting for transfers between devices, mixer_layer(): lax.all_to_all(packed, 'seq', split_axis=0, concat_axis=0, tiled=True)  46.4 us
    all_gather x1, blocking collectives, mixer_layer(): collected = lax.all_gather(row_pair, 'req', axis=0, tiled=True)  30.7 us
    unnamed x95, local copies, waits for them, and re-layouts  19 us
    all_gather x1, waiting for transfers between devices, mixer_layer(): gated_all = lax.all_gather(gated, 'seq', axis=1, tiled=True)  18.6 us
    dot_general x8, matrix products, group_inner(): jnp.einsum('tsk,skp->tkp', lower, x_g, preferred_element_type=jnp.float32)  17.1 us
    dot_general x1, matrix products, mixer_layer(): jnp.dot(gated_all, w_full, preferred_element_type=jnp.float32)  15.7 us
    dot_general x8, matrix products, group_inner(): jnp.einsum('tsk,skp->tkp', upper, x_g, preferred_element_type=jnp.float32)  11.9 us
    all_gather x1, blocking collectives, mixer_layer(): row_pair = lax.all_gather(picked_rows, 'seq', axis=1, tiled=True)  10.5 us
  transfers between devices with their start and end apart: 3, of which 2 were waited for; matrix products, arithmetic and copies ran while one was open for 41% of the time, Pallas kernels for 0%

profile of v5, /device:TPU:1, one launch (start us, length us, event | category | flops | bytes accessed | tf_op | source)
XLA Modules:
  0.0 273.6 jit_solution(6157112720607279057)
XLA Ops:
  7.2 1.5 copy-done
  8.8 0.8 constant_dynamic-slice_fusion
  9.6 1.1 fusion.158
  10.9 4.1 %copy.214 = bf16[128,8192]{0,1:T(8,128)(2,1)} copy(bf16[128,8192]{1,0:T(8,128)(2,1)} %param.21) | data formatting | bytes 4194304 | tf_op args[0]
  15.0 3.2 %copy.215 = bf16[128,8192]{0,1:T(8,128)(2,1)S(1)} copy(bf16[128,8192]{1,0:T(8,128)(2,1)} %param.23) | data formatting | bytes 4194304 | tf_op args[2]
  18.5 3.3 %constant_dynamic-update-slice_fusion.4 = bf16[4,128,4640]{1,2,0:T(8,128)(2,1)} fusion(bf16[4,128,2048]{1,2,0:T(8,128)(2,1)} %bitcast.321), kind=kLoop, calls=%fused_computation.212 | loop fusion | bytes 4194304
  21.8 1.7 constant_dynamic-update-slice_fusion.3
  23.5 0.8 constant_dynamic-update-slice_fusion.2
  24.3 0.8 constant_dynamic-update-slice_fusion.1
  25.7 5.1 %all-to-all-start = ((bf16[4,128,4640]{1,2,0:T(8,128)(2,1)}), bf16[4,128,4640]{1,2,0:T(8,128)(2,1)}, u32[]{:S(2)}, u32[]{:S(2)}) async-start(bf16[4,128,4640]{1,2,0:T(8,128)(2,1)} %constant_dynamic-update-slice_fusion), calls=%async_computation | async-start | bytes 9502720 | tf_op jit(solution)/shard_map/all_to_all | solution.py:124
  36.2 1.9 compare_convert_fusion.7
  38.2 0.7 fusion.149
  39.6 46.4 %all-to-all-done = bf16[4,128,4640]{1,2,0:T(8,128)(2,1)} async-done(((bf16[4,128,4640]{1,2,0:T(8,128)(2,1)}), bf16[4,128,4640]{1,2,0:T(8,128)(2,1)}, u32[]{:S(2)}, u32[]{:S(2)}) %all-to-all-start) | async-done | bytes 4751392 | tf_op jit(solution)/shard_map/all_to_all | solution.py:124
  85.9 2.7 copy_bitcast_fusion
  88.7 2.2 copy-done.2
  97.2 1.1 fusion.156
  98.4 0.9 fusion.162
  99.9 2.5 fusion.157
  103.8 1.3 fusion.144
  105.4 1.3 fusion.141
  107.0 1.3 fusion.138
  108.9 1.2 broadcast.230.clone.3
  110.1 12.2 %while.40 = (s32[]{:T(128)}, f32[2,128,16,64]{1,3,2,0:T(8,128)}, bf16[2,128,16,64]{1,3,2,0:T(8,128)(2,1)}, pred[2,128,128]{2,1,0:T(8,128)(4,1)}, f32[2,128,16]{1...) while((s32[]{:T(128)}, f32[2,128,16,64]{1,3,2,0:T(8,128)}, ...), condition=%wide.region_4.5_spmd, body=%wide.region_3.4_spmd.sunk | while | flops 71172096 | bytes 2508385 | solution.py:45
  110.8 0.8 dynamic-slice_bitcast_fusion.29
  111.7 0.7 dynamic-slice_bitcast_fusion.30
  112.4 1.5 fusion.219
  113.9 2.3 fusion.220
  116.9 0.8 dynamic-slice_bitcast_fusion.29
  118.5 1.5 fusion.219
  120.0 2.4 fusion.220
  122.3 2.8 %fusion.89 = f32[128,2,16,64]{0,3,2,1:T(8,128)} fusion(bf16[128,2,128,1]{0,2,3,1:T(8,128)(2,1)} %bitcast.362, bf16[128,2,16,64]{0,3,2,1:T(8,128)(2,1)} %bitcast.325, f32[2,128,16,64]{1,3,2,0:T(8,128)} %get-tuple-element.150, f32[128]{0:T(128)} %copy-done.35, f32[128,2,16]{0,2,1:T(8,128)} %exponential_multiply_fusion.3, f32[2,16]{1,0:T(2,128)} %mul.478), kind=kOutput, calls=%fused_computation.118 | convolution fusion | flops 68943872 | bytes 2704000 | tf_op jit(solution)/shard_map/tgn,gkpn->tgkp/dot_general | solution.py:69
  125.1 1.3 broadcast_in_dim.70
  126.4 1.2 broadcast.230.clone.2
  127.6 10.6 %while.41 = (s32[]{:T(128)}, f32[2,128,16,64]{1,3,2,0:T(8,128)}, bf16[2,128,16,64]{1,3,2,0:T(8,128)(2,1)}, pred[2,128,128]{2,1,0:T(8,128)(4,1)}, f32[2,128,16]{1...) while((s32[]{:T(128)}, f32[2,128,16,64]{1,3,2,0:T(8,128)}, ...), condition=%wide.region_7.8_spmd, body=%wide.region_6.7_spmd.sunk | while | flops 71172096 | bytes 2508385 | solution.py:45
  127.6 0.7 dynamic-slice_bitcast_fusion.31
  129.1 1.5 fusion.224
  130.6 2.3 fusion.225
  134.4 1.5 fusion.224
  135.9 2.4 fusion.225
  138.2 3.1 %fusion.103 = f32[128,2,16,64]{0,3,2,1:T(8,128)} fusion(f32[2,16,64,128]{3,2,1,0:T(8,128)} %fusion.144, bf16[128,2,128,1]{0,2,3,1:T(8,128)(2,1)} %bitcast.349, bf16[128,2,16,64]{0,3,2,1:T(8,128)(2,1)} %bitcast.333, f32[2,128,16,64]{1,3,2,0:T(8,128)} %get-tuple-element.151, f32[2,16,64,128]{3,2,1,0:T(8,128)S(1)} %fusion.104, f32[128]{0:T(128)} %copy-done.34, ...), kind=kOutput, calls=%fused_computation.137 | convolution fusion | flops 69992448 | bytes 4801152 | tf_op jit(solution)/shard_map/tgn,gkpn->tgkp/dot_general | solution.py:70
  141.5 6.2 %while.42 = (s32[]{:T(128)}, f32[2,128,16,64]{1,3,2,0:T(8,128)S(1)}, bf16[2,128,16,64]{1,3,2,0:T(8,128)(2,1)}, pred[2,128,128]{2,1,0:T(8,128)(4,1)S(1)}, f32[2,1...) while((s32[]{:T(128)}, ...), condition=%wide.region_10.11_spmd, body=%wide.region_9.10_spmd.sunk | while | flops 71172096 | bytes 2508385 | solution.py:45
  141.6 1.5 fusion.229
  143.1 1.5 fusion.230
  144.7 1.5 fusion.229
  146.2 1.5 fusion.230
  147.8 1.0 copy-done.8
  148.8 2.1 fusion.98
  150.9 1.1 broadcast.230.clone
  152.1 7.8 %while.43 = (s32[]{:T(128)}, f32[2,128,16,64]{1,3,2,0:T(8,128)}, bf16[2,128,16,64]{1,3,2,0:T(8,128)(2,1)}, pred[2,128,128]{2,1,0:T(8,128)(4,1)S(1)}, f32[2,128,1...) while((s32[]{:T(128)}, f32[2,128,16,64]{1,3,2,0:T(8,128)}, ...), condition=%wide.region_13.14_spmd, body=%wide.region_12.13_spmd.sunk | while | flops 71172096 | bytes 2508385 | solution.py:45
  152.1 1.5 fusion.234
  153.6 2.3 fusion.235
  156.0 1.5 fusion.234
  157.5 2.3 fusion.235
  159.9 2.2 fusion.93
  162.2 2.6 bitcast_reduce_fusion
  164.8 1.8 fusion.85
  166.6 2.2 convolution_convert_fusion
  168.9 9.4 %all_gather.17 = bf16[2,8192]{1,0:T(2,128)(2,1)S(1)} all-gather(bf16[2,2048]{1,0:T(2,128)(2,1)S(1)} %convolution_convert_fusion), channel_id=1, replica_groups=mesh['req'=32,'seq'=4] {'seq'}, dimensions={1}, use_global_device_ids=true | all-gather | bytes 40960 | tf_op jit(solution)/shard_map/all_gather | solution.py:171
  178.3 9.4 %fusion.111 = f32[2,1024]{1,0:T(2,128)S(1)} fusion(bf16[2,8192]{1,0:T(2,128)(2,1)S(1)} %all_gather.17, bf16[8192,1024]{1,0:T(8,128)(2,1)} %all-gather.6.cloned.1.call-done), kind=kOutput, calls=%fused_computation.154 | convolution fusion | flops 33558528 | bytes 16818176 | tf_op jit(solution)/shard_map/dot_general | solution.py:173
  188.1 10.5 %all_gather.18 = bf16[2,4096]{1,0:T(2,128)(2,1)S(1)} all-gather(bf16[2,1024]{1,0:T(2,128)(2,1)S(1)} %fusion.112), channel_id=1, replica_groups=mesh['req'=32,'seq'=4] {'seq'}, dimensions={1}, use_global_device_ids=true | all-gather | bytes 20480 | tf_op jit(solution)/shard_map/all_gather | solution.py:177
  198.6 30.7 %all-gather = bf16[32,2,4096]{2,1,0:T(2,128)(2,1)S(1)} all-gather(bf16[1,2,4096]{2,1,0:T(2,128)(2,1)S(1)} %bitcast.381), channel_id=1, replica_groups=mesh['req'=32,'seq'=4] {'req'}, dimensions={0}, use_global_device_ids=true | all-gather | bytes 540672 | tf_op jit(solution)/shard_map/all_gather | solution.py:178
  229.6 2.8 %fusion.119 = f32[64,256]{1,0:T(8,128)} fusion(bf16[4096,256]{1,0:T(8,128)(2,1)} %param.32, f32[64,4096]{1,0:T(8,128)S(1)} %reshape.471, f32[4096]{0:T(1024)S(1)} %copy-done.29, f32[64]{0:T(128)S(1)} %add_rsqrt_fusion.1), kind=kOutput, calls=%fused_computation.168 | convolution fusion | flops 135004160 | bytes 3227904 | tf_op jit(solution)/shard_map/dot_general | solution.py:182
  232.4 18.6 %all-gather.4.cloned.1.call-done = bf16[512,8192]{0,1:T(8,128)(2,1)} async-done(((bf16[512,2048]{0,1:T(8,128)(2,1)}), bf16[512,8192]{0,1:T(8,128)(2,1)}) %all-gather.4.cloned.1.call-update) | async-done | bytes 8388624 | tf_op jit(solution)/shard_map/all_gather | solution.py:166
  251.0 15.7 %add_convert_fusion = bf16[512,1024]{1,0:T(8,128)(2,1)} fusion(bf16[512,1024]{1,0:T(8,128)(2,1)S(1)} %copy-done.14, bf16[512,8192]{0,1:T(8,128)(2,1)} %all-gather.4.cloned.1.call-done, bf16[8192,1024]{1,0:T(8,128)(2,1)} %all-gather.6.cloned.1.call-done), kind=kOutput, calls=%fused_computation.112 | convolution fusion | flops 8592556032 | bytes 27262976 | tf_op jit(solution)/shard_map/dot_general | solution.py:184
  (170 shorter events, 18.8 us)
Async XLA Ops:
  7.2 1.6 copy-start
  7.2 171.1 %all-gather.6.cloned.1.call-start = ((), (), s32[]{:S(2)}) async-start(), calls=%async_computation.2 | async-start | bytes 17301504 | tf_op jit(solution)/shard_map/all_gather | solution.py:165
  10.9 7.5 %copy-start.28 = (bf16[128,128]{1,0:T(8,128)(2,1)S(1)}, bf16[128,128]{1,0:T(8,128)(2,1)}, u32[]{:S(2)}) copy-start(bf16[128,128]{1,0:T(8,128)(2,1)} %param.24) | copy-start | bytes 98308
  25.7 5.4 %copy-start.40 = (s32[1,2]{1,0:T(1,128)S(1)}, s32[1,2]{1,0:T(1,128)}, u32[]{:S(2)}) copy-start(s32[1,2]{1,0:T(1,128)} %param.33) | copy-start | bytes 28
  25.7 9.5 %copy-start.41 = (f32[128]{0:T(128)S(1)}, f32[128]{0:T(128)}, u32[]{:S(2)}) copy-start(f32[128]{0:T(128)} %param.25) | copy-start | bytes 1540
  25.7 9.6 %copy-start.42 = (f32[128]{0:T(128)S(1)}, f32[128]{0:T(128)}, u32[]{:S(2)}) copy-start(f32[128]{0:T(128)} %param.27) | copy-start | bytes 1540
  25.7 10.4 %copy-start.43 = (f32[128]{0:T(128)S(1)}, f32[128]{0:T(128)}, u32[]{:S(2)}) copy-start(f32[128]{0:T(128)} %param.26) | copy-start | bytes 1540
  25.7 60.2 %all-to-all-start = ((bf16[4,128,4640]{1,2,0:T(8,128)(2,1)}), bf16[4,128,4640]{1,2,0:T(8,128)(2,1)}, u32[]{:S(2)}, u32[]{:S(2)}) async-start(bf16[4,128,4640]{1,2,0:T(8,128)(2,1)} %constant_dynamic-update-slice_fusion), calls=%async_computation | async-start | bytes 9502720 | tf_op jit(solution)/shard_map/all_to_all | solution.py:124
  30.9 220.1 %all-gather.4.cloned.1.call-start = ((), (), s32[]{:S(2)}) async-start(), calls=%async_computation.1 | async-start | bytes 10485760 | tf_op jit(solution)/shard_map/all_gather | solution.py:166
  31.3 4.8 %copy-start.38 = (s32[2,1]{0,1:T(1,128)}, s32[2,1]{0,1:T(1,128)S(1)}, u32[]{:S(2)}) copy-start(s32[2,1]{0,1:T(1,128)S(1)} %reduce-window.7) | copy-start | bytes 28
  36.2 60.4 %copy-start.31 = (f32[128]{0:T(128)}, f32[128]{0:T(128)S(1)}, u32[]{:S(2)}) copy-start(f32[128]{0:T(128)S(1)} %get-tuple-element.304) | copy-start | bytes 1540
  36.2 60.4 %copy-start.33 = (f32[128]{0:T(128)}, f32[128]{0:T(128)S(1)}, u32[]{:S(2)}) copy-start(f32[128]{0:T(128)S(1)} %get-tuple-element.305) | copy-start | bytes 1540
  36.2 60.4 %copy-start.34 = (f32[128]{0:T(128)}, f32[128]{0:T(128)S(1)}, u32[]{:S(2)}) copy-start(f32[128]{0:T(128)S(1)} %get-tuple-element.306) | copy-start | bytes 1540
  36.2 60.4 %copy-start.35 = (f32[128]{0:T(128)}, f32[128]{0:T(128)S(1)}, u32[]{:S(2)}) copy-start(f32[128]{0:T(128)S(1)} %get-tuple-element.307) | copy-start | bytes 1540
  88.7 2.2 copy-start.2
  91.8 10.9 %copy-start.18 = (f32[128,32]{0,1:T(8,128)}, f32[128,32]{0,1:T(8,128)S(1)}, u32[]{:S(2)}) copy-start(f32[128,32]{0,1:T(8,128)S(1)} %copy.226) | copy-start | bytes 49156
  92.1 10.7 %copy-start.16 = (f32[128,32]{0,1:T(8,128)}, f32[128,32]{0,1:T(8,128)S(1)}, u32[]{:S(2)}) copy-start(f32[128,32]{0,1:T(8,128)S(1)} %copy.235) | copy-start | bytes 49156
  98.3 4.8 %copy-start.15 = (bf16[128,256]{0,1:T(8,128)(2,1)}, bf16[128,256]{0,1:T(8,128)(2,1)S(1)}, u32[]{:S(2)}) copy-start(bf16[128,256]{0,1:T(8,128)(2,1)S(1)} %get-tuple-element.261) | copy-start | bytes 196612
  98.3 5.4 %copy-start.13 = (bf16[128,256]{0,1:T(8,128)(2,1)}, bf16[128,256]{0,1:T(8,128)(2,1)S(1)}, u32[]{:S(2)}) copy-start(bf16[128,256]{0,1:T(8,128)(2,1)S(1)} %get-tuple-element.267) | copy-start | bytes 196612
  98.4 7.0 %copy-start.11 = (bf16[128,256]{0,1:T(8,128)(2,1)}, bf16[128,256]{0,1:T(8,128)(2,1)S(1)}, u32[]{:S(2)}) copy-start(bf16[128,256]{0,1:T(8,128)(2,1)S(1)} %get-tuple-element.265) | copy-start | bytes 196612
  98.4 8.7 %copy-start.9 = (bf16[128,256]{0,1:T(8,128)(2,1)}, bf16[128,256]{0,1:T(8,128)(2,1)S(1)}, u32[]{:S(2)}) copy-start(bf16[128,256]{0,1:T(8,128)(2,1)S(1)} %get-tuple-element.263) | copy-start | bytes 196612
  102.4 2.6 copy-start.3
  102.4 2.6 copy-start.5
  102.4 4.3 %copy-start.4 = (bf16[128,2048]{0,1:T(8,128)(2,1)}, bf16[128,2048]{0,1:T(8,128)(2,1)S(1)}, u32[]{:S(2)}) copy-start(bf16[128,2048]{0,1:T(8,128)(2,1)S(1)} %get-tuple-element.270) | copy-start | bytes 1572868
  102.8 2.3 copy-start.36
  103.7 3.0 %copy-start.37 = (f32[2,16]{1,0:T(2,128)S(1)}, f32[2,16]{1,0:T(2,128)}, u32[]{:S(2)}) copy-start(f32[2,16]{1,0:T(2,128)} %mul.535) | copy-start | bytes 388
  105.4 2.9 %copy-start.27 = (pred[128,128]{1,0:T(8,128)(4,1)S(1)}, pred[128,128]{1,0:T(8,128)(4,1)}, u32[]{:S(2)}) copy-start(pred[128,128]{1,0:T(8,128)(4,1)} %get-tuple-element.315) | copy-start | bytes 49156
  127.6 10.6 %copy-start.24 = (f32[128,2,16]{0,2,1:T(8,128)S(1)}, f32[128,2,16]{0,2,1:T(8,128)}, u32[]{:S(2)}) copy-start(f32[128,2,16]{0,2,1:T(8,128)} %get-tuple-element.309) | copy-start | bytes 49156
  138.2 3.1 %copy-start.26 = (pred[128,128]{1,0:T(8,128)(4,1)S(1)}, pred[128,128]{1,0:T(8,128)(4,1)}, u32[]{:S(2)}) copy-start(pred[128,128]{1,0:T(8,128)(4,1)} %get-tuple-element.313) | copy-start | bytes 49156
  138.2 3.3 %copy-start.17 = (f32[128,32]{0,1:T(8,128)S(1)}, f32[128,32]{0,1:T(8,128)}, u32[]{:S(2)}) copy-start(f32[128,32]{0,1:T(8,128)} %copy-done.16) | copy-start | bytes 49156
  138.2 3.3 %copy-start.20 = (f32[128,32]{0,1:T(8,128)S(1)}, f32[128,32]{0,1:T(8,128)}, u32[]{:S(2)}) copy-start(f32[128,32]{0,1:T(8,128)} %get-tuple-element.289) | copy-start | bytes 49156
  141.5 7.3 %copy-start.12 = (bf16[128,256]{0,1:T(8,128)(2,1)S(1)}, bf16[128,256]{0,1:T(8,128)(2,1)}, u32[]{:S(2)}) copy-start(bf16[128,256]{0,1:T(8,128)(2,1)} %copy-done.11) | copy-start | bytes 196612
  141.5 7.3 %copy-start.23 = (f32[128,2,16]{0,2,1:T(8,128)S(1)}, f32[128,2,16]{0,2,1:T(8,128)}, u32[]{:S(2)}) copy-start(f32[128,2,16]{0,2,1:T(8,128)} %get-tuple-element.308) | copy-start | bytes 49156
  147.7 1.1 copy-start.8
  147.7 3.1 %copy-start.25 = (pred[128,128]{1,0:T(8,128)(4,1)S(1)}, pred[128,128]{1,0:T(8,128)(4,1)}, u32[]{:S(2)}) copy-start(pred[128,128]{1,0:T(8,128)(4,1)} %get-tuple-element.312) | copy-start | bytes 49156
  147.8 4.3 %copy-start.19 = (f32[128,32]{0,1:T(8,128)S(1)}, f32[128,32]{0,1:T(8,128)}, u32[]{:S(2)}) copy-start(f32[128,32]{0,1:T(8,128)} %get-tuple-element.279) | copy-start | bytes 49156
  147.8 4.3 %copy-start.21 = (f32[2,128,16]{1,2,0:T(8,128)S(1)}, f32[2,128,16]{1,2,0:T(8,128)}, u32[]{:S(2)}) copy-start(f32[2,128,16]{1,2,0:T(8,128)} %copy.246) | copy-start | bytes 49156
  152.0 7.8 %copy-start.10 = (bf16[128,256]{0,1:T(8,128)(2,1)S(1)}, bf16[128,256]{0,1:T(8,128)(2,1)}, u32[]{:S(2)}) copy-start(bf16[128,256]{0,1:T(8,128)(2,1)} %copy-done.9) | copy-start | bytes 196612
  152.0 7.8 %copy-start.22 = (f32[128,2,16]{0,2,1:T(8,128)S(1)}, f32[128,2,16]{0,2,1:T(8,128)}, u32[]{:S(2)}) copy-start(f32[128,2,16]{0,2,1:T(8,128)} %copy.252) | copy-start | bytes 49156
  152.1 7.8 %copy-start.30 = (f32[2,16]{1,0:T(2,128)S(1)}, f32[2,16]{1,0:T(2,128)}, u32[]{:S(2)}) copy-start(f32[2,16]{1,0:T(2,128)} %mul.478) | copy-start | bytes 388
  152.1 7.8 %copy-start.32 = (f32[128]{0:T(128)S(1)}, f32[128]{0:T(128)}, u32[]{:S(2)}) copy-start(f32[128]{0:T(128)} %copy-done.31) | copy-start | bytes 1540
  159.8 2.2 copy-start.6
  159.8 2.3 copy-start.7
  162.2 2.6 dynamic-slice-start
  164.8 1.8 copy-start.39
  178.3 9.5 %copy-start.14 = (bf16[512,1024]{1,0:T(8,128)(2,1)S(1)}, bf16[512,1024]{1,0:T(8,128)(2,1)}, u32[]{:S(2)}) copy-start(bf16[512,1024]{1,0:T(8,128)(2,1)} %param.29) | copy-start | bytes 3145732
  187.8 41.9 %copy-start.29 = (f32[4096]{0:T(1024)S(1)}, f32[4096]{0:T(1024)}, u32[]{:S(2)}) copy-start(f32[4096]{0:T(1024)} %param.31) | copy-start | bytes 49156
  251.0 15.7 %copy-start.1 = (bf16[256,4096]{1,0:T(8,128)(2,1)S(1)}, bf16[256,4096]{1,0:T(8,128)(2,1)}, u32[]{:S(2)}) copy-start(bf16[256,4096]{1,0:T(8,128)(2,1)} %param.30) | copy-start | bytes 6291460
Sparse Core Ops, SparseCore 0:
  10.2 76.2 all-gather.5
  166.7 84.2 all-gather.3

commit v6 on v3

--- a/solution.py
+++ b/solution.py
@@ -104,27 +104,7 @@
     heads_all = a_log.shape[0]
     heads = heads_all // seq_count
     groups = NGROUPS // seq_count
-    share = inner // seq_count
-    bshare = groups * STATE
     group_rows = rows * seq_count
-
-    def by_dest(part, width):
-        return part.reshape(rows, seq_count, width).transpose(1, 0, 2)
-
-    def to_heads(part, width):
-        moved = lax.all_to_all(by_dest(part, width), "seq", split_axis=0, concat_axis=0, tiled=True)
-        return moved.reshape(group_rows, width)
-
-    xg = to_heads(xs, share)
-    bg = to_heads(bc[:, : NGROUPS * STATE], bshare)
-    cg = to_heads(bc[:, NGROUPS * STATE :], bshare)
-    dg = to_heads(dt_raw, heads)
-    zg = to_heads(zgate, share)
-
-    my_heads = lambda v: lax.dynamic_slice_in_dim(v, place * heads, heads)
-    rate = jnp.exp(my_heads(a_log))
-    skipw = my_heads(d_skip)
-    steps_dt = jax.nn.softplus(dg.astype(jnp.float32) + my_heads(dt_bias)[None, :])
 
     lens = lengths[0]
     slots = lens.shape[0]
@@ -132,46 +112,99 @@
     positions = jnp.arange(group_rows, dtype=jnp.int32)
     segment = jnp.sum((positions[:, None] >= ends[None, :]).astype(jnp.int32), axis=1)
     live = segment < slots
-
-    gain = lax.dynamic_slice_in_dim(norm_gain, place * share, share)
+    group_pos = jnp.arange(group_rows, dtype=jnp.int32)
+    picker = (group_pos[None, :] == (ends - 1)[:, None]).astype(jnp.bfloat16)
+
     width = resid.shape[1]
     w_cols = lax.dynamic_slice_in_dim(w_out, place * width, width, axis=1)
     w_full = lax.all_gather(w_cols, "req", axis=0, tiled=True)
-
-    state_in = jnp.zeros((heads, HEAD_DIM, STATE), jnp.float32)
-    prev_seg = jnp.array(-1, jnp.int32)
-    inputs = (xg, bg, cg, steps_dt)
-    mixers = []
-    for chunk in range(seq_count):
-        lo, hi = chunk * rows, (chunk + 1) * rows
-        xb, bb, cb, db = (part[lo:hi] for part in inputs)
-        if chunk > 0:
-            xb, bb, cb, db = lax.optimization_barrier((xb, bb, cb, db, gated))[:4]
-        local, keep, state, carry_w, cmat = block_terms(
-            xb, bb, cb, db, segment[lo:hi], live[lo:hi], prev_seg, rate, skipw, groups,
+    w_blocks = w_full.reshape(seq_count, groups, inner // NGROUPS, width)
+
+    block_cols = inner // NGROUPS
+    block_heads = heads // groups
+
+    def by_dest(part, width_of, half):
+        piece = part.reshape(rows, seq_count, groups, width_of)[:, :, half, :]
+        return piece.transpose(1, 0, 2)
+
+    moves = []
+    for half in range(groups):
+        packed = jnp.concatenate(
+            [
+                by_dest(xs, block_cols, half),
+                by_dest(zgate, block_cols, half),
+                by_dest(bc[:, : NGROUPS * STATE], STATE, half),
+                by_dest(bc[:, NGROUPS * STATE :], STATE, half),
+                by_dest(dt_raw, block_heads, half),
+            ],
+            axis=2,
         )
-        y4 = (local + carry_term(state_in, cmat, carry_w, groups)) * live[lo:hi].astype(
-            jnp.float32
-        )[:, None, None, None]
-        state_in = keep[:, None, None] * state_in + state
-        prev_seg = segment[hi - 1]
-        gated = gate_norm(y4.reshape(rows, share), zg[lo:hi], gain, groups)
-        gated_all = lax.all_gather(gated, "seq", axis=1, tiled=True)
-        mixers.append(jnp.dot(gated_all, w_full, preferred_element_type=jnp.float32))
-    mixer = jnp.concatenate(mixers, axis=0).astype(jnp.bfloat16)
-    layer_out = (resid.astype(jnp.float32) + mixer.astype(jnp.float32)).astype(jnp.bfloat16)
-
-    group_pos = jnp.arange(group_rows, dtype=jnp.int32)
-    picker = (group_pos[None, :] == (ends - 1)[:, None]).astype(jnp.bfloat16)
-    picked_rows = jnp.dot(picker, layer_out, preferred_element_type=jnp.float32).astype(
-        jnp.bfloat16
-    )
+        moves.append(lax.all_to_all(packed, "seq", split_axis=0, concat_axis=0, tiled=True))
+
+    gated_parts = []
+    picked_parts = []
+    for half in range(groups):
+        moved = moves[half]
+        if half > 0:
+            moved = lax.optimization_barrier((moved, gated))[0]
+        moved = moved.reshape(group_rows, -1)
+        xg = moved[:, :block_cols]
+        zg = moved[:, block_cols : 2 * block_cols]
+        bg = moved[:, 2 * block_cols : 2 * block_cols + STATE]
+        cg = moved[:, 2 * block_cols + STATE : 2 * block_cols + 2 * STATE]
+        dg = moved[:, 2 * block_cols + 2 * STATE :]
+
+        first_head = (place * groups + half) * block_heads
+        my_heads = lambda v: lax.dynamic_slice_in_dim(v, first_head, block_heads)
+        rate = jnp.exp(my_heads(a_log))
+        skipw = my_heads(d_skip)
+        steps_dt = jax.nn.softplus(dg.astype(jnp.float32) + my_heads(dt_bias)[None, :])
+
+        state_in = jnp.zeros((block_heads, HEAD_DIM, STATE), jnp.float32)
+        prev_seg = jnp.array(-1, jnp.int32)
+        ys = []
+        for chunk in range(seq_count):
+            lo, hi = chunk * rows, (chunk + 1) * rows
+            local, keep, state, carry_w, cmat = block_terms(
+                xg[lo:hi], bg[lo:hi], cg[lo:hi], steps_dt[lo:hi], segment[lo:hi], live[lo:hi],
+                prev_seg, rate, skipw, 1,
+            )
+            y4 = (local + carry_term(state_in, cmat, carry_w, 1)) * live[lo:hi].astype(
+                jnp.float32
+            )[:, None, None, None]
+            ys.append(y4.reshape(rows, block_cols))
+            state_in = keep[:, None, None] * state_in + state
+            prev_seg = segment[hi - 1]
+        y = jnp.concatenate(ys, axis=0)
+        gain = lax.dynamic_slice_in_dim(norm_gain, (place * groups + half) * block_cols, block_cols)
+        gated = gate_norm(y, zg, gain, 1)
+        gated_parts.append(lax.all_gather(gated, "seq", axis=1, tiled=True))
+        picked = jnp.dot(picker, gated, preferred_element_type=jnp.float32).astype(jnp.bfloat16)
+        picked_parts.append(lax.all_gather(picked, "seq", axis=1, tiled=True))
+
+    picked_resid = jnp.dot(picker, resid, preferred_element_type=jnp.float32)
+    picked_mixer = sum(
+        jnp.dot(picked_parts[half], w_blocks[:, half].reshape(-1, width),
+                preferred_element_type=jnp.float32)
+        for half in range(groups)
+    )
+    picked_rows = (
+        picked_resid + picked_mixer.astype(jnp.bfloat16).astype(jnp.float32)
+    ).astype(jnp.bfloat16)
     row_pair = lax.all_gather(picked_rows, "seq", axis=1, tiled=True)
     collected = lax.all_gather(row_pair, "req", axis=0, tiled=True)
     last_rows = collected.astype(jnp.float32)
     meansq = jnp.mean(last_rows * last_rows, axis=-1, keepdims=True)
     normed = (last_rows * lax.rsqrt(meansq + 1e-05) * final_gain[None, :]).astype(jnp.bfloat16)
     logits = jnp.dot(normed, head_weight, preferred_element_type=jnp.float32)
+
+    mixer_f32 = None
+    for half in range(groups):
+        part = jnp.dot(gated_parts[half], w_blocks[:, half].reshape(-1, width),
+                       preferred_element_type=jnp.float32)
+        mixer_f32 = part if mixer_f32 is None else mixer_f32 + part
+    mixer = mixer_f32.astype(jnp.bfloat16)
+    layer_out = (resid.astype(jnp.float32) + mixer.astype(jnp.float32)).astype(jnp.bfloat16)
     return (layer_out, logits)
 
 

time: 445 us -> 227 us (0.51)
  waiting for transfers between devices: 219 us -> 31.4 us
  matrix products: 73 us -> 47.4 us
  blocking collectives: 39.9 us -> 65.1 us
  other arithmetic: 26.4 us -> 12.5 us
  starting transfers between devices: 21.9 us -> 10 us
    all_gather x4 -> x2, waiting for transfers between devices: 103 us -> 0.01 us  [mixer_layer(): gated_parts.append(lax.all_gather(gated, 'seq', axis=1, tiled=True))]
    all_gather x1, waiting for transfers between devices: 75.5 us -> 0.01 us  [mixer_layer(): w_full = lax.all_gather(w_cols, 'req', axis=0, tiled=True)]
    unnamed x95 -> x43, local copies, waits for them, and re-layouts: 3.12 us -> 23.7 us
    all_gather x0 -> x2, blocking collectives: none -> 20.5 us  [mixer_layer(): picked_parts.append(lax.all_gather(picked, 'seq', axis=1, tiled=True))]
    all_to_all x5 -> x2, starting transfers between devices: 21.6 us -> 9.73 us  [mixer_layer(): lax.all_to_all(packed, 'seq', split_axis=0, concat_axis=0, tiled=True)]
    mul x27 -> x0, local copies, waits for them, and re-layouts: 9.56 us -> none  [the longest x16 2.98 us: group_inner(): weights = decay * scores_g[:, :, None] * inflow_g[None, :, :]]
    dot_general x5 -> x7, matrix products: 35.4 us -> 26 us  [the longest x2 21.3 us: mixer_layer(): jnp.dot(gated_parts[half], w_blocks[:, half].reshape(-1, width), preferre...]
    all_to_all x5 -> x2, waiting for transfers between devices: 39.1 us -> 31.4 us  [mixer_layer(): lax.all_to_all(packed, 'seq', split_axis=0, concat_axis=0, tiled=True)]
  transfers between devices with their start and end apart: 10 -> 5, of which waited for: 9 -> 2; matrix products, arithmetic and copies ran while one was open for 14% -> 35% of each run, Pallas kernels for 0% -> 0%
where the time goes in v6:
time: 227 us; the launch traced here: 226 us
  blocking collectives  65.1 us (29%)
  matrix products  47.4 us (21%)
  local copies, waits for them, and re-layouts  42 us (19%)
  waiting for transfers between devices  31.4 us (14%)
  between operations  17.7 us (8%)
  other arithmetic  12.5 us (6%)
  starting transfers between devices  10 us (4%)
    all_gather x1, blocking collectives, mixer_layer(): collected = lax.all_gather(row_pair, 'req', axis=0, tiled=True)  35.4 us
    all_to_all x2, waiting for transfers between devices, mixer_layer(): lax.all_to_all(packed, 'seq', split_axis=0, concat_axis=0, tiled=True)  31.4 us
    unnamed x43, local copies, waits for them, and re-layouts  23.7 us
    dot_general x2, matrix products, mixer_layer(): jnp.dot(gated_parts[half], w_blocks[:, half].reshape(-1, width), preferre...  21.3 us
    all_gather x2, blocking collectives, mixer_layer(): picked_parts.append(lax.all_gather(picked, 'seq', axis=1, tiled=True))  20.5 us
    all_to_all x2, starting transfers between devices, mixer_layer(): lax.all_to_all(packed, 'seq', split_axis=0, concat_axis=0, tiled=True)  9.73 us
    all_gather x1, blocking collectives, mixer_layer(): row_pair = lax.all_gather(picked_rows, 'seq', axis=1, tiled=True)  9.12 us
    slice x1, local copies, waits for them, and re-layouts, mixer_layer(): w_blocks[:, half].reshape(-1, width)  6.93 us
  transfers between devices with their start and end apart: 5, of which 2 were waited for; matrix products, arithmetic and copies ran while one was open for 35% of the time, Pallas kernels for 0%

profile of v6, /device:TPU:1, one launch (start us, length us, event | category | flops | bytes accessed | tf_op | source)
XLA Modules:
  0.0 226.1 jit_solution(6444778939979590185)
XLA Ops:
  7.2 1.5 copy-done
  8.8 0.9 constant_dynamic-slice_fusion
  9.7 1.0 copy.424
  10.7 1.1 fusion.303
  12.1 2.5 %copy.417 = bf16[128,8192]{0,1:T(8,128)(2,1)} copy(bf16[128,8192]{1,0:T(8,128)(2,1)S(1)} %copy-done.10) | data formatting | bytes 4194304 | tf_op args[0]
  14.6 3.2 %copy.418 = bf16[128,8192]{0,1:T(8,128)(2,1)S(1)} copy(bf16[128,8192]{1,0:T(8,128)(2,1)} %param.15) | data formatting | bytes 4194304 | tf_op args[2]
  17.8 2.9 %fusion.74 = (bf16[4,128,2320]{1,2,0:T(8,128)(2,1)}, bf16[4,128,2320]{1,2,0:T(8,128)(2,1)S(1)}) fusion(bf16[128,4,2,1024]{0,3,2,1:T(8,128)(2,1)} %bitcast.493), kind=kLoop, calls=%fused_computation.114 | loop fusion | bytes 4194304
  20.7 1.4 fusion.73
  22.0 0.7 fusion.167
  22.8 0.7 fusion.166
  23.5 0.6 constant_dynamic-update-slice_fusion.1
  24.1 1.4 copy-done.9
  25.5 5.1 %all-to-all-start = ((bf16[4,128,2320]{1,2,0:T(8,128)(2,1)}), bf16[4,128,2320]{1,2,0:T(8,128)(2,1)}, u32[]{:S(2)}, u32[]{:S(2)}) async-start(bf16[4,128,2320]{1,2,0:T(8,128)(2,1)} %copy-done.9), calls=%async_computation | async-start | bytes 4751360 | tf_op jit(solution)/shard_map/all_to_all | solution.py:142
  30.9 0.6 fusion.306
  34.9 0.7 fusion.304
  35.6 1.9 slice_convert_fusion
  37.8 21.9 %all-to-all-done = bf16[4,128,2320]{1,2,0:T(8,128)(2,1)} async-done(((bf16[4,128,2320]{1,2,0:T(8,128)(2,1)}), bf16[4,128,2320]{1,2,0:T(8,128)(2,1)}, u32[]{:S(2)}, u32[]{:S(2)}) %all-to-all-start) | async-done | bytes 2375712 | tf_op jit(solution)/shard_map/all_to_all | solution.py:142
  59.7 4.6 %all-to-all-start.1 = ((bf16[4,128,2320]{1,2,0:T(8,128)(2,1)}), bf16[4,128,2320]{1,2,0:T(8,128)(2,1)}, u32[]{:S(2)}, u32[]{:S(2)}) async-start(bf16[4,128,2320]{1,2,0:T(8,128)(2,1)} %get-tuple-element.243), calls=%async_computation.1 | async-start | bytes 4751360 | tf_op jit(solution)/shard_map/all_to_all | solution.py:142
  64.4 2.1 copy_bitcast_fusion.1
  66.5 1.4 copy-done.6
  70.2 1.7 subtract_convert_fusion.27
  71.9 0.4 copy-done.7
  72.7 0.5 fusion.143
  73.3 0.6 fusion.51
  75.2 0.5 fusion.149
  75.7 0.6 fusion.146
  78.5 0.6 fusion.53
  79.1 0.5 fusion.152
  79.7 0.6 fusion.57
  80.3 0.6 fusion.55
  80.9 0.7 multiply_reduce_fusion.1
  81.6 1.2 multiply_convert_fusion.1
  82.8 9.4 %all-to-all-done.1 = bf16[4,128,2320]{1,2,0:T(8,128)(2,1)} async-done(((bf16[4,128,2320]{1,2,0:T(8,128)(2,1)}), bf16[4,128,2320]{1,2,0:T(8,128)(2,1)}, u32[]{:S(2)}, u32[]{:S(2)}) %all-to-all-start.1) | async-done | bytes 2375712 | tf_op jit(solution)/shard_map/all_to_all | solution.py:142
  92.3 1.8 copy_bitcast_fusion
  94.1 1.5 copy-done.4
  97.2 1.0 fusion.194
  98.2 1.0 fusion.241
  99.1 1.0 fusion.231
  100.4 1.3 fusion.301
  102.4 0.5 fusion.155
  102.9 1.5 subtract_convert_fusion.21
  104.5 0.6 fusion.39
  105.9 0.5 fusion.161
  106.5 0.6 fusion.158
  107.0 0.6 fusion.164
  109.8 0.6 fusion.59
  110.4 0.6 fusion.63
  111.1 0.6 fusion.61
  111.7 0.7 multiply_reduce_fusion
  112.4 1.3 multiply_convert_fusion
  113.9 0.4 convolution_convert_fusion.1
  114.2 10.0 %all_gather.24 = bf16[2,4096]{1,0:T(2,128)(2,1)S(1)} all-gather(bf16[2,1024]{1,0:T(2,128)(2,1)S(1)} %convolution_convert_fusion.1), channel_id=1, replica_groups=mesh['req'=32,'seq'=4] {'seq'}, dimensions={1}, use_global_device_ids=true | all-gather | bytes 20480 | tf_op jit(solution)/shard_map/all_gather | solution.py:183
  124.2 1.6 convolution_convert_fusion
  125.8 10.5 %all_gather.25 = bf16[2,4096]{1,0:T(2,128)(2,1)S(1)} all-gather(bf16[2,1024]{1,0:T(2,128)(2,1)S(1)} %convolution_convert_fusion), channel_id=1, replica_groups=mesh['req'=32,'seq'=4] {'seq'}, dimensions={1}, use_global_device_ids=true | all-gather | bytes 20480 | tf_op jit(solution)/shard_map/all_gather | solution.py:183
  136.4 6.9 %fusion.300 = (bf16[4,1,1024,1024]{3,2,1,0:T(8,128)(2,1)S(1)}, bf16[4,1,1024,1024]{3,2,1,0:T(8,128)(2,1)S(1)}) fusion(bf16[4,2,1024,1024]{3,2,1,0:T(8,128)(2,1)} %bitcast.491), kind=kLoop, calls=%fused_computation.434 | loop fusion | bytes 33554432 | tf_op jit(solution)/shard_map/slice | solution.py:203
  143.3 1.2 fusion.310
  144.5 2.0 copy-done.3
  146.5 2.5 %copy-done.2 = bf16[4,1,1024,1024]{3,2,1,0:T(8,128)(2,1)} copy-done((bf16[4,1,1024,1024]{3,2,1,0:T(8,128)(2,1)}, bf16[4,1,1024,1024]{3,2,1,0:T(8,128)(2,1)S(1)}, u32[]{:S(2)}) %copy-start.2) | copy-done | bytes 8388632
  149.0 1.2 fusion.72
  150.6 9.1 %all_gather.26 = bf16[2,4096]{1,0:T(2,128)(2,1)S(1)} all-gather(bf16[2,1024]{1,0:T(2,128)(2,1)S(1)} %fusion.70), channel_id=1, replica_groups=mesh['req'=32,'seq'=4] {'seq'}, dimensions={1}, use_global_device_ids=true | all-gather | bytes 20480 | tf_op jit(solution)/shard_map/all_gather | solution.py:194
  159.7 35.4 %all-gather = bf16[32,2,4096]{2,1,0:T(2,128)(2,1)S(1)} all-gather(bf16[1,2,4096]{2,1,0:T(2,128)(2,1)S(1)} %bitcast.533), channel_id=1, replica_groups=mesh['req'=32,'seq'=4] {'req'}, dimensions={0}, use_global_device_ids=true | all-gather | bytes 540672 | tf_op jit(solution)/shard_map/all_gather | solution.py:195
  195.5 2.7 %fusion.85 = f32[64,256]{1,0:T(8,128)} fusion(bf16[4096,256]{1,0:T(8,128)(2,1)} %param.24, f32[64,4096]{1,0:T(8,128)S(1)} %reshape.871, f32[4096]{0:T(1024)S(1)} %copy-done.12, f32[64]{0:T(128)S(1)} %add_rsqrt_fusion.2), kind=kOutput, calls=%fused_computation.145 | convolution fusion | flops 135004160 | bytes 3227904 | tf_op jit(solution)/shard_map/dot_general | solution.py:199
  198.2 10.5 %fusion.309 = f32[512,1024]{1,0:T(8,128)} fusion(bf16[512,4096]{0,1:T(8,128)(2,1)} %all-gather.5.cloned.1.call-done, bf16[4096,1024]{1,0:T(8,128)(2,1)} %bitcast.490), kind=kOutput, calls=%fused_computation.443 | convolution fusion | flops 4294967296 | bytes 14680064 | tf_op jit(solution)/shard_map/dot_general | solution.py:203
  208.7 10.8 %add_convert_fusion = bf16[512,1024]{1,0:T(8,128)(2,1)} fusion(bf16[512,1024]{1,0:T(8,128)(2,1)S(1)} %copy-done.11, f32[512,1024]{1,0:T(8,128)} %fusion.309, bf16[512,4096]{0,1:T(8,128)(2,1)} %all-gather.9.cloned.1.call-done, bf16[4096,1024]{1,0:T(8,128)(2,1)} %bitcast.488), kind=kOutput, calls=%fused_computation.14 | convolution fusion | flops 4298113024 | bytes 16777216 | tf_op jit(solution)/shard_map/dot_general | solution.py:203
  (143 shorter events, 13.5 us)
Async XLA Ops:
  7.2 1.6 copy-start
  7.2 129.2 %all-gather.7.cloned.1.call-start = ((), (), s32[]{:S(2)}) async-start(), calls=%async_computation.3 | async-start | bytes 17301504 | tf_op jit(solution)/shard_map/all_gather | solution.py:120
  9.6 2.5 %copy-start.10 = (bf16[128,8192]{1,0:T(8,128)(2,1)S(1)}, bf16[128,8192]{1,0:T(8,128)(2,1)}, u32[]{:S(2)}) copy-start(bf16[128,8192]{1,0:T(8,128)(2,1)} %param.13) | copy-start | bytes 6291460
  24.1 1.4 copy-start.9
  25.5 5.2 %copy-start.16 = (s32[1,2]{1,0:T(1,128)S(1)}, s32[1,2]{1,0:T(1,128)}, u32[]{:S(2)}) copy-start(s32[1,2]{1,0:T(1,128)} %param.25) | copy-start | bytes 28
  25.5 9.3 %copy-start.13 = (f32[128]{0:T(128)S(1)}, f32[128]{0:T(128)}, u32[]{:S(2)}) copy-start(f32[128]{0:T(128)} %param.17) | copy-start | bytes 1540
  25.5 9.4 %copy-start.14 = (f32[128]{0:T(128)S(1)}, f32[128]{0:T(128)}, u32[]{:S(2)}) copy-start(f32[128]{0:T(128)} %param.18) | copy-start | bytes 1540
  25.5 9.4 %copy-start.15 = (f32[128]{0:T(128)S(1)}, f32[128]{0:T(128)}, u32[]{:S(2)}) copy-start(f32[128]{0:T(128)} %param.19) | copy-start | bytes 1540
  25.5 34.2 %all-to-all-start = ((bf16[4,128,2320]{1,2,0:T(8,128)(2,1)}), bf16[4,128,2320]{1,2,0:T(8,128)(2,1)}, u32[]{:S(2)}, u32[]{:S(2)}) async-start(bf16[4,128,2320]{1,2,0:T(8,128)(2,1)} %copy-done.9), calls=%async_computation | async-start | bytes 4751360 | tf_op jit(solution)/shard_map/all_to_all | solution.py:142
  59.7 32.6 %all-to-all-start.1 = ((bf16[4,128,2320]{1,2,0:T(8,128)(2,1)}), bf16[4,128,2320]{1,2,0:T(8,128)(2,1)}, u32[]{:S(2)}, u32[]{:S(2)}) async-start(bf16[4,128,2320]{1,2,0:T(8,128)(2,1)} %get-tuple-element.243), calls=%async_computation.1 | async-start | bytes 4751360 | tf_op jit(solution)/shard_map/all_to_all | solution.py:142
  64.3 133.9 %all-gather.5.cloned.1.call-start = ((), (), s32[]{:S(2)}) async-start(), calls=%async_computation.2 | async-start | bytes 5242880 | tf_op jit(solution)/shard_map/all_gather | solution.py:181
  66.5 1.4 copy-start.6
  70.1 2.3 %copy-start.7 = (bf16[512,2320]{0,1:T(8,128)(2,1)S(1)}, bf16[512,2320]{0,1:T(8,128)(2,1)}, u32[]{:S(2)}) copy-start(bf16[512,2320]{0,1:T(8,128)(2,1)} %copy-done.6) | copy-start | bytes 7127044
  94.1 1.5 copy-start.4
  101.8 107.0 %all-gather.9.cloned.1.call-start = ((), (), s32[]{:S(2)}) async-start(), calls=%async_computation.4 | async-start | bytes 5242880 | tf_op jit(solution)/shard_map/all_gather | solution.py:181
  102.9 2.1 copy-start.5
  112.4 1.5 copy-start.8
  143.3 3.2 %copy-start.3 = (bf16[4,1,1024,1024]{3,2,1,0:T(8,128)(2,1)}, bf16[4,1,1024,1024]{3,2,1,0:T(8,128)(2,1)S(1)}, u32[]{:S(2)}) copy-start(bf16[4,1,1024,1024]{3,2,1,0:T(8,128)(2,1)S(1)} %get-tuple-element.154) | copy-start | bytes 25165828
  143.3 5.7 %copy-start.2 = (bf16[4,1,1024,1024]{3,2,1,0:T(8,128)(2,1)}, bf16[4,1,1024,1024]{3,2,1,0:T(8,128)(2,1)S(1)}, u32[]{:S(2)}) copy-start(bf16[4,1,1024,1024]{3,2,1,0:T(8,128)(2,1)S(1)} %get-tuple-element.146) | copy-start | bytes 25165828
  149.0 1.2 copy-start.11
  150.3 45.2 %copy-start.12 = (f32[4096]{0:T(1024)S(1)}, f32[4096]{0:T(1024)}, u32[]{:S(2)}) copy-start(f32[4096]{0:T(1024)} %param.23) | copy-start | bytes 49156
  208.7 10.8 %copy-start.1 = (bf16[256,4096]{1,0:T(8,128)(2,1)S(1)}, bf16[256,4096]{1,0:T(8,128)(2,1)}, u32[]{:S(2)}) copy-start(bf16[256,4096]{1,0:T(8,128)(2,1)} %param.22) | copy-start | bytes 6291460
Sparse Core Ops, SparseCore 0:
  10.2 76.2 all-gather.6
  101.9 50.4 all-gather.4
  154.0 48.4 all-gather.8

commit v7 on v6

--- a/solution.py
+++ b/solution.py
@@ -146,7 +146,7 @@
     for half in range(groups):
         moved = moves[half]
         if half > 0:
-            moved = lax.optimization_barrier((moved, gated))[0]
+            moved = lax.optimization_barrier((moved, gated, picked_parts[-1]))[0]
         moved = moved.reshape(group_rows, -1)
         xg = moved[:, :block_cols]
         zg = moved[:, block_cols : 2 * block_cols]
@@ -180,14 +180,13 @@
         gated = gate_norm(y, zg, gain, 1)
         gated_parts.append(lax.all_gather(gated, "seq", axis=1, tiled=True))
         picked = jnp.dot(picker, gated, preferred_element_type=jnp.float32).astype(jnp.bfloat16)
-        picked_parts.append(lax.all_gather(picked, "seq", axis=1, tiled=True))
+        picked = lax.all_gather(picked, "seq", axis=1, tiled=True)
+        picked_parts.append(
+            jnp.dot(picked, w_blocks[:, half].reshape(-1, width), preferred_element_type=jnp.float32)
+        )
 
     picked_resid = jnp.dot(picker, resid, preferred_element_type=jnp.float32)
-    picked_mixer = sum(
-        jnp.dot(picked_parts[half], w_blocks[:, half].reshape(-1, width),
-                preferred_element_type=jnp.float32)
-        for half in range(groups)
-    )
+    picked_mixer = sum(picked_parts)
     picked_rows = (
         picked_resid + picked_mixer.astype(jnp.bfloat16).astype(jnp.float32)
     ).astype(jnp.bfloat16)

time: 227 us -> 224 us (0.987)
  waiting for transfers between devices: 31.4 us -> 22.2 us
  matrix products: 47.4 us -> 52.1 us
    all_to_all x2, waiting for transfers between devices: 31.4 us -> 22.2 us  [mixer_layer(): lax.all_to_all(packed, 'seq', split_axis=0, concat_axis=0, tiled=True)]
    dot_general x2, matrix products: 2.38 us -> 5.85 us  [mixer_layer(): jnp.dot(picked, w_blocks[:, half].reshape(-1, width), preferred_element_t...]
    slice x1, local copies, waits for them, and re-layouts: 6.93 us -> 10 us  [mixer_layer(): w_blocks[:, half].reshape(-1, width)]
    unnamed x43 -> x39, local copies, waits for them, and re-layouts: 23.7 us -> 22.1 us
  transfers between devices with their start and end apart: 5 -> 5, of which waited for: 2 -> 1; matrix products, arithmetic and copies ran while one was open for 35% -> 39% of each run, Pallas kernels for 0% -> 0%
where the time goes in v7:
time: 224 us; the launch traced here: 223 us
  blocking collectives  65.7 us (29%)
  matrix products  52.1 us (23%)
  local copies, waits for them, and re-layouts  43.4 us (19%)
  waiting for transfers between devices  22.2 us (10%)
  between operations  17.4 us (8%)
  other arithmetic  12.5 us (6%)
  starting transfers between devices  9.82 us (4%)
    all_gather x1, blocking collectives, mixer_layer(): collected = lax.all_gather(row_pair, 'req', axis=0, tiled=True)  34.2 us
    all_to_all x2, waiting for transfers between devices, mixer_layer(): lax.all_to_all(packed, 'seq', split_axis=0, concat_axis=0, tiled=True)  22.2 us
    unnamed x39, local copies, waits for them, and re-layouts  22.1 us
    all_gather x2, blocking collectives, mixer_layer(): picked = lax.all_gather(picked, 'seq', axis=1, tiled=True)  21.4 us
    dot_general x2, matrix products, mixer_layer(): jnp.dot(gated_parts[half], w_blocks[:, half].reshape(-1, width), preferre...  21.3 us
    slice x1, local copies, waits for them, and re-layouts, mixer_layer(): w_blocks[:, half].reshape(-1, width)  10 us
    all_gather x1, blocking collectives, mixer_layer(): row_pair = lax.all_gather(picked_rows, 'seq', axis=1, tiled=True)  9.98 us
    all_to_all x2, starting transfers between devices, mixer_layer(): lax.all_to_all(packed, 'seq', split_axis=0, concat_axis=0, tiled=True)  9.7 us
  transfers between devices with their start and end apart: 5, of which 1 were waited for; matrix products, arithmetic and copies ran while one was open for 39% of the time, Pallas kernels for 0%

profile of v7, /device:TPU:1, one launch (start us, length us, event | category | flops | bytes accessed | tf_op | source)
XLA Modules:
  0.0 223.1 jit_solution(3029703536686864329)
XLA Ops:
  7.2 1.5 copy-done
  8.8 0.8 constant_dynamic-slice_fusion
  9.6 1.0 copy.424
  10.7 1.1 fusion.303
  12.1 2.4 %copy.417 = bf16[128,8192]{0,1:T(8,128)(2,1)} copy(bf16[128,8192]{1,0:T(8,128)(2,1)S(1)} %copy-done.8) | data formatting | bytes 4194304 | tf_op args[0]
  14.5 3.2 %copy.418 = bf16[128,8192]{0,1:T(8,128)(2,1)S(1)} copy(bf16[128,8192]{1,0:T(8,128)(2,1)} %param.15) | data formatting | bytes 4194304 | tf_op args[2]
  17.8 2.9 %fusion.74 = (bf16[4,128,2320]{1,2,0:T(8,128)(2,1)}, bf16[4,128,2320]{1,2,0:T(8,128)(2,1)S(1)}) fusion(bf16[128,4,2,1024]{0,3,2,1:T(8,128)(2,1)} %bitcast.493), kind=kLoop, calls=%fused_computation.114 | loop fusion | bytes 4194304
  20.6 1.3 fusion.73
  22.0 0.7 fusion.167
  22.7 0.7 fusion.166
  23.4 0.6 constant_dynamic-update-slice_fusion.1
  24.0 1.4 copy-done.7
  25.4 5.1 %all-to-all-start = ((bf16[4,128,2320]{1,2,0:T(8,128)(2,1)}), bf16[4,128,2320]{1,2,0:T(8,128)(2,1)}, u32[]{:S(2)}, u32[]{:S(2)}) async-start(bf16[4,128,2320]{1,2,0:T(8,128)(2,1)} %copy-done.7), calls=%async_computation | async-start | bytes 4751360 | tf_op jit(solution)/shard_map/all_to_all | solution.py:142
  30.8 0.6 fusion.306
  34.7 0.7 fusion.304
  35.4 1.8 slice_convert_fusion
  37.5 22.2 %all-to-all-done = bf16[4,128,2320]{1,2,0:T(8,128)(2,1)} async-done(((bf16[4,128,2320]{1,2,0:T(8,128)(2,1)}), bf16[4,128,2320]{1,2,0:T(8,128)(2,1)}, u32[]{:S(2)}, u32[]{:S(2)}) %all-to-all-start) | async-done | bytes 2375712 | tf_op jit(solution)/shard_map/all_to_all | solution.py:142
  59.6 4.6 %all-to-all-start.1 = ((bf16[4,128,2320]{1,2,0:T(8,128)(2,1)}), bf16[4,128,2320]{1,2,0:T(8,128)(2,1)}, u32[]{:S(2)}, u32[]{:S(2)}) async-start(bf16[4,128,2320]{1,2,0:T(8,128)(2,1)} %get-tuple-element.243), calls=%async_computation.1 | async-start | bytes 4751360 | tf_op jit(solution)/shard_map/all_to_all | solution.py:142
  64.3 2.1 copy_bitcast_fusion.1
  66.4 1.4 copy-done.5
  70.1 1.8 subtract_convert_fusion.27
  71.8 0.4 copy-done.6
  72.6 0.5 fusion.143
  73.1 0.6 fusion.51
  75.0 0.5 fusion.149
  75.5 0.6 fusion.146
  76.1 0.6 fusion.152
  76.7 0.2 fusion.18
  78.9 0.6 fusion.53
  79.5 0.6 fusion.57
  80.1 0.6 fusion.55
  80.8 0.7 multiply_reduce_fusion.1
  81.4 1.2 multiply_convert_fusion.1
  82.8 1.6 convolution_convert_fusion.1
  84.3 12.3 %all_gather.23 = bf16[2,4096]{1,0:T(2,128)(2,1)S(1)} all-gather(bf16[2,1024]{1,0:T(2,128)(2,1)S(1)} %convolution_convert_fusion.1), channel_id=1, replica_groups=mesh['req'=32,'seq'=4] {'seq'}, dimensions={1}, use_global_device_ids=true | all-gather | bytes 20480 | tf_op jit(solution)/shard_map/all_gather | solution.py:183
  96.7 10.0 %fusion.300 = (bf16[4,1,1024,1024]{3,2,1,0:T(8,128)(2,1)}, bf16[4,1,1024,1024]{3,2,1,0:T(8,128)(2,1)S(1)}) fusion(bf16[4,2,1024,1024]{3,2,1,0:T(8,128)(2,1)} %bitcast.491), kind=kLoop, calls=%fused_computation.434 | loop fusion | bytes 33554432 | tf_op jit(solution)/shard_map/slice | solution.py:202
  106.7 3.2 %copy-done.2 = bf16[4,1,1024,1024]{3,2,1,0:T(8,128)(2,1)} copy-done((bf16[4,1,1024,1024]{3,2,1,0:T(8,128)(2,1)}, bf16[4,1,1024,1024]{3,2,1,0:T(8,128)(2,1)S(1)}, u32[]{:S(2)}) %copy-start.2) | copy-done | bytes 8388632
  109.9 1.2 fusion.310
  111.1 1.9 copy_bitcast_fusion
  113.0 1.5 copy-done.3
  115.1 1.0 fusion.194
  116.1 1.0 fusion.241
  117.0 1.0 fusion.231
  119.3 1.3 fusion.301
  121.0 0.5 fusion.155
  121.6 1.5 subtract_convert_fusion.21
  123.1 0.6 fusion.39
  124.6 0.5 fusion.161
  125.1 0.6 fusion.158
  125.7 0.6 fusion.164
  128.5 0.6 fusion.59
  129.1 0.6 fusion.63
  129.7 0.6 fusion.61
  130.4 0.7 multiply_reduce_fusion
  131.0 1.2 multiply_convert_fusion
  132.3 1.6 convolution_convert_fusion
  133.9 9.1 %all_gather.25 = bf16[2,4096]{1,0:T(2,128)(2,1)S(1)} all-gather(bf16[2,1024]{1,0:T(2,128)(2,1)S(1)} %convolution_convert_fusion), channel_id=1, replica_groups=mesh['req'=32,'seq'=4] {'seq'}, dimensions={1}, use_global_device_ids=true | all-gather | bytes 20480 | tf_op jit(solution)/shard_map/all_gather | solution.py:183
  143.1 4.7 %fusion.72 = f32[2,1024]{1,0:T(2,128)S(1)} fusion(f32[2,1024]{1,0:T(2,128)S(1)} %fusion.310, bf16[2,4096]{1,0:T(2,128)(2,1)S(1)} %all_gather.25, bf16[4096,1024]{1,0:T(8,128)(2,1)} %bitcast.487), kind=kOutput, calls=%fused_computation.108 | convolution fusion | flops 16783360 | bytes 8421376 | tf_op jit(solution)/shard_map/dot_general | solution.py:185
  147.7 0.3 fusion.70
  148.0 10.0 %all_gather.26 = bf16[2,4096]{1,0:T(2,128)(2,1)S(1)} all-gather(bf16[2,1024]{1,0:T(2,128)(2,1)S(1)} %fusion.70), channel_id=1, replica_groups=mesh['req'=32,'seq'=4] {'seq'}, dimensions={1}, use_global_device_ids=true | all-gather | bytes 20480 | tf_op jit(solution)/shard_map/all_gather | solution.py:193
  158.0 34.2 %all-gather = bf16[32,2,4096]{2,1,0:T(2,128)(2,1)S(1)} all-gather(bf16[1,2,4096]{2,1,0:T(2,128)(2,1)S(1)} %bitcast.533), channel_id=1, replica_groups=mesh['req'=32,'seq'=4] {'req'}, dimensions={0}, use_global_device_ids=true | all-gather | bytes 540672 | tf_op jit(solution)/shard_map/all_gather | solution.py:194
  192.6 2.7 %fusion.85 = f32[64,256]{1,0:T(8,128)} fusion(bf16[4096,256]{1,0:T(8,128)(2,1)} %param.24, f32[64,4096]{1,0:T(8,128)S(1)} %reshape.871, f32[4096]{0:T(1024)S(1)} %copy-done.10, f32[64]{0:T(128)S(1)} %add_rsqrt_fusion.2), kind=kOutput, calls=%fused_computation.145 | convolution fusion | flops 135004160 | bytes 3227904 | tf_op jit(solution)/shard_map/dot_general | solution.py:198
  195.3 10.5 %fusion.309 = f32[512,1024]{1,0:T(8,128)} fusion(bf16[512,4096]{0,1:T(8,128)(2,1)} %all-gather.5.cloned.1.call-done, bf16[4096,1024]{1,0:T(8,128)(2,1)} %bitcast.490), kind=kOutput, calls=%fused_computation.443 | convolution fusion | flops 4294967296 | bytes 14680064 | tf_op jit(solution)/shard_map/dot_general | solution.py:202
  205.8 10.8 %add_convert_fusion = bf16[512,1024]{1,0:T(8,128)(2,1)} fusion(bf16[512,1024]{1,0:T(8,128)(2,1)S(1)} %copy-done.9, f32[512,1024]{1,0:T(8,128)} %fusion.309, bf16[512,4096]{0,1:T(8,128)(2,1)} %all-gather.9.cloned.1.call-done, bf16[4096,1024]{1,0:T(8,128)(2,1)} %bitcast.488), kind=kOutput, calls=%fused_computation.14 | convolution fusion | flops 4298113024 | bytes 16777216 | tf_op jit(solution)/shard_map/dot_general | solution.py:202
  (139 shorter events, 12.7 us)
Async XLA Ops:
  7.2 1.6 copy-start
  7.2 89.5 %all-gather.7.cloned.1.call-start = ((), (), s32[]{:S(2)}) async-start(), calls=%async_computation.3 | async-start | bytes 17301504 | tf_op jit(solution)/shard_map/all_gather | solution.py:120
  9.6 2.5 %copy-start.8 = (bf16[128,8192]{1,0:T(8,128)(2,1)S(1)}, bf16[128,8192]{1,0:T(8,128)(2,1)}, u32[]{:S(2)}) copy-start(bf16[128,8192]{1,0:T(8,128)(2,1)} %param.13) | copy-start | bytes 6291460
  24.0 1.4 copy-start.7
  25.4 5.2 %copy-start.14 = (s32[1,2]{1,0:T(1,128)S(1)}, s32[1,2]{1,0:T(1,128)}, u32[]{:S(2)}) copy-start(s32[1,2]{1,0:T(1,128)} %param.25) | copy-start | bytes 28
  25.4 9.1 %copy-start.11 = (f32[128]{0:T(128)S(1)}, f32[128]{0:T(128)}, u32[]{:S(2)}) copy-start(f32[128]{0:T(128)} %param.17) | copy-start | bytes 1540
  25.4 9.2 %copy-start.12 = (f32[128]{0:T(128)S(1)}, f32[128]{0:T(128)}, u32[]{:S(2)}) copy-start(f32[128]{0:T(128)} %param.18) | copy-start | bytes 1540
  25.4 9.2 %copy-start.13 = (f32[128]{0:T(128)S(1)}, f32[128]{0:T(128)}, u32[]{:S(2)}) copy-start(f32[128]{0:T(128)} %param.19) | copy-start | bytes 1540
  25.4 34.2 %all-to-all-start = ((bf16[4,128,2320]{1,2,0:T(8,128)(2,1)}), bf16[4,128,2320]{1,2,0:T(8,128)(2,1)}, u32[]{:S(2)}, u32[]{:S(2)}) async-start(bf16[4,128,2320]{1,2,0:T(8,128)(2,1)} %copy-done.7), calls=%async_computation | async-start | bytes 4751360 | tf_op jit(solution)/shard_map/all_to_all | solution.py:142
  59.6 51.5 %all-to-all-start.1 = ((bf16[4,128,2320]{1,2,0:T(8,128)(2,1)}), bf16[4,128,2320]{1,2,0:T(8,128)(2,1)}, u32[]{:S(2)}, u32[]{:S(2)}) async-start(bf16[4,128,2320]{1,2,0:T(8,128)(2,1)} %get-tuple-element.243), calls=%async_computation.1 | async-start | bytes 4751360 | tf_op jit(solution)/shard_map/all_to_all | solution.py:142
  64.2 131.1 %all-gather.5.cloned.1.call-start = ((), (), s32[]{:S(2)}) async-start(), calls=%async_computation.2 | async-start | bytes 5242880 | tf_op jit(solution)/shard_map/all_gather | solution.py:181
  66.4 1.4 copy-start.5
  70.0 2.3 %copy-start.6 = (bf16[512,2320]{0,1:T(8,128)(2,1)S(1)}, bf16[512,2320]{0,1:T(8,128)(2,1)}, u32[]{:S(2)}) copy-start(bf16[512,2320]{0,1:T(8,128)(2,1)} %copy-done.5) | copy-start | bytes 7127044
  82.7 123.1 %all-gather.9.cloned.1.call-start = ((), (), s32[]{:S(2)}) async-start(), calls=%async_computation.4 | async-start | bytes 5242880 | tf_op jit(solution)/shard_map/all_gather | solution.py:181
  106.7 3.2 %copy-start.2 = (bf16[4,1,1024,1024]{3,2,1,0:T(8,128)(2,1)}, bf16[4,1,1024,1024]{3,2,1,0:T(8,128)(2,1)S(1)}, u32[]{:S(2)}) copy-start(bf16[4,1,1024,1024]{3,2,1,0:T(8,128)(2,1)S(1)} %get-tuple-element.154) | copy-start | bytes 25165828
  113.0 1.5 copy-start.3
  121.6 2.2 copy-start.4
  143.0 4.7 %copy-start.9 = (bf16[512,1024]{1,0:T(8,128)(2,1)S(1)}, bf16[512,1024]{1,0:T(8,128)(2,1)}, u32[]{:S(2)}) copy-start(bf16[512,1024]{1,0:T(8,128)(2,1)} %param.21) | copy-start | bytes 3145732
  147.7 44.9 %copy-start.10 = (f32[4096]{0:T(1024)S(1)}, f32[4096]{0:T(1024)}, u32[]{:S(2)}) copy-start(f32[4096]{0:T(1024)} %param.23) | copy-start | bytes 49156
  205.8 10.8 %copy-start.1 = (bf16[256,4096]{1,0:T(8,128)(2,1)S(1)}, bf16[256,4096]{1,0:T(8,128)(2,1)}, u32[]{:S(2)}) copy-start(bf16[256,4096]{1,0:T(8,128)(2,1)} %param.22) | copy-start | bytes 6291460
Sparse Core Ops, SparseCore 0:
  10.2 76.3 all-gather.6
  88.9 47.0 all-gather.4
  137.6 48.6 all-gather.8

commit v8 on v7

--- a/solution.py
+++ b/solution.py
@@ -146,7 +146,7 @@
     for half in range(groups):
         moved = moves[half]
         if half > 0:
-            moved = lax.optimization_barrier((moved, gated, picked_parts[-1]))[0]
+            moved = lax.optimization_barrier((moved, gated))[0]
         moved = moved.reshape(group_rows, -1)
         xg = moved[:, :block_cols]
         zg = moved[:, block_cols : 2 * block_cols]
@@ -179,14 +179,13 @@
         gain = lax.dynamic_slice_in_dim(norm_gain, (place * groups + half) * block_cols, block_cols)
         gated = gate_norm(y, zg, gain, 1)
         gated_parts.append(lax.all_gather(gated, "seq", axis=1, tiled=True))
-        picked = jnp.dot(picker, gated, preferred_element_type=jnp.float32).astype(jnp.bfloat16)
-        picked = lax.all_gather(picked, "seq", axis=1, tiled=True)
         picked_parts.append(
-            jnp.dot(picked, w_blocks[:, half].reshape(-1, width), preferred_element_type=jnp.float32)
+            jnp.dot(picker, gated, preferred_element_type=jnp.float32).astype(jnp.bfloat16)
         )
 
     picked_resid = jnp.dot(picker, resid, preferred_element_type=jnp.float32)
-    picked_mixer = sum(picked_parts)
+    picked = lax.all_gather(jnp.stack(picked_parts, axis=1), "seq", axis=0)
+    picked_mixer = jnp.einsum("sthj,shjo->to", picked, w_blocks, preferred_element_type=jnp.float32)
     picked_rows = (
         picked_resid + picked_mixer.astype(jnp.bfloat16).astype(jnp.float32)
     ).astype(jnp.bfloat16)

time: 224 us -> 221 us (0.987)
  blocking collectives: 65.7 us -> 53.3 us
  waiting for transfers between devices: 22.2 us -> 31.8 us
    all_gather x2 -> x1, blocking collectives: 21.4 us -> 10.6 us  [mixer_layer(): picked = lax.all_gather(jnp.stack(picked_parts, axis=1), 'seq', axis=0)]
    all_to_all x2, waiting for transfers between devices: 22.2 us -> 31 us  [mixer_layer(): lax.all_to_all(packed, 'seq', split_axis=0, concat_axis=0, tiled=True)]
    unnamed x39, local copies, waits for them, and re-layouts: 22.1 us -> 19 us
    dot_general x2 -> x1, matrix products: 5.85 us -> 7.24 us  [mixer_layer(): jnp.einsum('sthj,shjo->to', picked, w_blocks, preferred_element_type=jnp....]
  transfers between devices with their start and end apart: 5 -> 5, of which waited for: 1 -> 3; matrix products, arithmetic and copies ran while one was open for 39% -> 41% of each run, Pallas kernels for 0% -> 0%
where the time goes in v8:
time: 221 us; the launch traced here: 220 us
  blocking collectives  53.3 us (24%)
  matrix products  52.5 us (24%)
  local copies, waits for them, and re-layouts  42.1 us (19%)
  waiting for transfers between devices  31.8 us (14%)
  between operations  17.7 us (8%)
  other arithmetic  12.6 us (6%)
  starting transfers between devices  9.97 us (5%)
    all_gather x1, blocking collectives, mixer_layer(): collected = lax.all_gather(row_pair, 'req', axis=0, tiled=True)  32.2 us
    all_to_all x2, waiting for transfers between devices, mixer_layer(): lax.all_to_all(packed, 'seq', split_axis=0, concat_axis=0, tiled=True)  31 us
    dot_general x2, matrix products, mixer_layer(): jnp.dot(gated_parts[half], w_blocks[:, half].reshape(-1, width), preferre...  21.4 us
    unnamed x39, local copies, waits for them, and re-layouts  19 us
    slice x1, local copies, waits for them, and re-layouts, mixer_layer(): w_blocks[:, half].reshape(-1, width)  11.7 us
    all_gather x1, blocking collectives, mixer_layer(): picked = lax.all_gather(jnp.stack(picked_parts, axis=1), 'seq', axis=0)  10.6 us
    all_gather x1, blocking collectives, mixer_layer(): row_pair = lax.all_gather(picked_rows, 'seq', axis=1, tiled=True)  10.5 us
    all_to_all x2, starting transfers between devices, mixer_layer(): lax.all_to_all(packed, 'seq', split_axis=0, concat_axis=0, tiled=True)  9.66 us
  transfers between devices with their start and end apart: 5, of which 3 were waited for; matrix products, arithmetic and copies ran while one was open for 41% of the time, Pallas kernels for 0%

profile of v8, /device:TPU:1, one launch (start us, length us, event | category | flops | bytes accessed | tf_op | source)
XLA Modules:
  0.0 219.9 jit_solution(12328697791922768446)
XLA Ops:
  7.2 1.5 copy-done
  8.8 0.8 constant_dynamic-slice_fusion
  9.6 1.0 copy.434
  10.6 1.1 fusion.315
  12.1 2.4 %copy.427 = bf16[128,8192]{0,1:T(8,128)(2,1)} copy(bf16[128,8192]{1,0:T(8,128)(2,1)S(1)} %copy-done.8) | data formatting | bytes 4194304 | tf_op args[0]
  14.5 3.2 %copy.428 = bf16[128,8192]{0,1:T(8,128)(2,1)S(1)} copy(bf16[128,8192]{1,0:T(8,128)(2,1)} %param.15) | data formatting | bytes 4194304 | tf_op args[2]
  17.7 2.9 %fusion.85 = (bf16[4,128,2320]{1,2,0:T(8,128)(2,1)}, bf16[4,128,2320]{1,2,0:T(8,128)(2,1)S(1)}) fusion(bf16[128,4,2,1024]{0,3,2,1:T(8,128)(2,1)} %bitcast.499), kind=kLoop, calls=%fused_computation.118 | loop fusion | bytes 4194304
  20.7 1.3 fusion.84
  22.0 0.7 fusion.178
  22.7 0.7 fusion.177
  23.4 0.6 constant_dynamic-update-slice_fusion.1
  24.0 1.4 copy-done.7
  25.5 5.1 %all-to-all-start = ((bf16[4,128,2320]{1,2,0:T(8,128)(2,1)}), bf16[4,128,2320]{1,2,0:T(8,128)(2,1)}, u32[]{:S(2)}, u32[]{:S(2)}) async-start(bf16[4,128,2320]{1,2,0:T(8,128)(2,1)} %copy-done.7), calls=%async_computation | async-start | bytes 4751360 | tf_op jit(solution)/shard_map/all_to_all | solution.py:142
  30.9 0.7 fusion.318
  35.0 0.7 fusion.316
  35.8 2.0 slice_convert_fusion
  38.0 21.7 %all-to-all-done = bf16[4,128,2320]{1,2,0:T(8,128)(2,1)} async-done(((bf16[4,128,2320]{1,2,0:T(8,128)(2,1)}), bf16[4,128,2320]{1,2,0:T(8,128)(2,1)}, u32[]{:S(2)}, u32[]{:S(2)}) %all-to-all-start) | async-done | bytes 2375712 | tf_op jit(solution)/shard_map/all_to_all | solution.py:142
  59.7 4.5 %all-to-all-start.1 = ((bf16[4,128,2320]{1,2,0:T(8,128)(2,1)}), bf16[4,128,2320]{1,2,0:T(8,128)(2,1)}, u32[]{:S(2)}, u32[]{:S(2)}) async-start(bf16[4,128,2320]{1,2,0:T(8,128)(2,1)} %get-tuple-element.243), calls=%async_computation.1 | async-start | bytes 4751360 | tf_op jit(solution)/shard_map/all_to_all | solution.py:142
  64.2 2.1 copy_bitcast_fusion.1
  66.3 1.4 copy-done.4
  70.1 1.8 subtract_convert_fusion.27
  71.8 0.3 copy-done.5
  72.6 0.5 fusion.154
  73.1 0.6 fusion.53
  75.0 0.5 fusion.160
  75.5 0.6 fusion.157
  76.5 0.2 fusion.21
  78.3 0.6 fusion.55
  78.9 0.5 fusion.163
  79.5 0.6 fusion.59
  80.1 0.6 fusion.57
  80.7 0.7 multiply_reduce_fusion.1
  81.4 1.2 multiply_convert_fusion.1
  82.7 9.3 %all-to-all-done.1 = bf16[4,128,2320]{1,2,0:T(8,128)(2,1)} async-done(((bf16[4,128,2320]{1,2,0:T(8,128)(2,1)}), bf16[4,128,2320]{1,2,0:T(8,128)(2,1)}, u32[]{:S(2)}, u32[]{:S(2)}) %all-to-all-start.1) | async-done | bytes 2375712 | tf_op jit(solution)/shard_map/all_to_all | solution.py:142
  92.0 1.8 copy_bitcast_fusion
  93.9 1.4 copy-done.2
  96.9 1.0 fusion.205
  97.9 1.0 fusion.253
  98.8 1.0 fusion.243
  100.1 1.3 fusion.313
  102.0 0.5 fusion.166
  102.6 1.5 subtract_convert_fusion.21
  104.1 0.6 fusion.41
  105.6 0.5 fusion.172
  106.2 0.6 fusion.169
  106.7 0.6 fusion.175
  107.7 0.2 fusion.24
  109.5 0.6 fusion.61
  110.1 0.6 fusion.65
  110.8 0.6 fusion.63
  111.4 0.7 multiply_reduce_fusion
  112.1 1.3 multiply_convert_fusion
  113.5 0.4 fusion.82
  113.9 1.7 fusion.83
  115.7 10.6 %all-gather = bf16[8,2,1024]{2,1,0:T(2,128)(2,1)S(1)} all-gather(bf16[2,2,1024]{2,1,0:T(2,128)(2,1)S(1)} %copy.506), channel_id=2, replica_groups=mesh['req'=32,'seq'=4] {'seq'}, dimensions={0}, use_global_device_ids=true | all-gather | bytes 40960 | tf_op jit(solution)/shard_map/all_gather | solution.py:187
  126.3 7.2 %fusion.79 = f32[2,1024]{1,0:T(2,128)S(1)} fusion(bf16[4,2,1024,1024]{3,2,1,0:T(8,128)(2,1)} %bitcast.496, bf16[4,2,2,1024]{3,2,1,0:T(2,128)(2,1)S(1)} %bitcast.540), kind=kOutput, calls=%fused_computation.110 | convolution fusion | flops 33558528 | bytes 16818176 | tf_op jit(solution)/shard_map/sthj,shjo->to/dot_general | solution.py:188
  133.5 0.3 fusion.75
  133.8 10.5 %all_gather.26 = bf16[2,4096]{1,0:T(2,128)(2,1)S(1)} all-gather(bf16[2,1024]{1,0:T(2,128)(2,1)S(1)} %fusion.75), channel_id=1, replica_groups=mesh['req'=32,'seq'=4] {'seq'}, dimensions={1}, use_global_device_ids=true | all-gather | bytes 20480 | tf_op jit(solution)/shard_map/all_gather | solution.py:192
  144.3 32.2 %all-gather.1 = bf16[32,2,4096]{2,1,0:T(2,128)(2,1)S(1)} all-gather(bf16[1,2,4096]{2,1,0:T(2,128)(2,1)S(1)} %bitcast.542), channel_id=1, replica_groups=mesh['req'=32,'seq'=4] {'req'}, dimensions={0}, use_global_device_ids=true | all-gather | bytes 540672 | tf_op jit(solution)/shard_map/all_gather | solution.py:193
  176.9 2.8 %fusion.96 = f32[64,256]{1,0:T(8,128)} fusion(bf16[4096,256]{1,0:T(8,128)(2,1)} %param.24, f32[64,4096]{1,0:T(8,128)S(1)} %reshape.872, f32[4096]{0:T(1024)S(1)} %copy-done.10, f32[64]{0:T(128)S(1)} %add_rsqrt_fusion.2), kind=kOutput, calls=%fused_computation.149 | convolution fusion | flops 135004160 | bytes 3227904 | tf_op jit(solution)/shard_map/dot_general | solution.py:197
  179.6 11.7 %fusion.312 = (bf16[4,1,1024,1024]{3,2,1,0:T(8,128)(2,1)}, bf16[4,1,1024,1024]{3,2,1,0:T(8,128)(2,1)}) fusion(bf16[4,2,1024,1024]{3,2,1,0:T(8,128)(2,1)} %bitcast.497), kind=kLoop, calls=%fused_computation.440 | loop fusion | bytes 33554432 | tf_op jit(solution)/shard_map/slice | solution.py:201
  191.3 10.6 %fusion.321 = f32[512,1024]{1,0:T(8,128)} fusion(bf16[512,4096]{0,1:T(8,128)(2,1)} %all-gather.6.cloned.1.call-done, bf16[4096,1024]{1,0:T(8,128)(2,1)} %bitcast.501), kind=kOutput, calls=%fused_computation.449 | convolution fusion | flops 4294967296 | bytes 14680064 | tf_op jit(solution)/shard_map/dot_general | solution.py:201
  201.9 0.7 all-gather.10.cloned.1.call-done
  202.6 10.8 %add_convert_fusion = bf16[512,1024]{1,0:T(8,128)(2,1)} fusion(bf16[512,1024]{1,0:T(8,128)(2,1)S(1)} %copy-done.9, f32[512,1024]{1,0:T(8,128)} %fusion.321, bf16[512,4096]{0,1:T(8,128)(2,1)} %all-gather.10.cloned.1.call-done, bf16[4096,1024]{1,0:T(8,128)(2,1)} %bitcast.500), kind=kOutput, calls=%fused_computation.16 | convolution fusion | flops 4298113024 | bytes 16777216 | tf_op jit(solution)/shard_map/dot_general | solution.py:201
  (139 shorter events, 12.8 us)
Async XLA Ops:
  7.2 1.6 copy-start
  7.2 119.1 %all-gather.8.cloned.1.call-start = ((), (), s32[]{:S(2)}) async-start(), calls=%async_computation.3 | async-start | bytes 17301504 | tf_op jit(solution)/shard_map/all_gather | solution.py:120
  9.6 2.5 %copy-start.8 = (bf16[128,8192]{1,0:T(8,128)(2,1)S(1)}, bf16[128,8192]{1,0:T(8,128)(2,1)}, u32[]{:S(2)}) copy-start(bf16[128,8192]{1,0:T(8,128)(2,1)} %param.13) | copy-start | bytes 6291460
  24.0 1.4 copy-start.7
  25.4 5.2 %copy-start.14 = (s32[1,2]{1,0:T(1,128)S(1)}, s32[1,2]{1,0:T(1,128)}, u32[]{:S(2)}) copy-start(s32[1,2]{1,0:T(1,128)} %param.25) | copy-start | bytes 28
  25.4 9.4 %copy-start.11 = (f32[128]{0:T(128)S(1)}, f32[128]{0:T(128)}, u32[]{:S(2)}) copy-start(f32[128]{0:T(128)} %param.17) | copy-start | bytes 1540
  25.4 9.5 %copy-start.12 = (f32[128]{0:T(128)S(1)}, f32[128]{0:T(128)}, u32[]{:S(2)}) copy-start(f32[128]{0:T(128)} %param.18) | copy-start | bytes 1540
  25.4 9.5 %copy-start.13 = (f32[128]{0:T(128)S(1)}, f32[128]{0:T(128)}, u32[]{:S(2)}) copy-start(f32[128]{0:T(128)} %param.19) | copy-start | bytes 1540
  25.5 34.2 %all-to-all-start = ((bf16[4,128,2320]{1,2,0:T(8,128)(2,1)}), bf16[4,128,2320]{1,2,0:T(8,128)(2,1)}, u32[]{:S(2)}, u32[]{:S(2)}) async-start(bf16[4,128,2320]{1,2,0:T(8,128)(2,1)} %copy-done.7), calls=%async_computation | async-start | bytes 4751360 | tf_op jit(solution)/shard_map/all_to_all | solution.py:142
  59.7 32.3 %all-to-all-start.1 = ((bf16[4,128,2320]{1,2,0:T(8,128)(2,1)}), bf16[4,128,2320]{1,2,0:T(8,128)(2,1)}, u32[]{:S(2)}, u32[]{:S(2)}) async-start(bf16[4,128,2320]{1,2,0:T(8,128)(2,1)} %get-tuple-element.243), calls=%async_computation.1 | async-start | bytes 4751360 | tf_op jit(solution)/shard_map/all_to_all | solution.py:142
  64.2 127.1 %all-gather.6.cloned.1.call-start = ((), (), s32[]{:S(2)}) async-start(), calls=%async_computation.2 | async-start | bytes 5242880 | tf_op jit(solution)/shard_map/all_gather | solution.py:181
  66.3 1.4 copy-start.4
  69.9 2.2 %copy-start.5 = (bf16[512,2320]{0,1:T(8,128)(2,1)S(1)}, bf16[512,2320]{0,1:T(8,128)(2,1)}, u32[]{:S(2)}) copy-start(bf16[512,2320]{0,1:T(8,128)(2,1)} %copy-done.4) | copy-start | bytes 7127044
  93.9 1.4 copy-start.2
  101.4 101.2 %all-gather.10.cloned.1.call-start = ((), (), s32[]{:S(2)}) async-start(), calls=%async_computation.4 | async-start | bytes 5242880 | tf_op jit(solution)/shard_map/all_gather | solution.py:181
  102.6 2.1 copy-start.3
  112.1 1.5 copy-start.6
  126.3 7.2 %copy-start.9 = (bf16[512,1024]{1,0:T(8,128)(2,1)S(1)}, bf16[512,1024]{1,0:T(8,128)(2,1)}, u32[]{:S(2)}) copy-start(bf16[512,1024]{1,0:T(8,128)(2,1)} %param.21) | copy-start | bytes 3145732
  133.5 43.3 %copy-start.10 = (f32[4096]{0:T(1024)S(1)}, f32[4096]{0:T(1024)}, u32[]{:S(2)}) copy-start(f32[4096]{0:T(1024)} %param.23) | copy-start | bytes 49156
  202.6 10.8 %copy-start.1 = (bf16[256,4096]{1,0:T(8,128)(2,1)S(1)}, bf16[256,4096]{1,0:T(8,128)(2,1)}, u32[]{:S(2)}) copy-start(bf16[256,4096]{1,0:T(8,128)(2,1)} %param.22) | copy-start | bytes 6291460
Sparse Core Ops, SparseCore 0:
  10.2 76.3 all-gather.7
  101.6 50.6 all-gather.5
  154.0 48.5 all-gather.9

commit v9 on v8

--- a/solution.py
+++ b/solution.py
@@ -82,6 +82,29 @@
     return normed.astype(jnp.bfloat16)
 
 
+def gather_by_shifts(value, axis):
+    count, mine = lax.axis_size(axis), lax.axis_index(axis)
+    parts = [value]
+    for shift in range(1, count):
+        pairs = [(i, (i + shift) % count) for i in range(count)]
+        parts.append(lax.ppermute(value, axis, perm=pairs))
+    order = (mine - jnp.arange(count, dtype=jnp.int32)) % count
+    return jnp.take(jnp.stack(parts), order, axis=0)
+
+
+def gather_by_doubling(value, axis):
+    count, mine = lax.axis_size(axis), lax.axis_index(axis)
+    acc = value[None]
+    step = 1
+    while step < count:
+        pairs = [(i, i ^ step) for i in range(count)]
+        other = lax.ppermute(acc, axis, perm=pairs)
+        low = (mine // step) % 2 == 0
+        acc = jnp.where(low, jnp.concatenate([acc, other]), jnp.concatenate([other, acc]))
+        step *= 2
+    return acc
+
+
 def mixer_layer(
     xs,
     bc,
@@ -184,14 +207,14 @@
         )
 
     picked_resid = jnp.dot(picker, resid, preferred_element_type=jnp.float32)
-    picked = lax.all_gather(jnp.stack(picked_parts, axis=1), "seq", axis=0)
+    picked = gather_by_shifts(jnp.stack(picked_parts, axis=1), "seq")
     picked_mixer = jnp.einsum("sthj,shjo->to", picked, w_blocks, preferred_element_type=jnp.float32)
     picked_rows = (
         picked_resid + picked_mixer.astype(jnp.bfloat16).astype(jnp.float32)
     ).astype(jnp.bfloat16)
-    row_pair = lax.all_gather(picked_rows, "seq", axis=1, tiled=True)
-    collected = lax.all_gather(row_pair, "req", axis=0, tiled=True)
-    last_rows = collected.astype(jnp.float32)
+    row_pair = gather_by_shifts(picked_rows, "seq").transpose(1, 0, 2).reshape(slots, -1)
+    collected = gather_by_doubling(row_pair, "req")
+    last_rows = collected.reshape(-1, seq_count * width).astype(jnp.float32)
     meansq = jnp.mean(last_rows * last_rows, axis=-1, keepdims=True)
     normed = (last_rows * lax.rsqrt(meansq + 1e-05) * final_gain[None, :]).astype(jnp.bfloat16)
     logits = jnp.dot(normed, head_weight, preferred_element_type=jnp.float32)

time: 221 us -> 228 us (1.032)
  blocking collectives: 53.3 us -> 0 us
  waiting for transfers between devices: 31.8 us -> 65.7 us
  starting transfers between devices: 9.97 us -> 31.8 us
  local copies, waits for them, and re-layouts: 42.1 us -> 45.3 us
    all_gather x3 -> x0, blocking collectives: 53.3 us -> none  [the longest x1 32.2 us: mixer_layer(): collected = lax.all_gather(row_pair, 'req', axis=0, tiled=True)]
    all_gather x2, waiting for transfers between devices: 0.7 us -> 27.1 us  [mixer_layer(): gated_parts.append(lax.all_gather(gated, 'seq', axis=1, tiled=True))]
    ppermute x0 -> x11, starting transfers between devices: none -> 21.9 us  [the longest x5 14.8 us: gather_by_doubling(): other = lax.ppermute(acc, axis, perm=pairs)]
    ppermute x0 -> x11, waiting for transfers between devices: none -> 7.28 us  [the longest x6 4.73 us: gather_by_shifts(): parts.append(lax.ppermute(value, axis, perm=pairs))]
    unnamed x39 -> x41, local copies, waits for them, and re-layouts: 19 us -> 19.5 us
  transfers between devices with their start and end apart: 5 -> 16, of which waited for: 3 -> 10; matrix products, arithmetic and copies ran while one was open for 41% -> 43% of each run, Pallas kernels for 0% -> 0%
where the time goes in v9:
time: 228 us; the launch traced here: 227 us
  waiting for transfers between devices  65.7 us (29%)
  matrix products  52.7 us (23%)
  local copies, waits for them, and re-layouts  45.3 us (20%)
  starting transfers between devices  31.8 us (14%)
  between operations  17.6 us (8%)
  other arithmetic  14.1 us (6%)
    all_to_all x2, waiting for transfers between devices, mixer_layer(): lax.all_to_all(packed, 'seq', split_axis=0, concat_axis=0, tiled=True)  31.3 us
    all_gather x2, waiting for transfers between devices, mixer_layer(): gated_parts.append(lax.all_gather(gated, 'seq', axis=1, tiled=True))  27.1 us
    dot_general x2, matrix products, mixer_layer(): jnp.dot(gated_parts[half], w_blocks[:, half].reshape(-1, width), preferre...  21.9 us
    unnamed x41, local copies, waits for them, and re-layouts  19.5 us
    ppermute x5, starting transfers between devices, gather_by_doubling(): other = lax.ppermute(acc, axis, perm=pairs)  14.8 us
    slice x1, local copies, waits for them, and re-layouts, mixer_layer(): w_blocks[:, half].reshape(-1, width)  11.6 us
    all_to_all x2, starting transfers between devices, mixer_layer(): lax.all_to_all(packed, 'seq', split_axis=0, concat_axis=0, tiled=True)  9.65 us
    dot_general x1, matrix products, mixer_layer(): jnp.einsum('sthj,shjo->to', picked, w_blocks, preferred_element_type=jnp....  7.19 us
  transfers between devices with their start and end apart: 16, of which 10 were waited for; matrix products, arithmetic and copies ran while one was open for 43% of the time, Pallas kernels for 0%

profile of v9, /device:TPU:1, one launch (start us, length us, event | category | flops | bytes accessed | tf_op | source)
XLA Modules:
  0.0 227.3 jit_solution(14455603413116575130)
XLA Ops:
  7.2 1.5 copy-done
  8.8 0.8 constant_dynamic-slice_fusion
  9.6 1.0 copy.525
  10.6 1.1 fusion.320
  12.1 2.4 %copy.518 = bf16[128,8192]{0,1:T(8,128)(2,1)} copy(bf16[128,8192]{1,0:T(8,128)(2,1)S(1)} %copy-done.9) | data formatting | bytes 4194304 | tf_op args[0]
  14.5 3.2 %copy.519 = bf16[128,8192]{0,1:T(8,128)(2,1)S(1)} copy(bf16[128,8192]{1,0:T(8,128)(2,1)} %param.15) | data formatting | bytes 4194304 | tf_op args[2]
  17.7 2.9 %fusion.85 = (bf16[4,128,2320]{1,2,0:T(8,128)(2,1)}, bf16[4,128,2320]{1,2,0:T(8,128)(2,1)S(1)}) fusion(bf16[128,4,2,1024]{0,3,2,1:T(8,128)(2,1)} %bitcast.511), kind=kLoop, calls=%fused_computation.120 | loop fusion | bytes 4194304
  20.6 1.4 fusion.84
  22.0 0.7 fusion.179
  22.7 0.7 fusion.178
  23.4 0.6 constant_dynamic-update-slice_fusion.1
  24.0 1.4 copy-done.8
  25.5 5.1 %all-to-all-start = ((bf16[4,128,2320]{1,2,0:T(8,128)(2,1)}), bf16[4,128,2320]{1,2,0:T(8,128)(2,1)}, u32[]{:S(2)}, u32[]{:S(2)}) async-start(bf16[4,128,2320]{1,2,0:T(8,128)(2,1)} %copy-done.8), calls=%async_computation | async-start | bytes 4751360 | tf_op jit(solution)/shard_map/all_to_all | solution.py:165
  30.9 0.6 fusion.323
  34.8 0.7 fusion.321
  35.6 1.9 slice_convert_fusion
  37.7 22.0 %all-to-all-done = bf16[4,128,2320]{1,2,0:T(8,128)(2,1)} async-done(((bf16[4,128,2320]{1,2,0:T(8,128)(2,1)}), bf16[4,128,2320]{1,2,0:T(8,128)(2,1)}, u32[]{:S(2)}, u32[]{:S(2)}) %all-to-all-start) | async-done | bytes 2375712 | tf_op jit(solution)/shard_map/all_to_all | solution.py:165
  59.6 4.5 %all-to-all-start.1 = ((bf16[4,128,2320]{1,2,0:T(8,128)(2,1)}), bf16[4,128,2320]{1,2,0:T(8,128)(2,1)}, u32[]{:S(2)}, u32[]{:S(2)}) async-start(bf16[4,128,2320]{1,2,0:T(8,128)(2,1)} %get-tuple-element.245), calls=%async_computation.1 | async-start | bytes 4751360 | tf_op jit(solution)/shard_map/all_to_all | solution.py:165
  64.2 2.1 copy_bitcast_fusion.1
  66.3 1.4 copy-done.4
  70.0 1.8 subtract_convert_fusion.27
  73.1 0.6 fusion.53
  78.3 0.6 fusion.55
  79.5 0.6 fusion.59
  80.1 0.6 fusion.57
  80.7 0.7 multiply_reduce_fusion.1
  81.4 1.2 multiply_convert_fusion.1
  82.6 9.3 %all-to-all-done.1 = bf16[4,128,2320]{1,2,0:T(8,128)(2,1)} async-done(((bf16[4,128,2320]{1,2,0:T(8,128)(2,1)}), bf16[4,128,2320]{1,2,0:T(8,128)(2,1)}, u32[]{:S(2)}, u32[]{:S(2)}) %all-to-all-start.1) | async-done | bytes 2375712 | tf_op jit(solution)/shard_map/all_to_all | solution.py:165
  91.9 1.8 copy_bitcast_fusion
  93.8 1.4 copy-done.2
  96.8 1.0 fusion.206
  97.8 1.0 fusion.254
  98.8 1.0 fusion.261
  99.7 1.0 fusion.244
  101.0 1.3 fusion.318
  103.9 1.5 subtract_convert_fusion.21
  110.7 0.6 fusion.61
  111.3 0.6 fusion.65
  111.9 0.6 fusion.63
  112.5 0.7 multiply_reduce_fusion
  113.9 0.6 copy-done.7
  115.0 1.1 collective-permute-start
  116.1 1.6 collective-permute-start.2
  117.7 1.0 collective-permute-done.1
  118.8 0.6 gather_fusion
  119.4 7.2 %fusion.79 = f32[2,1024]{1,0:T(2,128)S(1)} fusion(bf16[4,2,1024,1024]{3,2,1,0:T(8,128)(2,1)} %bitcast.508, bf16[4,2,2,1024]{3,1,2,0:T(2,128)(2,1)S(1)} %gather_fusion, pred[4]{0:T(512)(128)(4,1)S(1)} %compare_and_fusion), kind=kOutput, calls=%fused_computation.112 | convolution fusion | flops 33574912 | bytes 16818180 | tf_op jit(solution)/shard_map/sthj,shjo->to/dot_general | solution.py:211
  126.9 3.3 %collective-permute-start.5 = (bf16[2,1024]{1,0:T(2,128)(2,1)S(1)}, bf16[2,1024]{1,0:T(2,128)(2,1)S(1)}, u32[]{:S(2)}, u32[]{:S(2)}) collective-permute-start(bf16[2,1024]{1,0:T(2,128)(2,1)S(1)} %fusion.75), channel_id=1, source_target_pairs={{0,3},{1,0},{2,1},{3,2},{4,7},{5,4},{6,5},{7,6},{8,11},{9,8},{10,9... | collective-permute-start | bytes 12296 | tf_op jit(solution)/shard_map/ppermute | solution.py:90
  130.3 0.6 collective-permute-start.3
  131.1 3.3 %collective-permute-done.4 = bf16[2,1024]{1,0:T(2,128)(2,1)S(1)} collective-permute-done((bf16[2,1024]{1,0:T(2,128)(2,1)S(1)}, bf16[2,1024]{1,0:T(2,128)(2,1)S(1)}, u32[]{:S(2)}, u32[]{:S(2)}) %collective-permute-start.4) | collective-permute-done | bytes 4128 | tf_op jit(solution)/shard_map/ppermute | solution.py:90
  134.6 0.6 gather_fusion.1
  135.3 5.5 %collective-permute-start.6 = (bf16[1,2,4096]{2,1,0:T(2,128)(2,1)S(1)}, bf16[1,2,4096]{2,1,0:T(2,128)(2,1)S(1)}, u32[]{:S(2)}, u32[]{:S(2)}) collective-permute-start(bf16[1,2,4096]{2,1,0:T(2,128)(2,1)S(1)} %bitcast.553), channel_id=1, source_target_pairs={{0,4},{4,0},{8,12},{12,8},{16,20},{20,16},{24,28},{28,24},{32,36},... | collective-permute-start | bytes 49160 | tf_op jit(solution)/shard_map/ppermute | solution.py:101
  140.8 0.8 collective-permute-done.6
  141.7 1.9 collective-permute-start.7
  143.5 1.7 collective-permute-done.7
  145.4 3.5 %collective-permute-start.8 = (bf16[4,2,4096]{2,1,0:T(2,128)(2,1)S(1)}, bf16[4,2,4096]{2,1,0:T(2,128)(2,1)S(1)}, u32[]{:S(2)}, u32[]{:S(2)}) collective-permute-start(bf16[4,2,4096]{2,1,0:T(2,128)(2,1)S(1)} %broadcast_select_fusion.3), channel_id=1, source_target_pairs={{0,16},{4,20},{8,24},{12,28},{16,0},{20,4},{24,8},{28,12},{32,48},... | collective-permute-start | bytes 196616 | tf_op jit(solution)/shard_map/ppermute | solution.py:101
  148.9 11.6 %fusion.317 = (bf16[4,1,1024,1024]{3,2,1,0:T(8,128)(2,1)}, bf16[4,1,1024,1024]{3,2,1,0:T(8,128)(2,1)}) fusion(bf16[4,2,1024,1024]{3,2,1,0:T(8,128)(2,1)} %bitcast.509), kind=kLoop, calls=%fused_computation.465 | loop fusion | bytes 33554432 | tf_op jit(solution)/shard_map/slice | solution.py:224
  160.8 1.4 collective-permute-start.9
  162.3 11.2 %fusion.326 = f32[512,1024]{1,0:T(8,128)} fusion(bf16[512,4096]{0,1:T(8,128)(2,1)} %all-gather.4.cloned.1.call-done, bf16[4096,1024]{1,0:T(8,128)(2,1)} %bitcast.513), kind=kOutput, calls=%fused_computation.474 | convolution fusion | flops 4294967296 | bytes 14680064 | tf_op jit(solution)/shard_map/dot_general | solution.py:224
  174.1 2.5 %collective-permute-start.10 = (bf16[16,2,4096]{2,1,0:T(2,128)(2,1)S(1)}, bf16[16,2,4096]{2,1,0:T(2,128)(2,1)S(1)}, u32[]{:S(2)}, u32[]{:S(2)}) collective-permute-start(bf16[16,2,4096]{2,1,0:T(2,128)(2,1)S(1)} %broadcast_select_fusion.1), channel_id=1, source_target_pairs={{0,64},{4,68},{8,72},{12,76},{16,80},{20,84},{24,88},{28,92},{32,9... | collective-permute-start | bytes 786440 | tf_op jit(solution)/shard_map/ppermute | solution.py:101
  176.6 27.1 %all-gather.8.cloned.1.call-done = bf16[512,4096]{0,1:T(8,128)(2,1)} async-done(((bf16[512,1024]{0,1:T(8,128)(2,1)}), bf16[512,4096]{0,1:T(8,128)(2,1)}) %all-gather.8.cloned.1.call-update) | async-done | bytes 4194320 | tf_op jit(solution)/shard_map/all_gather | solution.py:204
  203.7 10.6 %add_convert_fusion = bf16[512,1024]{1,0:T(8,128)(2,1)} fusion(bf16[512,1024]{1,0:T(8,128)(2,1)S(1)} %copy-done.10, f32[512,1024]{1,0:T(8,128)} %fusion.326, bf16[512,4096]{0,1:T(8,128)(2,1)} %all-gather.8.cloned.1.call-done, bf16[4096,1024]{1,0:T(8,128)(2,1)} %bitcast.512), kind=kOutput, calls=%fused_computation.18 | convolution fusion | flops 4298113024 | bytes 16777216 | tf_op jit(solution)/shard_map/dot_general | solution.py:224
  214.3 1.5 multiply_reduce_fusion.2
  215.9 1.7 reshape.939
  217.7 3.1 %fusion.97 = f32[64,256]{1,0:T(8,128)} fusion(bf16[4096,256]{1,0:T(8,128)(2,1)} %param.24, f32[64,4096]{1,0:T(8,128)} %reshape.939, f32[4096]{0:T(1024)S(1)} %copy-done.11, f32[64]{0:T(128)S(1)} %rsqrt.30), kind=kOutput, calls=%fused_computation.153 | convolution fusion | flops 135004160 | bytes 3227904 | tf_op jit(solution)/shard_map/dot_general | solution.py:220
  (173 shorter events, 21.5 us)
Async XLA Ops:
  7.2 1.6 copy-start
  7.2 112.2 %all-gather.6.cloned.1.call-start = ((), (), s32[]{:S(2)}) async-start(), calls=%async_computation.3 | async-start | bytes 17301504 | tf_op jit(solution)/shard_map/all_gather | solution.py:143
  9.6 2.5 %copy-start.9 = (bf16[128,8192]{1,0:T(8,128)(2,1)S(1)}, bf16[128,8192]{1,0:T(8,128)(2,1)}, u32[]{:S(2)}) copy-start(bf16[128,8192]{1,0:T(8,128)(2,1)} %param.13) | copy-start | bytes 6291460
  24.0 1.4 copy-start.8
  25.5 5.2 %copy-start.15 = (s32[1,2]{1,0:T(1,128)S(1)}, s32[1,2]{1,0:T(1,128)}, u32[]{:S(2)}) copy-start(s32[1,2]{1,0:T(1,128)} %param.25) | copy-start | bytes 28
  25.5 9.1 %copy-start.12 = (f32[128]{0:T(128)S(1)}, f32[128]{0:T(128)}, u32[]{:S(2)}) copy-start(f32[128]{0:T(128)} %param.17) | copy-start | bytes 1540
  25.5 9.2 %copy-start.13 = (f32[128]{0:T(128)S(1)}, f32[128]{0:T(128)}, u32[]{:S(2)}) copy-start(f32[128]{0:T(128)} %param.18) | copy-start | bytes 1540
  25.5 9.2 %copy-start.14 = (f32[128]{0:T(128)S(1)}, f32[128]{0:T(128)}, u32[]{:S(2)}) copy-start(f32[128]{0:T(128)} %param.19) | copy-start | bytes 1540
  25.5 34.2 %all-to-all-start = ((bf16[4,128,2320]{1,2,0:T(8,128)(2,1)}), bf16[4,128,2320]{1,2,0:T(8,128)(2,1)}, u32[]{:S(2)}, u32[]{:S(2)}) async-start(bf16[4,128,2320]{1,2,0:T(8,128)(2,1)} %copy-done.8), calls=%async_computation | async-start | bytes 4751360 | tf_op jit(solution)/shard_map/all_to_all | solution.py:165
  59.6 32.3 %all-to-all-start.1 = ((bf16[4,128,2320]{1,2,0:T(8,128)(2,1)}), bf16[4,128,2320]{1,2,0:T(8,128)(2,1)}, u32[]{:S(2)}, u32[]{:S(2)}) async-start(bf16[4,128,2320]{1,2,0:T(8,128)(2,1)} %get-tuple-element.245), calls=%async_computation.1 | async-start | bytes 4751360 | tf_op jit(solution)/shard_map/all_to_all | solution.py:165
  64.2 98.1 %all-gather.4.cloned.1.call-start = ((), (), s32[]{:S(2)}) async-start(), calls=%async_computation.2 | async-start | bytes 5242880 | tf_op jit(solution)/shard_map/all_gather | solution.py:204
  66.3 1.4 copy-start.4
  69.9 2.2 copy-start.5
  93.8 1.4 copy-start.2
  96.1 6.5 %copy-start.6 = (bf16[512,1024]{0,1:T(8,128)(2,1)S(1)}, bf16[512,1024]{0,1:T(8,128)(2,1)}, u32[]{:S(2)}) copy-start(bf16[512,1024]{0,1:T(8,128)(2,1)} %multiply_convert_fusion.1) | copy-start | bytes 3145732
  102.4 101.3 %all-gather.8.cloned.1.call-start = ((), (), s32[]{:S(2)}) async-start(), calls=%async_computation.4 | async-start | bytes 5242880 | tf_op jit(solution)/shard_map/all_gather | solution.py:204
  103.9 2.1 copy-start.3
  113.5 1.0 copy-start.7
  114.5 4.1 %collective-permute-start.1 = (bf16[2,2,1024]{2,0,1:T(2,128)(2,1)S(1)}, bf16[2,2,1024]{2,0,1:T(2,128)(2,1)S(1)}, u32[]{:S(2)}, u32[]{:S(2)}) collective-permute-start(bf16[2,2,1024]{2,0,1:T(2,128)(2,1)S(1)} %pad_maximum_fusion.2), channel_id=1, source_target_pairs={{0,2},{1,3},{2,0},{3,1},{4,6},{5,7},{6,4},{7,5},{8,10},{9,11},{10,... | collective-permute-start | bytes 24584 | tf_op jit(solution)/shard_map/ppermute | solution.py:90
  115.0 3.7 %collective-permute-start = (bf16[2,2,1024]{2,0,1:T(2,128)(2,1)S(1)}, bf16[2,2,1024]{2,0,1:T(2,128)(2,1)S(1)}, u32[]{:S(2)}, u32[]{:S(2)}) collective-permute-start(bf16[2,2,1024]{2,0,1:T(2,128)(2,1)S(1)} %pad_maximum_fusion.2), channel_id=1, source_target_pairs={{0,1},{1,2},{2,3},{3,0},{4,5},{5,6},{6,7},{7,4},{8,9},{9,10},{10,1... | collective-permute-start | bytes 24584 | tf_op jit(solution)/shard_map/ppermute | solution.py:90
  116.1 2.6 %collective-permute-start.2 = (bf16[2,2,1024]{2,0,1:T(2,128)(2,1)S(1)}, bf16[2,2,1024]{2,0,1:T(2,128)(2,1)S(1)}, u32[]{:S(2)}, u32[]{:S(2)}) collective-permute-start(bf16[2,2,1024]{2,0,1:T(2,128)(2,1)S(1)} %pad_maximum_fusion.2), channel_id=1, source_target_pairs={{0,3},{1,0},{2,1},{3,2},{4,7},{5,4},{6,5},{7,6},{8,11},{9,8},{10,9... | collective-permute-start | bytes 24584 | tf_op jit(solution)/shard_map/ppermute | solution.py:90
  119.4 7.2 %copy-start.10 = (bf16[512,1024]{1,0:T(8,128)(2,1)S(1)}, bf16[512,1024]{1,0:T(8,128)(2,1)}, u32[]{:S(2)}) copy-start(bf16[512,1024]{1,0:T(8,128)(2,1)} %param.21) | copy-start | bytes 3145732
  126.9 4.2 %collective-permute-start.5 = (bf16[2,1024]{1,0:T(2,128)(2,1)S(1)}, bf16[2,1024]{1,0:T(2,128)(2,1)S(1)}, u32[]{:S(2)}, u32[]{:S(2)}) collective-permute-start(bf16[2,1024]{1,0:T(2,128)(2,1)S(1)} %fusion.75), channel_id=1, source_target_pairs={{0,3},{1,0},{2,1},{3,2},{4,7},{5,4},{6,5},{7,6},{8,11},{9,8},{10,9... | collective-permute-start | bytes 12296 | tf_op jit(solution)/shard_map/ppermute | solution.py:90
  130.2 4.2 %collective-permute-start.4 = (bf16[2,1024]{1,0:T(2,128)(2,1)S(1)}, bf16[2,1024]{1,0:T(2,128)(2,1)S(1)}, u32[]{:S(2)}, u32[]{:S(2)}) collective-permute-start(bf16[2,1024]{1,0:T(2,128)(2,1)S(1)} %fusion.75), channel_id=1, source_target_pairs={{0,2},{1,3},{2,0},{3,1},{4,6},{5,7},{6,4},{7,5},{8,10},{9,11},{10,... | collective-permute-start | bytes 12296 | tf_op jit(solution)/shard_map/ppermute | solution.py:90
  130.3 4.3 %collective-permute-start.3 = (bf16[2,1024]{1,0:T(2,128)(2,1)S(1)}, bf16[2,1024]{1,0:T(2,128)(2,1)S(1)}, u32[]{:S(2)}, u32[]{:S(2)}) collective-permute-start(bf16[2,1024]{1,0:T(2,128)(2,1)S(1)} %fusion.75), channel_id=1, source_target_pairs={{0,1},{1,2},{2,3},{3,0},{4,5},{5,6},{6,7},{7,4},{8,9},{9,10},{10,1... | collective-permute-start | bytes 12296 | tf_op jit(solution)/shard_map/ppermute | solution.py:90
  135.3 6.4 %collective-permute-start.6 = (bf16[1,2,4096]{2,1,0:T(2,128)(2,1)S(1)}, bf16[1,2,4096]{2,1,0:T(2,128)(2,1)S(1)}, u32[]{:S(2)}, u32[]{:S(2)}) collective-permute-start(bf16[1,2,4096]{2,1,0:T(2,128)(2,1)S(1)} %bitcast.553), channel_id=1, source_target_pairs={{0,4},{4,0},{8,12},{12,8},{16,20},{20,16},{24,28},{28,24},{32,36},... | collective-permute-start | bytes 49160 | tf_op jit(solution)/shard_map/ppermute | solution.py:101
  141.7 3.6 %collective-permute-start.7 = (bf16[2,2,4096]{2,1,0:T(2,128)(2,1)S(1)}, bf16[2,2,4096]{2,1,0:T(2,128)(2,1)S(1)}, u32[]{:S(2)}, u32[]{:S(2)}) collective-permute-start(bf16[2,2,4096]{2,1,0:T(2,128)(2,1)S(1)} %broadcast_select_fusion.5), channel_id=1, source_target_pairs={{0,8},{4,12},{8,0},{12,4},{16,24},{20,28},{24,16},{28,20},{32,40},... | collective-permute-start | bytes 98312 | tf_op jit(solution)/shard_map/ppermute | solution.py:101
  145.4 15.1 %collective-permute-start.8 = (bf16[4,2,4096]{2,1,0:T(2,128)(2,1)S(1)}, bf16[4,2,4096]{2,1,0:T(2,128)(2,1)S(1)}, u32[]{:S(2)}, u32[]{:S(2)}) collective-permute-start(bf16[4,2,4096]{2,1,0:T(2,128)(2,1)S(1)} %broadcast_select_fusion.3), channel_id=1, source_target_pairs={{0,16},{4,20},{8,24},{12,28},{16,0},{20,4},{24,8},{28,12},{32,48},... | collective-permute-start | bytes 196616 | tf_op jit(solution)/shard_map/ppermute | solution.py:101
  160.8 12.7 %collective-permute-start.9 = (bf16[8,2,4096]{2,1,0:T(2,128)(2,1)S(1)}, bf16[8,2,4096]{2,1,0:T(2,128)(2,1)S(1)}, u32[]{:S(2)}, u32[]{:S(2)}) collective-permute-start(bf16[8,2,4096]{2,1,0:T(2,128)(2,1)S(1)} %broadcast_select_fusion.2), channel_id=1, source_target_pairs={{0,32},{4,36},{8,40},{12,44},{16,48},{20,52},{24,56},{28,60},{32,0... | collective-permute-start | bytes 393224 | tf_op jit(solution)/shard_map/ppermute | solution.py:101
  174.1 40.2 %collective-permute-start.10 = (bf16[16,2,4096]{2,1,0:T(2,128)(2,1)S(1)}, bf16[16,2,4096]{2,1,0:T(2,128)(2,1)S(1)}, u32[]{:S(2)}, u32[]{:S(2)}) collective-permute-start(bf16[16,2,4096]{2,1,0:T(2,128)(2,1)S(1)} %broadcast_select_fusion.1), channel_id=1, source_target_pairs={{0,64},{4,68},{8,72},{12,76},{16,80},{20,84},{24,88},{28,92},{32,9... | collective-permute-start | bytes 786440 | tf_op jit(solution)/shard_map/ppermute | solution.py:101
  214.3 3.3 %copy-start.11 = (f32[4096]{0:T(1024)S(1)}, f32[4096]{0:T(1024)}, u32[]{:S(2)}) copy-start(f32[4096]{0:T(1024)} %param.23) | copy-start | bytes 49156
  215.9 4.8 %copy-start.1 = (bf16[256,4096]{1,0:T(8,128)(2,1)S(1)}, bf16[256,4096]{1,0:T(8,128)(2,1)}, u32[]{:S(2)}) copy-start(bf16[256,4096]{1,0:T(8,128)(2,1)} %param.22) | copy-start | bytes 6291460
Sparse Core Ops, SparseCore 0:
  10.2 76.3 all-gather.5
  102.5 50.8 all-gather.3
  155.0 48.6 all-gather.7

commit v10 on v9

--- a/solution.py
+++ b/solution.py
@@ -221,8 +221,11 @@
 
     mixer_f32 = None
     for half in range(groups):
-        part = jnp.dot(gated_parts[half], w_blocks[:, half].reshape(-1, width),
-                       preferred_element_type=jnp.float32)
+        part = None
+        for src in range(seq_count):
+            cols = gated_parts[half][:, src * block_cols : (src + 1) * block_cols]
+            piece = jnp.dot(cols, w_blocks[src, half], preferred_element_type=jnp.float32)
+            part = piece if part is None else part + piece
         mixer_f32 = part if mixer_f32 is None else mixer_f32 + part
     mixer = mixer_f32.astype(jnp.bfloat16)
     layer_out = (resid.astype(jnp.float32) + mixer.astype(jnp.float32)).astype(jnp.bfloat16)

time: 228 us -> 246 us (1.079)
  waiting for transfers between devices: 65.7 us -> 96 us
  local copies, waits for them, and re-layouts: 45.3 us -> 29.5 us
  matrix products: 52.7 us -> 60.1 us
  starting transfers between devices: 31.8 us -> 25.7 us
    all_gather x2, waiting for transfers between devices: 27.1 us -> 61.9 us  [mixer_layer(): gated_parts.append(lax.all_gather(gated, 'seq', axis=1, tiled=True))]
    slice x1 -> x0, local copies, waits for them, and re-layouts: 11.6 us -> none  [mixer_layer(): w_blocks[:, half].reshape(-1, width)]
    dot_general x2 -> x8, matrix products: 21.9 us -> 31.8 us  [mixer_layer(): jnp.dot(cols, w_blocks[src, half], preferred_element_type=jnp.float32)]
    ppermute x5, starting transfers between devices: 14.8 us -> 9.18 us  [gather_by_doubling(): other = lax.ppermute(acc, axis, perm=pairs)]
    ppermute x6, waiting for transfers between devices: 4.73 us -> 1.04 us  [gather_by_shifts(): parts.append(lax.ppermute(value, axis, perm=pairs))]
    dot_general x8, matrix products: 4.56 us -> 1.46 us  [block_terms(): jnp.einsum('tgn,sgn->gts', cmat, bmat, preferred_element_type=jnp.float32)]
    unnamed x41 -> x55, local copies, waits for them, and re-layouts: 19.5 us -> 17.1 us
  transfers between devices with their start and end apart: 16 -> 16, of which waited for: 10 -> 7; matrix products, arithmetic and copies ran while one was open for 43% -> 36% of each run, Pallas kernels for 0% -> 0%
where the time goes in v10:
time: 246 us; the launch traced here: 244 us
  waiting for transfers between devices  96 us (39%)
  matrix products  60.1 us (24%)
  local copies, waits for them, and re-layouts  29.5 us (12%)
  starting transfers between devices  25.7 us (10%)
  between operations  17.9 us (7%)
  other arithmetic  15 us (6%)
    all_gather x2, waiting for transfers between devices, mixer_layer(): gated_parts.append(lax.all_gather(gated, 'seq', axis=1, tiled=True))  61.9 us
    dot_general x8, matrix products, mixer_layer(): jnp.dot(cols, w_blocks[src, half], preferred_element_type=jnp.float32)  31.8 us
    all_to_all x2, waiting for transfers between devices, mixer_layer(): lax.all_to_all(packed, 'seq', split_axis=0, concat_axis=0, tiled=True)  31.2 us
    unnamed x55, local copies, waits for them, and re-layouts  17.1 us
    all_to_all x2, starting transfers between devices, mixer_layer(): lax.all_to_all(packed, 'seq', split_axis=0, concat_axis=0, tiled=True)  9.77 us
    ppermute x5, starting transfers between devices, gather_by_doubling(): other = lax.ppermute(acc, axis, perm=pairs)  9.18 us
    dot_general x1, matrix products, mixer_layer(): jnp.einsum('sthj,shjo->to', picked, w_blocks, preferred_element_type=jnp....  7.56 us
    ppermute x6, starting transfers between devices, gather_by_shifts(): parts.append(lax.ppermute(value, axis, perm=pairs))  6.43 us
  transfers between devices with their start and end apart: 16, of which 7 were waited for; matrix products, arithmetic and copies ran while one was open for 36% of the time, Pallas kernels for 0%

profile of v10, /device:TPU:1, one launch (start us, length us, event | category | flops | bytes accessed | tf_op | source)
XLA Modules:
  0.0 244.4 jit_solution(14266090602382766105)
XLA Ops:
  7.2 1.5 copy-done
  8.8 0.9 constant_dynamic-slice_fusion
  9.7 1.0 copy.525
  10.7 1.1 fusion.335
  12.1 2.4 %copy.518 = bf16[128,8192]{0,1:T(8,128)(2,1)} copy(bf16[128,8192]{1,0:T(8,128)(2,1)S(1)} %copy-done.15) | data formatting | bytes 4194304 | tf_op args[0]
  14.6 3.2 %copy.519 = bf16[128,8192]{0,1:T(8,128)(2,1)S(1)} copy(bf16[128,8192]{1,0:T(8,128)(2,1)} %param.15) | data formatting | bytes 4194304 | tf_op args[2]
  17.8 1.7 fusion.103
  19.9 1.4 copy-done.8
  21.3 1.4 copy-done.9
  22.8 5.1 %all-to-all-start = ((bf16[4,128,2320]{1,2,0:T(8,128)(2,1)}), bf16[4,128,2320]{1,2,0:T(8,128)(2,1)}, u32[]{:S(2)}, u32[]{:S(2)}) async-start(bf16[4,128,2320]{1,2,0:T(8,128)(2,1)} %copy-done.8), calls=%async_computation | async-start | bytes 4751360 | tf_op jit(solution)/shard_map/all_to_all | solution.py:165
  28.2 0.6 fusion.338
  32.2 0.7 fusion.336
  32.9 1.9 slice_convert_fusion
  35.1 21.9 %all-to-all-done = bf16[4,128,2320]{1,2,0:T(8,128)(2,1)} async-done(((bf16[4,128,2320]{1,2,0:T(8,128)(2,1)}), bf16[4,128,2320]{1,2,0:T(8,128)(2,1)}, u32[]{:S(2)}, u32[]{:S(2)}) %all-to-all-start) | async-done | bytes 2375712 | tf_op jit(solution)/shard_map/all_to_all | solution.py:165
  56.9 4.6 %all-to-all-start.1 = ((bf16[4,128,2320]{1,2,0:T(8,128)(2,1)}), bf16[4,128,2320]{1,2,0:T(8,128)(2,1)}, u32[]{:S(2)}, u32[]{:S(2)}) async-start(bf16[4,128,2320]{1,2,0:T(8,128)(2,1)} %copy-done.9), calls=%async_computation.1 | async-start | bytes 4751360 | tf_op jit(solution)/shard_map/all_to_all | solution.py:165
  61.8 2.1 copy_bitcast_fusion.1
  63.9 1.4 copy-done.4
  67.7 1.6 subtract_convert_fusion.27
  70.6 0.6 fusion.61
  75.9 0.6 fusion.63
  77.0 0.6 fusion.67
  77.7 0.6 fusion.65
  78.3 0.7 multiply_reduce_fusion.1
  79.0 1.2 multiply_convert_fusion.1
  80.2 9.4 %all-to-all-done.1 = bf16[4,128,2320]{1,2,0:T(8,128)(2,1)} async-done(((bf16[4,128,2320]{1,2,0:T(8,128)(2,1)}), bf16[4,128,2320]{1,2,0:T(8,128)(2,1)}, u32[]{:S(2)}, u32[]{:S(2)}) %all-to-all-start.1) | async-done | bytes 2375712 | tf_op jit(solution)/shard_map/all_to_all | solution.py:165
  89.6 1.8 copy_bitcast_fusion
  91.4 1.4 copy-done.2
  95.1 1.5 subtract_convert_fusion.21
  97.9 0.6 fusion.49
  100.8 0.6 fusion.192
  103.9 0.6 fusion.69
  104.5 0.6 fusion.73
  105.1 0.6 fusion.71
  105.7 0.7 multiply_reduce_fusion
  106.4 1.3 multiply_convert_fusion
  107.7 0.7 all-gather.4.cloned.1.call-update
  109.9 1.1 collective-permute-start
  111.0 1.6 collective-permute-start.2
  112.6 0.9 collective-permute-done.1
  113.7 0.6 gather_fusion
  114.3 7.6 %fusion.87 = f32[2,1024]{1,0:T(2,128)S(1)} fusion(bf16[4,2,1024,1024]{3,2,1,0:T(8,128)(2,1)} %bitcast.530, bf16[4,2,2,1024]{3,1,2,0:T(2,128)(2,1)S(1)} %gather_fusion, pred[4]{0:T(512)(128)(4,1)S(1)} %compare_and_fusion), kind=kOutput, calls=%fused_computation.128 | convolution fusion | flops 33574912 | bytes 16818180 | tf_op jit(solution)/shard_map/sthj,shjo->to/dot_general | solution.py:211
  122.2 2.7 %collective-permute-start.5 = (bf16[2,1024]{1,0:T(2,128)(2,1)S(1)}, bf16[2,1024]{1,0:T(2,128)(2,1)S(1)}, u32[]{:S(2)}, u32[]{:S(2)}) collective-permute-start(bf16[2,1024]{1,0:T(2,128)(2,1)S(1)} %fusion.83), channel_id=1, source_target_pairs={{0,3},{1,0},{2,1},{3,2},{4,7},{5,4},{6,5},{7,6},{8,11},{9,8},{10,9... | collective-permute-start | bytes 12296 | tf_op jit(solution)/shard_map/ppermute | solution.py:90
  124.9 0.6 collective-permute-start.3
  125.5 32.7 %all-gather.8.cloned.1.call-done = bf16[512,4096]{0,1:T(8,128)(2,1)} async-done(((bf16[512,1024]{0,1:T(8,128)(2,1)}), bf16[512,4096]{0,1:T(8,128)(2,1)}) %all-gather.8.cloned.1.call-update) | async-done | bytes 4194320 | tf_op jit(solution)/shard_map/all_gather | solution.py:204
  158.1 4.7 %fusion.10 = f32[512,1024]{1,0:T(8,128)} fusion(bf16[4,2,1024,1024]{3,2,1,0:T(8,128)(2,1)} %bitcast.531, bf16[512,4096]{0,1:T(8,128)(2,1)} %all-gather.8.cloned.1.call-done), kind=kOutput, calls=%fused_computation.19 | convolution fusion | flops 1073741824 | bytes 5242880 | tf_op jit(solution)/shard_map/dot_general | solution.py:227
  162.8 4.3 %fusion.11 = f32[512,1024]{1,0:T(8,128)} fusion(bf16[4,2,1024,1024]{3,2,1,0:T(8,128)(2,1)} %bitcast.532, bf16[512,4096]{0,1:T(8,128)(2,1)S(1)} %copy-done.21), kind=kOutput, calls=%fused_computation.21 | convolution fusion | flops 1073741824 | bytes 5242880 | tf_op jit(solution)/shard_map/dot_general | solution.py:227
  167.1 4.2 %fusion.12 = f32[512,1024]{1,0:T(8,128)} fusion(bf16[4,2,1024,1024]{3,2,1,0:T(8,128)(2,1)} %bitcast.533, bf16[512,4096]{0,1:T(8,128)(2,1)S(1)} %copy-done.21), kind=kOutput, calls=%fused_computation.23 | convolution fusion | flops 1073741824 | bytes 5242880 | tf_op jit(solution)/shard_map/dot_general | solution.py:227
  171.3 0.6 gather_fusion.1
  172.0 0.9 collective-permute-start.6
  172.9 4.5 %fusion.13 = f32[512,1024]{1,0:T(8,128)} fusion(bf16[4,2,1024,1024]{3,2,1,0:T(8,128)(2,1)} %bitcast.534, bf16[512,4096]{0,1:T(8,128)(2,1)} %all-gather.8.cloned.1.call-done), kind=kOutput, calls=%fused_computation.25 | convolution fusion | flops 1073741824 | bytes 5242880 | tf_op jit(solution)/shard_map/dot_general | solution.py:227
  177.5 1.6 collective-permute-start.7
  179.2 29.2 %all-gather.4.cloned.1.call-done = bf16[512,4096]{0,1:T(8,128)(2,1)} async-done(((bf16[512,1024]{0,1:T(8,128)(2,1)}), bf16[512,4096]{0,1:T(8,128)(2,1)}) %all-gather.4.cloned.1.call-update) | async-done | bytes 4194320 | tf_op jit(solution)/shard_map/all_gather | solution.py:204
  208.4 3.3 %fusion.14 = f32[512,1024]{1,0:T(8,128)S(1)} fusion(bf16[4,2,1024,1024]{3,2,1,0:T(8,128)(2,1)} %bitcast.535, bf16[512,4096]{0,1:T(8,128)(2,1)} %all-gather.4.cloned.1.call-done), kind=kOutput, calls=%fused_computation.27 | convolution fusion | flops 1073741824 | bytes 5242880 | tf_op jit(solution)/shard_map/dot_general | solution.py:227
  211.9 3.0 %collective-permute-start.8 = (bf16[4,2,4096]{2,1,0:T(2,128)(2,1)S(1)}, bf16[4,2,4096]{2,1,0:T(2,128)(2,1)S(1)}, u32[]{:S(2)}, u32[]{:S(2)}) collective-permute-start(bf16[4,2,4096]{2,1,0:T(2,128)(2,1)S(1)} %broadcast_select_fusion.3), channel_id=1, source_target_pairs={{0,16},{4,20},{8,24},{12,28},{16,0},{20,4},{24,8},{28,12},{32,48},... | collective-permute-start | bytes 196616 | tf_op jit(solution)/shard_map/ppermute | solution.py:101
  214.8 3.0 %fusion.15 = f32[512,1024]{1,0:T(8,128)S(1)} fusion(bf16[4,2,1024,1024]{3,2,1,0:T(8,128)(2,1)} %bitcast.536, bf16[512,4096]{0,1:T(8,128)(2,1)S(1)} %copy-done.16), kind=kOutput, calls=%fused_computation.29 | convolution fusion | flops 1073741824 | bytes 5242880 | tf_op jit(solution)/shard_map/dot_general | solution.py:227
  218.2 1.3 collective-permute-start.9
  219.4 3.4 %fusion.16 = f32[512,1024]{1,0:T(8,128)S(1)} fusion(bf16[4,2,1024,1024]{3,2,1,0:T(8,128)(2,1)} %bitcast.537, bf16[512,4096]{0,1:T(8,128)(2,1)S(1)} %copy-done.16), kind=kOutput, calls=%fused_computation.31 | convolution fusion | flops 1073741824 | bytes 5242880 | tf_op jit(solution)/shard_map/dot_general | solution.py:227
  222.9 0.6 broadcast_select_fusion.1
  223.5 2.4 collective-permute-start.10
  225.9 4.4 %add_convert_fusion = bf16[512,1024]{1,0:T(8,128)(2,1)} fusion(bf16[512,1024]{1,0:T(8,128)(2,1)S(1)} %copy-done.10, f32[512,1024]{1,0:T(8,128)S(1)} %copy-done.11, f32[512,1024]{1,0:T(8,128)S(1)} %copy-done.12, f32[512,1024]{1,0:T(8,128)S(1)} %copy-done.14, f32[512,1024]{1,0:T(8,128)S(1)} %copy-done.13, f32[512,1024]{1,0:T(8,128)S(1)} %fusion.14, ...), kind=kOutput, calls=%fused_computation.34 | convolution fusion | flops 1080033280 | bytes 19922944 | tf_op jit(solution)/shard_map/dot_general | solution.py:227
  230.3 1.1 collective-permute-done.10
  231.5 1.5 multiply_reduce_fusion.2
  233.1 1.7 reshape.939
  234.8 3.1 %fusion.113 = f32[64,256]{1,0:T(8,128)} fusion(bf16[4096,256]{1,0:T(8,128)(2,1)} %param.24, f32[64,4096]{1,0:T(8,128)} %reshape.939, f32[4096]{0:T(1024)S(1)} %copy-done.17, f32[64]{0:T(128)S(1)} %rsqrt.30), kind=kOutput, calls=%fused_computation.177 | convolution fusion | flops 135004160 | bytes 3227904 | tf_op jit(solution)/shard_map/dot_general | solution.py:220
  (192 shorter events, 21.1 us)
Async XLA Ops:
  7.2 1.6 copy-start
  7.2 107.1 %all-gather.6.cloned.1.call-start = ((), (), s32[]{:S(2)}) async-start(), calls=%async_computation.3 | async-start | bytes 17301504 | tf_op jit(solution)/shard_map/all_gather | solution.py:143
  9.7 2.5 %copy-start.15 = (bf16[128,8192]{1,0:T(8,128)(2,1)S(1)}, bf16[128,8192]{1,0:T(8,128)(2,1)}, u32[]{:S(2)}) copy-start(bf16[128,8192]{1,0:T(8,128)(2,1)} %param.13) | copy-start | bytes 6291460
  19.9 1.4 copy-start.8
  21.3 1.4 copy-start.9
  22.8 5.2 %copy-start.22 = (s32[1,2]{1,0:T(1,128)S(1)}, s32[1,2]{1,0:T(1,128)}, u32[]{:S(2)}) copy-start(s32[1,2]{1,0:T(1,128)} %param.25) | copy-start | bytes 28
  22.8 9.3 %copy-start.18 = (f32[128]{0:T(128)S(1)}, f32[128]{0:T(128)}, u32[]{:S(2)}) copy-start(f32[128]{0:T(128)} %param.17) | copy-start | bytes 1540
  22.8 9.4 %copy-start.19 = (f32[128]{0:T(128)S(1)}, f32[128]{0:T(128)}, u32[]{:S(2)}) copy-start(f32[128]{0:T(128)} %param.18) | copy-start | bytes 1540
  22.8 9.4 %copy-start.20 = (f32[128]{0:T(128)S(1)}, f32[128]{0:T(128)}, u32[]{:S(2)}) copy-start(f32[128]{0:T(128)} %param.19) | copy-start | bytes 1540
  22.8 34.2 %all-to-all-start = ((bf16[4,128,2320]{1,2,0:T(8,128)(2,1)}), bf16[4,128,2320]{1,2,0:T(8,128)(2,1)}, u32[]{:S(2)}, u32[]{:S(2)}) async-start(bf16[4,128,2320]{1,2,0:T(8,128)(2,1)} %copy-done.8), calls=%async_computation | async-start | bytes 4751360 | tf_op jit(solution)/shard_map/all_to_all | solution.py:165
  56.9 32.6 %all-to-all-start.1 = ((bf16[4,128,2320]{1,2,0:T(8,128)(2,1)}), bf16[4,128,2320]{1,2,0:T(8,128)(2,1)}, u32[]{:S(2)}, u32[]{:S(2)}) async-start(bf16[4,128,2320]{1,2,0:T(8,128)(2,1)} %copy-done.9), calls=%async_computation.1 | async-start | bytes 4751360 | tf_op jit(solution)/shard_map/all_to_all | solution.py:165
  61.6 96.6 %all-gather.8.cloned.1.call-start = ((), (), s32[]{:S(2)}) async-start(), calls=%async_computation.4 | async-start | bytes 5242880 | tf_op jit(solution)/shard_map/all_gather | solution.py:204
  63.9 1.4 copy-start.4
  67.5 2.2 copy-start.5
  91.4 1.4 copy-start.2
  95.0 2.0 copy-start.3
  106.4 2.2 copy-start.6
  107.7 1.3 copy-start.7
  107.7 100.7 %all-gather.4.cloned.1.call-start = ((), (), s32[]{:S(2)}) async-start(), calls=%async_computation.2 | async-start | bytes 5242880 | tf_op jit(solution)/shard_map/all_gather | solution.py:204
  109.4 4.1 %collective-permute-start.1 = (bf16[2,2,1024]{2,0,1:T(2,128)(2,1)S(1)}, bf16[2,2,1024]{2,0,1:T(2,128)(2,1)S(1)}, u32[]{:S(2)}, u32[]{:S(2)}) collective-permute-start(bf16[2,2,1024]{2,0,1:T(2,128)(2,1)S(1)} %pad_maximum_fusion.2), channel_id=1, source_target_pairs={{0,2},{1,3},{2,0},{3,1},{4,6},{5,7},{6,4},{7,5},{8,10},{9,11},{10,... | collective-permute-start | bytes 24584 | tf_op jit(solution)/shard_map/ppermute | solution.py:90
  109.9 3.7 %collective-permute-start = (bf16[2,2,1024]{2,0,1:T(2,128)(2,1)S(1)}, bf16[2,2,1024]{2,0,1:T(2,128)(2,1)S(1)}, u32[]{:S(2)}, u32[]{:S(2)}) collective-permute-start(bf16[2,2,1024]{2,0,1:T(2,128)(2,1)S(1)} %pad_maximum_fusion.2), channel_id=1, source_target_pairs={{0,1},{1,2},{2,3},{3,0},{4,5},{5,6},{6,7},{7,4},{8,9},{9,10},{10,1... | collective-permute-start | bytes 24584 | tf_op jit(solution)/shard_map/ppermute | solution.py:90
  111.0 2.6 %collective-permute-start.2 = (bf16[2,2,1024]{2,0,1:T(2,128)(2,1)S(1)}, bf16[2,2,1024]{2,0,1:T(2,128)(2,1)S(1)}, u32[]{:S(2)}, u32[]{:S(2)}) collective-permute-start(bf16[2,2,1024]{2,0,1:T(2,128)(2,1)S(1)} %pad_maximum_fusion.2), channel_id=1, source_target_pairs={{0,3},{1,0},{2,1},{3,2},{4,7},{5,4},{6,5},{7,6},{8,11},{9,8},{10,9... | collective-permute-start | bytes 24584 | tf_op jit(solution)/shard_map/ppermute | solution.py:90
  114.3 7.6 %copy-start.10 = (bf16[512,1024]{1,0:T(8,128)(2,1)S(1)}, bf16[512,1024]{1,0:T(8,128)(2,1)}, u32[]{:S(2)}) copy-start(bf16[512,1024]{1,0:T(8,128)(2,1)} %param.21) | copy-start | bytes 3145732
  122.2 49.1 %collective-permute-start.5 = (bf16[2,1024]{1,0:T(2,128)(2,1)S(1)}, bf16[2,1024]{1,0:T(2,128)(2,1)S(1)}, u32[]{:S(2)}, u32[]{:S(2)}) collective-permute-start(bf16[2,1024]{1,0:T(2,128)(2,1)S(1)} %fusion.83), channel_id=1, source_target_pairs={{0,3},{1,0},{2,1},{3,2},{4,7},{5,4},{6,5},{7,6},{8,11},{9,8},{10,9... | collective-permute-start | bytes 12296 | tf_op jit(solution)/shard_map/ppermute | solution.py:90
  124.8 46.5 %collective-permute-start.4 = (bf16[2,1024]{1,0:T(2,128)(2,1)S(1)}, bf16[2,1024]{1,0:T(2,128)(2,1)S(1)}, u32[]{:S(2)}, u32[]{:S(2)}) collective-permute-start(bf16[2,1024]{1,0:T(2,128)(2,1)S(1)} %fusion.83), channel_id=1, source_target_pairs={{0,2},{1,3},{2,0},{3,1},{4,6},{5,7},{6,4},{7,5},{8,10},{9,11},{10,... | collective-permute-start | bytes 12296 | tf_op jit(solution)/shard_map/ppermute | solution.py:90
  124.9 46.4 %collective-permute-start.3 = (bf16[2,1024]{1,0:T(2,128)(2,1)S(1)}, bf16[2,1024]{1,0:T(2,128)(2,1)S(1)}, u32[]{:S(2)}, u32[]{:S(2)}) collective-permute-start(bf16[2,1024]{1,0:T(2,128)(2,1)S(1)} %fusion.83), channel_id=1, source_target_pairs={{0,1},{1,2},{2,3},{3,0},{4,5},{5,6},{6,7},{7,4},{8,9},{9,10},{10,1... | collective-permute-start | bytes 12296 | tf_op jit(solution)/shard_map/ppermute | solution.py:90
  158.1 4.7 %copy-start.21 = (bf16[512,4096]{0,1:T(8,128)(2,1)S(1)}, bf16[512,4096]{0,1:T(8,128)(2,1)}, u32[]{:S(2)}) copy-start(bf16[512,4096]{0,1:T(8,128)(2,1)} %all-gather.8.cloned.1.call-done) | copy-start | bytes 12582916
  172.0 5.4 %collective-permute-start.6 = (bf16[1,2,4096]{2,1,0:T(2,128)(2,1)S(1)}, bf16[1,2,4096]{2,1,0:T(2,128)(2,1)S(1)}, u32[]{:S(2)}, u32[]{:S(2)}) collective-permute-start(bf16[1,2,4096]{2,1,0:T(2,128)(2,1)S(1)} %bitcast.580), channel_id=1, source_target_pairs={{0,4},{4,0},{8,12},{12,8},{16,20},{20,16},{24,28},{28,24},{32,36},... | collective-permute-start | bytes 49160 | tf_op jit(solution)/shard_map/ppermute | solution.py:101
  177.5 34.2 %collective-permute-start.7 = (bf16[2,2,4096]{2,1,0:T(2,128)(2,1)S(1)}, bf16[2,2,4096]{2,1,0:T(2,128)(2,1)S(1)}, u32[]{:S(2)}, u32[]{:S(2)}) collective-permute-start(bf16[2,2,4096]{2,1,0:T(2,128)(2,1)S(1)} %broadcast_select_fusion.5), channel_id=1, source_target_pairs={{0,8},{4,12},{8,0},{12,4},{16,24},{20,28},{24,16},{28,20},{32,40},... | collective-permute-start | bytes 98312 | tf_op jit(solution)/shard_map/ppermute | solution.py:101
  208.4 6.4 %copy-start.16 = (bf16[512,4096]{0,1:T(8,128)(2,1)S(1)}, bf16[512,4096]{0,1:T(8,128)(2,1)}, u32[]{:S(2)}) copy-start(bf16[512,4096]{0,1:T(8,128)(2,1)} %all-gather.4.cloned.1.call-done) | copy-start | bytes 12582916
  211.9 6.0 %collective-permute-start.8 = (bf16[4,2,4096]{2,1,0:T(2,128)(2,1)S(1)}, bf16[4,2,4096]{2,1,0:T(2,128)(2,1)S(1)}, u32[]{:S(2)}, u32[]{:S(2)}) collective-permute-start(bf16[4,2,4096]{2,1,0:T(2,128)(2,1)S(1)} %broadcast_select_fusion.3), channel_id=1, source_target_pairs={{0,16},{4,20},{8,24},{12,28},{16,0},{20,4},{24,8},{28,12},{32,48},... | collective-permute-start | bytes 196616 | tf_op jit(solution)/shard_map/ppermute | solution.py:101
  214.8 11.0 %copy-start.14 = (f32[512,1024]{1,0:T(8,128)S(1)}, f32[512,1024]{1,0:T(8,128)}, u32[]{:S(2)}) copy-start(f32[512,1024]{1,0:T(8,128)} %fusion.13) | copy-start | bytes 6291460
  218.2 7.7 %copy-start.11 = (f32[512,1024]{1,0:T(8,128)S(1)}, f32[512,1024]{1,0:T(8,128)}, u32[]{:S(2)}) copy-start(f32[512,1024]{1,0:T(8,128)} %fusion.10) | copy-start | bytes 6291460
  218.2 7.7 %copy-start.12 = (f32[512,1024]{1,0:T(8,128)S(1)}, f32[512,1024]{1,0:T(8,128)}, u32[]{:S(2)}) copy-start(f32[512,1024]{1,0:T(8,128)} %fusion.11) | copy-start | bytes 6291460
  218.2 7.7 %copy-start.13 = (f32[512,1024]{1,0:T(8,128)S(1)}, f32[512,1024]{1,0:T(8,128)}, u32[]{:S(2)}) copy-start(f32[512,1024]{1,0:T(8,128)} %fusion.12) | copy-start | bytes 6291460
  218.2 4.7 %collective-permute-start.9 = (bf16[8,2,4096]{2,1,0:T(2,128)(2,1)S(1)}, bf16[8,2,4096]{2,1,0:T(2,128)(2,1)S(1)}, u32[]{:S(2)}, u32[]{:S(2)}) collective-permute-start(bf16[8,2,4096]{2,1,0:T(2,128)(2,1)S(1)} %broadcast_select_fusion.2), channel_id=1, source_target_pairs={{0,32},{4,36},{8,40},{12,44},{16,48},{20,52},{24,56},{28,60},{32,0... | collective-permute-start | bytes 393224 | tf_op jit(solution)/shard_map/ppermute | solution.py:101
  223.5 8.0 %collective-permute-start.10 = (bf16[16,2,4096]{2,1,0:T(2,128)(2,1)S(1)}, bf16[16,2,4096]{2,1,0:T(2,128)(2,1)S(1)}, u32[]{:S(2)}, u32[]{:S(2)}) collective-permute-start(bf16[16,2,4096]{2,1,0:T(2,128)(2,1)S(1)} %broadcast_select_fusion.1), channel_id=1, source_target_pairs={{0,64},{4,68},{8,72},{12,76},{16,80},{20,84},{24,88},{28,92},{32,9... | collective-permute-start | bytes 786440 | tf_op jit(solution)/shard_map/ppermute | solution.py:101
  230.3 4.4 %copy-start.17 = (f32[4096]{0:T(1024)S(1)}, f32[4096]{0:T(1024)}, u32[]{:S(2)}) copy-start(f32[4096]{0:T(1024)} %param.23) | copy-start | bytes 49156
  233.1 4.8 %copy-start.1 = (bf16[256,4096]{1,0:T(8,128)(2,1)S(1)}, bf16[256,4096]{1,0:T(8,128)(2,1)}, u32[]{:S(2)}) copy-start(bf16[256,4096]{1,0:T(8,128)(2,1)} %param.22) | copy-start | bytes 6291460
Sparse Core Ops, SparseCore 0:
  10.2 76.2 all-gather.5
  107.8 50.2 all-gather.7
  159.8 48.5 all-gather.3

commit v11 on v9

--- a/solution.py
+++ b/solution.py
@@ -141,13 +141,13 @@
     width = resid.shape[1]
     w_cols = lax.dynamic_slice_in_dim(w_out, place * width, width, axis=1)
     w_full = lax.all_gather(w_cols, "req", axis=0, tiled=True)
-    w_blocks = w_full.reshape(seq_count, groups, inner // NGROUPS, width)
+    w_blocks = w_full.reshape(groups, seq_count, inner // NGROUPS, width)
 
     block_cols = inner // NGROUPS
     block_heads = heads // groups
 
     def by_dest(part, width_of, half):
-        piece = part.reshape(rows, seq_count, groups, width_of)[:, :, half, :]
+        piece = part.reshape(rows, groups, seq_count, width_of)[:, half, :, :]
         return piece.transpose(1, 0, 2)
 
     moves = []
@@ -177,7 +177,7 @@
         cg = moved[:, 2 * block_cols + STATE : 2 * block_cols + 2 * STATE]
         dg = moved[:, 2 * block_cols + 2 * STATE :]
 
-        first_head = (place * groups + half) * block_heads
+        first_head = (half * seq_count + place) * block_heads
         my_heads = lambda v: lax.dynamic_slice_in_dim(v, first_head, block_heads)
         rate = jnp.exp(my_heads(a_log))
         skipw = my_heads(d_skip)
@@ -199,7 +199,7 @@
             state_in = keep[:, None, None] * state_in + state
             prev_seg = segment[hi - 1]
         y = jnp.concatenate(ys, axis=0)
-        gain = lax.dynamic_slice_in_dim(norm_gain, (place * groups + half) * block_cols, block_cols)
+        gain = lax.dynamic_slice_in_dim(norm_gain, (half * seq_count + place) * block_cols, block_cols)
         gated = gate_norm(y, zg, gain, 1)
         gated_parts.append(lax.all_gather(gated, "seq", axis=1, tiled=True))
         picked_parts.append(
@@ -208,7 +208,7 @@
 
     picked_resid = jnp.dot(picker, resid, preferred_element_type=jnp.float32)
     picked = gather_by_shifts(jnp.stack(picked_parts, axis=1), "seq")
-    picked_mixer = jnp.einsum("sthj,shjo->to", picked, w_blocks, preferred_element_type=jnp.float32)
+    picked_mixer = jnp.einsum("sthj,hsjo->to", picked, w_blocks, preferred_element_type=jnp.float32)
     picked_rows = (
         picked_resid + picked_mixer.astype(jnp.bfloat16).astype(jnp.float32)
     ).astype(jnp.bfloat16)
@@ -221,7 +221,7 @@
 
     mixer_f32 = None
     for half in range(groups):
-        part = jnp.dot(gated_parts[half], w_blocks[:, half].reshape(-1, width),
+        part = jnp.dot(gated_parts[half], w_blocks[half].reshape(-1, width),
                        preferred_element_type=jnp.float32)
         mixer_f32 = part if mixer_f32 is None else mixer_f32 + part
     mixer = mixer_f32.astype(jnp.bfloat16)

time: 228 us -> 233 us (1.022)
  waiting for transfers between devices: 65.7 us -> 85.6 us
  local copies, waits for them, and re-layouts: 45.3 us -> 29.8 us
    all_gather x2, waiting for transfers between devices: 27.1 us -> 45.7 us  [mixer_layer(): gated_parts.append(lax.all_gather(gated, 'seq', axis=1, tiled=True))]
    slice x1, local copies, waits for them, and re-layouts: 11.6 us -> 0.17 us  [mixer_layer(): bc[:, :NGROUPS * STATE]]
    dot_general x8, matrix products: 4.56 us -> 1.46 us  [block_terms(): jnp.einsum('tgn,sgn->gts', cmat, bmat, preferred_element_type=jnp.float32)]
  transfers between devices with their start and end apart: 16 -> 16, of which waited for: 10 -> 13; matrix products, arithmetic and copies ran while one was open for 43% -> 35% of each run, Pallas kernels for 0% -> 0%
where the time goes in v11:
time: 233 us
  waiting for transfers between devices  85.6 us (37%)
  matrix products  51.8 us (22%)
  starting transfers between devices  31.7 us (14%)
  local copies, waits for them, and re-layouts  29.8 us (13%)
  between operations  17.9 us (8%)
  other arithmetic  16 us (7%)
    all_gather x2, waiting for transfers between devices, mixer_layer(): gated_parts.append(lax.all_gather(gated, 'seq', axis=1, tiled=True))  45.7 us
    all_to_all x2, waiting for transfers between devices, mixer_layer(): lax.all_to_all(packed, 'seq', split_axis=0, concat_axis=0, tiled=True)  30.7 us
    dot_general x2, matrix products, mixer_layer(): jnp.dot(gated_parts[half], w_blocks[half].reshape(-1, width), preferred_e...  21.2 us
    unnamed x41, local copies, waits for them, and re-layouts  17.5 us
    ppermute x5, starting transfers between devices, gather_by_doubling(): other = lax.ppermute(acc, axis, perm=pairs)  14.9 us
    all_to_all x2, starting transfers between devices, mixer_layer(): lax.all_to_all(packed, 'seq', split_axis=0, concat_axis=0, tiled=True)  9.65 us
    dot_general x1, matrix products, mixer_layer(): jnp.einsum('sthj,hsjo->to', picked, w_blocks, preferred_element_type=jnp....  8.94 us
    ppermute x6, starting transfers between devices, gather_by_shifts(): parts.append(lax.ppermute(value, axis, perm=pairs))  6.81 us
  transfers between devices with their start and end apart: 16, of which 13 were waited for; matrix products, arithmetic and copies ran while one was open for 35% of the time, Pallas kernels for 0%

profile of v11, /device:TPU:1, one launch (start us, length us, event | category | flops | bytes accessed | tf_op | source)
XLA Modules:
  0.0 232.7 jit_solution(573145311861065704)
XLA Ops:
  7.2 1.5 copy-done
  8.8 0.9 constant_dynamic-slice_fusion
  9.7 4.1 %copy.413 = bf16[128,8192]{0,1:T(8,128)(2,1)} copy(bf16[128,8192]{1,0:T(8,128)(2,1)} %param.13) | data formatting | bytes 4194304 | tf_op args[0]
  13.8 3.3 %copy.414 = bf16[128,8192]{0,1:T(8,128)(2,1)S(1)} copy(bf16[128,8192]{1,0:T(8,128)(2,1)} %param.15) | data formatting | bytes 4194304 | tf_op args[2]
  17.6 1.7 fusion.86
  19.7 1.4 copy-done.7
  21.1 1.4 copy-done.8
  22.6 5.1 %all-to-all-start = ((bf16[4,128,2320]{1,2,0:T(8,128)(2,1)}), bf16[4,128,2320]{1,2,0:T(8,128)(2,1)}, u32[]{:S(2)}, u32[]{:S(2)}) async-start(bf16[4,128,2320]{1,2,0:T(8,128)(2,1)} %copy-done.7), calls=%async_computation | async-start | bytes 4751360 | tf_op jit(solution)/shard_map/all_to_all | solution.py:165
  28.0 0.7 fusion.321
  32.2 0.7 fusion.319
  32.9 2.0 slice_convert_fusion
  35.1 21.7 %all-to-all-done = bf16[4,128,2320]{1,2,0:T(8,128)(2,1)} async-done(((bf16[4,128,2320]{1,2,0:T(8,128)(2,1)}), bf16[4,128,2320]{1,2,0:T(8,128)(2,1)}, u32[]{:S(2)}, u32[]{:S(2)}) %all-to-all-start) | async-done | bytes 2375712 | tf_op jit(solution)/shard_map/all_to_all | solution.py:165
  56.8 4.5 %all-to-all-start.1 = ((bf16[4,128,2320]{1,2,0:T(8,128)(2,1)}), bf16[4,128,2320]{1,2,0:T(8,128)(2,1)}, u32[]{:S(2)}, u32[]{:S(2)}) async-start(bf16[4,128,2320]{1,2,0:T(8,128)(2,1)} %copy-done.8), calls=%async_computation.1 | async-start | bytes 4751360 | tf_op jit(solution)/shard_map/all_to_all | solution.py:165
  61.5 2.1 copy_bitcast_fusion.1
  63.7 1.4 copy-done.4
  67.4 1.7 subtract_convert_fusion.27
  70.5 0.6 fusion.59
  72.9 0.6 fusion.160
  75.7 0.6 fusion.61
  76.9 0.6 fusion.63
  77.5 0.6 fusion.65
  78.1 0.7 multiply_reduce_fusion.1
  78.8 1.2 multiply_convert_fusion.1
  80.0 9.1 %all-to-all-done.1 = bf16[4,128,2320]{1,2,0:T(8,128)(2,1)} async-done(((bf16[4,128,2320]{1,2,0:T(8,128)(2,1)}), bf16[4,128,2320]{1,2,0:T(8,128)(2,1)}, u32[]{:S(2)}, u32[]{:S(2)}) %all-to-all-start.1) | async-done | bytes 2375712 | tf_op jit(solution)/shard_map/all_to_all | solution.py:165
  89.1 1.8 copy_bitcast_fusion
  91.0 1.4 copy-done.2
  94.7 1.5 subtract_convert_fusion.21
  97.4 0.6 fusion.47
  99.8 0.6 fusion.172
  103.4 0.6 fusion.67
  104.0 0.6 fusion.69
  104.7 0.6 fusion.71
  105.3 0.7 multiply_reduce_fusion
  106.0 1.3 multiply_convert_fusion
  107.3 0.7 all-gather.4.cloned.1.call-update
  108.1 1.6 fusion.82
  110.4 1.8 collective-permute-start.1
  112.2 0.7 collective-permute-start.2
  112.9 0.9 collective-permute-done
  113.9 0.6 collective-permute-done.1
  114.8 0.6 gather_fusion
  115.4 8.9 %fusion.79 = f32[2,1024]{1,0:T(2,128)S(1)} fusion(bf16[2,4,1024,1024]{3,2,1,0:T(8,128)(2,1)} %bitcast.489, bf16[4,2,2,1024]{3,1,2,0:T(2,128)(2,1)S(1)} %gather_fusion, pred[4]{0:T(512)(128)(4,1)S(1)} %compare_and_fusion), kind=kOutput, calls=%fused_computation.113 | convolution fusion | flops 33574912 | bytes 16818180 | tf_op jit(solution)/shard_map/sthj,hsjo->to/dot_general | solution.py:211
  124.7 1.5 collective-permute-start.3
  126.2 1.7 collective-permute-start.4
  127.9 0.7 collective-permute-start.5
  129.0 1.4 collective-permute-done.4
  130.4 0.6 collective-permute-done.5
  131.0 0.6 gather_fusion.1
  131.7 5.5 %collective-permute-start.6 = (bf16[1,2,4096]{2,1,0:T(2,128)(2,1)S(1)}, bf16[1,2,4096]{2,1,0:T(2,128)(2,1)S(1)}, u32[]{:S(2)}, u32[]{:S(2)}) collective-permute-start(bf16[1,2,4096]{2,1,0:T(2,128)(2,1)S(1)} %bitcast.531), channel_id=1, source_target_pairs={{0,4},{4,0},{8,12},{12,8},{16,20},{20,16},{24,28},{28,24},{32,36},... | collective-permute-start | bytes 49160 | tf_op jit(solution)/shard_map/ppermute | solution.py:101
  137.2 0.8 collective-permute-done.6
  138.1 1.7 collective-permute-start.7
  139.8 1.7 collective-permute-done.7
  141.6 3.4 %collective-permute-start.8 = (bf16[4,2,4096]{2,1,0:T(2,128)(2,1)S(1)}, bf16[4,2,4096]{2,1,0:T(2,128)(2,1)S(1)}, u32[]{:S(2)}, u32[]{:S(2)}) collective-permute-start(bf16[4,2,4096]{2,1,0:T(2,128)(2,1)S(1)} %broadcast_select_fusion.3), channel_id=1, source_target_pairs={{0,16},{4,20},{8,24},{12,28},{16,0},{20,4},{24,8},{28,12},{32,48},... | collective-permute-start | bytes 196616 | tf_op jit(solution)/shard_map/ppermute | solution.py:101
  145.0 1.7 collective-permute-done.8
  147.0 1.5 collective-permute-start.9
  148.6 9.4 %all-gather.8.cloned.1.call-done = bf16[512,4096]{0,1:T(8,128)(2,1)} async-done(((bf16[512,1024]{0,1:T(8,128)(2,1)}), bf16[512,4096]{0,1:T(8,128)(2,1)}) %all-gather.8.cloned.1.call-update) | async-done | bytes 4194320 | tf_op jit(solution)/shard_map/all_gather | solution.py:204
  158.0 10.6 %fusion = f32[512,1024]{1,0:T(8,128)} fusion(bf16[512,4096]{0,1:T(8,128)(2,1)} %all-gather.8.cloned.1.call-done, bf16[8192,1024]{1,0:T(8,128)(2,1)} %all-gather.6.cloned.1.call-done), kind=kOutput, calls=%fused_computation.2 | convolution fusion | flops 4294967296 | bytes 14680064 | tf_op jit(solution)/shard_map/dot_general | solution.py:224
  168.6 0.6 broadcast_select_fusion.1
  169.1 2.8 %collective-permute-start.10 = (bf16[16,2,4096]{2,1,0:T(2,128)(2,1)S(1)}, bf16[16,2,4096]{2,1,0:T(2,128)(2,1)S(1)}, u32[]{:S(2)}, u32[]{:S(2)}) collective-permute-start(bf16[16,2,4096]{2,1,0:T(2,128)(2,1)S(1)} %broadcast_select_fusion.1), channel_id=1, source_target_pairs={{0,64},{4,68},{8,72},{12,76},{16,80},{20,84},{24,88},{28,92},{32,9... | collective-permute-start | bytes 786440 | tf_op jit(solution)/shard_map/ppermute | solution.py:101
  171.9 36.3 %all-gather.4.cloned.1.call-done = bf16[512,4096]{0,1:T(8,128)(2,1)} async-done(((bf16[512,1024]{0,1:T(8,128)(2,1)}), bf16[512,4096]{0,1:T(8,128)(2,1)}) %all-gather.4.cloned.1.call-update) | async-done | bytes 4194320 | tf_op jit(solution)/shard_map/all_gather | solution.py:204
  208.2 10.6 %add_convert_fusion = bf16[512,1024]{1,0:T(8,128)(2,1)} fusion(bf16[512,1024]{1,0:T(8,128)(2,1)S(1)} %copy-done.9, f32[512,1024]{1,0:T(8,128)} %fusion, bf16[512,4096]{0,1:T(8,128)(2,1)} %all-gather.4.cloned.1.call-done, bf16[8192,1024]{1,0:T(8,128)(2,1)} %all-gather.6.cloned.1.call-done), kind=kOutput, calls=%fused_computation.20 | convolution fusion | flops 4298113024 | bytes 16777216 | tf_op jit(solution)/shard_map/dot_general | solution.py:224
  218.9 2.3 multiply_reduce_fusion.2
  221.2 2.1 reshape.943
  223.4 2.7 %fusion.96 = f32[64,256]{1,0:T(8,128)} fusion(bf16[4096,256]{1,0:T(8,128)(2,1)} %param.24, f32[64,4096]{1,0:T(8,128)S(1)} %reshape.943, f32[4096]{0:T(1024)S(1)} %copy-done.12, f32[64]{0:T(128)S(1)} %rsqrt.30), kind=kOutput, calls=%fused_computation.155 | convolution fusion | flops 135004160 | bytes 3227904 | tf_op jit(solution)/shard_map/dot_general | solution.py:220
  (174 shorter events, 20.6 us)
Async XLA Ops:
  7.2 1.6 copy-start
  7.2 108.2 %all-gather.6.cloned.1.call-start = ((), (), s32[]{:S(2)}) async-start(), calls=%async_computation.3 | async-start | bytes 17301504 | tf_op jit(solution)/shard_map/all_gather | solution.py:143
  13.8 3.3 %copy-start.10 = (bf16[128,2048]{1,0:T(8,128)(2,1)S(1)}, bf16[128,2048]{1,0:T(8,128)(2,1)}, u32[]{:S(2)}) copy-start(bf16[128,2048]{1,0:T(8,128)(2,1)} %param.14) | copy-start | bytes 1572868
  13.8 3.7 %copy-start.11 = (bf16[128,128]{1,0:T(8,128)(2,1)S(1)}, bf16[128,128]{1,0:T(8,128)(2,1)}, u32[]{:S(2)}) copy-start(bf16[128,128]{1,0:T(8,128)(2,1)} %param.16) | copy-start | bytes 98308
  19.7 1.5 copy-start.7
  21.1 1.4 copy-start.8
  22.6 5.2 %copy-start.16 = (s32[1,2]{1,0:T(1,128)S(1)}, s32[1,2]{1,0:T(1,128)}, u32[]{:S(2)}) copy-start(s32[1,2]{1,0:T(1,128)} %param.25) | copy-start | bytes 28
  22.6 9.4 %copy-start.13 = (f32[128]{0:T(128)S(1)}, f32[128]{0:T(128)}, u32[]{:S(2)}) copy-start(f32[128]{0:T(128)} %param.17) | copy-start | bytes 1540
  22.6 9.5 %copy-start.14 = (f32[128]{0:T(128)S(1)}, f32[128]{0:T(128)}, u32[]{:S(2)}) copy-start(f32[128]{0:T(128)} %param.18) | copy-start | bytes 1540
  22.6 9.5 %copy-start.15 = (f32[128]{0:T(128)S(1)}, f32[128]{0:T(128)}, u32[]{:S(2)}) copy-start(f32[128]{0:T(128)} %param.19) | copy-start | bytes 1540
  22.6 34.2 %all-to-all-start = ((bf16[4,128,2320]{1,2,0:T(8,128)(2,1)}), bf16[4,128,2320]{1,2,0:T(8,128)(2,1)}, u32[]{:S(2)}, u32[]{:S(2)}) async-start(bf16[4,128,2320]{1,2,0:T(8,128)(2,1)} %copy-done.7), calls=%async_computation | async-start | bytes 4751360 | tf_op jit(solution)/shard_map/all_to_all | solution.py:165
  56.8 32.3 %all-to-all-start.1 = ((bf16[4,128,2320]{1,2,0:T(8,128)(2,1)}), bf16[4,128,2320]{1,2,0:T(8,128)(2,1)}, u32[]{:S(2)}, u32[]{:S(2)}) async-start(bf16[4,128,2320]{1,2,0:T(8,128)(2,1)} %copy-done.8), calls=%async_computation.1 | async-start | bytes 4751360 | tf_op jit(solution)/shard_map/all_to_all | solution.py:165
  61.3 96.7 %all-gather.8.cloned.1.call-start = ((), (), s32[]{:S(2)}) async-start(), calls=%async_computation.4 | async-start | bytes 5242880 | tf_op jit(solution)/shard_map/all_gather | solution.py:204
  63.6 1.5 copy-start.4
  67.3 2.3 copy-start.5
  91.0 1.4 copy-start.2
  94.6 2.0 copy-start.3
  106.0 3.7 %copy-start.6 = (bf16[512,1024]{0,1:T(8,128)(2,1)S(1)}, bf16[512,1024]{0,1:T(8,128)(2,1)}, u32[]{:S(2)}) copy-start(bf16[512,1024]{0,1:T(8,128)(2,1)} %multiply_convert_fusion.1) | copy-start | bytes 3145732
  107.3 101.0 %all-gather.4.cloned.1.call-start = ((), (), s32[]{:S(2)}) async-start(), calls=%async_computation.2 | async-start | bytes 5242880 | tf_op jit(solution)/shard_map/all_gather | solution.py:204
  110.1 3.8 %collective-permute-start = (bf16[2,2,1024]{2,0,1:T(2,128)(2,1)S(1)}, bf16[2,2,1024]{2,0,1:T(2,128)(2,1)S(1)}, u32[]{:S(2)}, u32[]{:S(2)}) collective-permute-start(bf16[2,2,1024]{2,0,1:T(2,128)(2,1)S(1)} %pad_maximum_fusion.2), channel_id=1, source_target_pairs={{0,1},{1,2},{2,3},{3,0},{4,5},{5,6},{6,7},{7,4},{8,9},{9,10},{10,1... | collective-permute-start | bytes 24584 | tf_op jit(solution)/shard_map/ppermute | solution.py:90
  110.4 4.0 %collective-permute-start.1 = (bf16[2,2,1024]{2,0,1:T(2,128)(2,1)S(1)}, bf16[2,2,1024]{2,0,1:T(2,128)(2,1)S(1)}, u32[]{:S(2)}, u32[]{:S(2)}) collective-permute-start(bf16[2,2,1024]{2,0,1:T(2,128)(2,1)S(1)} %pad_maximum_fusion.2), channel_id=1, source_target_pairs={{0,2},{1,3},{2,0},{3,1},{4,6},{5,7},{6,4},{7,5},{8,10},{9,11},{10,... | collective-permute-start | bytes 24584 | tf_op jit(solution)/shard_map/ppermute | solution.py:90
  112.2 2.5 %collective-permute-start.2 = (bf16[2,2,1024]{2,0,1:T(2,128)(2,1)S(1)}, bf16[2,2,1024]{2,0,1:T(2,128)(2,1)S(1)}, u32[]{:S(2)}, u32[]{:S(2)}) collective-permute-start(bf16[2,2,1024]{2,0,1:T(2,128)(2,1)S(1)} %pad_maximum_fusion.2), channel_id=1, source_target_pairs={{0,3},{1,0},{2,1},{3,2},{4,7},{5,4},{6,5},{7,6},{8,11},{9,8},{10,9... | collective-permute-start | bytes 24584 | tf_op jit(solution)/shard_map/ppermute | solution.py:90
  115.4 9.0 %copy-start.9 = (bf16[512,1024]{1,0:T(8,128)(2,1)S(1)}, bf16[512,1024]{1,0:T(8,128)(2,1)}, u32[]{:S(2)}) copy-start(bf16[512,1024]{1,0:T(8,128)(2,1)} %param.21) | copy-start | bytes 3145732
  124.7 4.3 %collective-permute-start.3 = (bf16[2,1024]{1,0:T(2,128)(2,1)S(1)}, bf16[2,1024]{1,0:T(2,128)(2,1)S(1)}, u32[]{:S(2)}, u32[]{:S(2)}) collective-permute-start(bf16[2,1024]{1,0:T(2,128)(2,1)S(1)} %fusion.80), channel_id=1, source_target_pairs={{0,1},{1,2},{2,3},{3,0},{4,5},{5,6},{6,7},{7,4},{8,9},{9,10},{10,1... | collective-permute-start | bytes 12296 | tf_op jit(solution)/shard_map/ppermute | solution.py:90
  126.2 4.2 %collective-permute-start.4 = (bf16[2,1024]{1,0:T(2,128)(2,1)S(1)}, bf16[2,1024]{1,0:T(2,128)(2,1)S(1)}, u32[]{:S(2)}, u32[]{:S(2)}) collective-permute-start(bf16[2,1024]{1,0:T(2,128)(2,1)S(1)} %fusion.80), channel_id=1, source_target_pairs={{0,2},{1,3},{2,0},{3,1},{4,6},{5,7},{6,4},{7,5},{8,10},{9,11},{10,... | collective-permute-start | bytes 12296 | tf_op jit(solution)/shard_map/ppermute | solution.py:90
  127.9 3.1 %collective-permute-start.5 = (bf16[2,1024]{1,0:T(2,128)(2,1)S(1)}, bf16[2,1024]{1,0:T(2,128)(2,1)S(1)}, u32[]{:S(2)}, u32[]{:S(2)}) collective-permute-start(bf16[2,1024]{1,0:T(2,128)(2,1)S(1)} %fusion.80), channel_id=1, source_target_pairs={{0,3},{1,0},{2,1},{3,2},{4,7},{5,4},{6,5},{7,6},{8,11},{9,8},{10,9... | collective-permute-start | bytes 12296 | tf_op jit(solution)/shard_map/ppermute | solution.py:90
  131.7 6.3 %collective-permute-start.6 = (bf16[1,2,4096]{2,1,0:T(2,128)(2,1)S(1)}, bf16[1,2,4096]{2,1,0:T(2,128)(2,1)S(1)}, u32[]{:S(2)}, u32[]{:S(2)}) collective-permute-start(bf16[1,2,4096]{2,1,0:T(2,128)(2,1)S(1)} %bitcast.531), channel_id=1, source_target_pairs={{0,4},{4,0},{8,12},{12,8},{16,20},{20,16},{24,28},{28,24},{32,36},... | collective-permute-start | bytes 49160 | tf_op jit(solution)/shard_map/ppermute | solution.py:101
  138.1 3.4 %collective-permute-start.7 = (bf16[2,2,4096]{2,1,0:T(2,128)(2,1)S(1)}, bf16[2,2,4096]{2,1,0:T(2,128)(2,1)S(1)}, u32[]{:S(2)}, u32[]{:S(2)}) collective-permute-start(bf16[2,2,4096]{2,1,0:T(2,128)(2,1)S(1)} %broadcast_select_fusion.5), channel_id=1, source_target_pairs={{0,8},{4,12},{8,0},{12,4},{16,24},{20,28},{24,16},{28,20},{32,40},... | collective-permute-start | bytes 98312 | tf_op jit(solution)/shard_map/ppermute | solution.py:101
  141.6 5.1 %collective-permute-start.8 = (bf16[4,2,4096]{2,1,0:T(2,128)(2,1)S(1)}, bf16[4,2,4096]{2,1,0:T(2,128)(2,1)S(1)}, u32[]{:S(2)}, u32[]{:S(2)}) collective-permute-start(bf16[4,2,4096]{2,1,0:T(2,128)(2,1)S(1)} %broadcast_select_fusion.3), channel_id=1, source_target_pairs={{0,16},{4,20},{8,24},{12,28},{16,0},{20,4},{24,8},{28,12},{32,48},... | collective-permute-start | bytes 196616 | tf_op jit(solution)/shard_map/ppermute | solution.py:101
  147.0 21.5 %collective-permute-start.9 = (bf16[8,2,4096]{2,1,0:T(2,128)(2,1)S(1)}, bf16[8,2,4096]{2,1,0:T(2,128)(2,1)S(1)}, u32[]{:S(2)}, u32[]{:S(2)}) collective-permute-start(bf16[8,2,4096]{2,1,0:T(2,128)(2,1)S(1)} %broadcast_select_fusion.2), channel_id=1, source_target_pairs={{0,32},{4,36},{8,40},{12,44},{16,48},{20,52},{24,56},{28,60},{32,0... | collective-permute-start | bytes 393224 | tf_op jit(solution)/shard_map/ppermute | solution.py:101
  169.1 49.7 %collective-permute-start.10 = (bf16[16,2,4096]{2,1,0:T(2,128)(2,1)S(1)}, bf16[16,2,4096]{2,1,0:T(2,128)(2,1)S(1)}, u32[]{:S(2)}, u32[]{:S(2)}) collective-permute-start(bf16[16,2,4096]{2,1,0:T(2,128)(2,1)S(1)} %broadcast_select_fusion.1), channel_id=1, source_target_pairs={{0,64},{4,68},{8,72},{12,76},{16,80},{20,84},{24,88},{28,92},{32,9... | collective-permute-start | bytes 786440 | tf_op jit(solution)/shard_map/ppermute | solution.py:101
  218.9 4.5 %copy-start.12 = (f32[4096]{0:T(1024)S(1)}, f32[4096]{0:T(1024)}, u32[]{:S(2)}) copy-start(f32[4096]{0:T(1024)} %param.23) | copy-start | bytes 49156
  221.2 5.0 %copy-start.1 = (bf16[256,4096]{1,0:T(8,128)(2,1)S(1)}, bf16[256,4096]{1,0:T(8,128)(2,1)}, u32[]{:S(2)}) copy-start(bf16[256,4096]{1,0:T(8,128)(2,1)} %param.22) | copy-start | bytes 6291460
Sparse Core Ops, SparseCore 0:
  10.2 76.2 all-gather.5
  107.4 50.5 all-gather.7
  159.7 48.5 all-gather.3

commit v12 on v11

--- a/solution.py
+++ b/solution.py
@@ -223,7 +223,10 @@
     for half in range(groups):
         part = jnp.dot(gated_parts[half], w_blocks[half].reshape(-1, width),
                        preferred_element_type=jnp.float32)
-        mixer_f32 = part if mixer_f32 is None else mixer_f32 + part
+        if mixer_f32 is None:
+            mixer_f32 = lax.optimization_barrier(part)
+        else:
+            mixer_f32 = mixer_f32 + part
     mixer = mixer_f32.astype(jnp.bfloat16)
     layer_out = (resid.astype(jnp.float32) + mixer.astype(jnp.float32)).astype(jnp.bfloat16)
     return (layer_out, logits)

time: 233 us -> 228 us (0.979)
  waiting for transfers between devices: 85.6 us -> 78.6 us
  local copies, waits for them, and re-layouts: 29.8 us -> 33.9 us
  starting transfers between devices: 31.7 us -> 28.1 us
    all_gather x2, waiting for transfers between devices: 45.7 us -> 34.5 us  [mixer_layer(): gated_parts.append(lax.all_gather(gated, 'seq', axis=1, tiled=True))]
    ppermute x6, waiting for transfers between devices: 4.1 us -> 8.39 us  [gather_by_shifts(): parts.append(lax.ppermute(value, axis, perm=pairs))]
    ppermute x6, starting transfers between devices: 6.81 us -> 3.57 us  [gather_by_shifts(): parts.append(lax.ppermute(value, axis, perm=pairs))]
    unnamed x41 -> x39, local copies, waits for them, and re-layouts: 17.5 us -> 20 us
  transfers between devices with their start and end apart: 16 -> 16, of which waited for: 13 -> 12; matrix products, arithmetic and copies ran while one was open for 35% -> 39% of each run, Pallas kernels for 0% -> 0%
where the time goes in v12:
time: 228 us; the launch traced here: 227 us
  waiting for transfers between devices  78.6 us (34%)
  matrix products  53.4 us (23%)
  local copies, waits for them, and re-layouts  33.9 us (15%)
  starting transfers between devices  28.1 us (12%)
  between operations  17.6 us (8%)
  other arithmetic  15.6 us (7%)
    all_gather x2, waiting for transfers between devices, mixer_layer(): gated_parts.append(lax.all_gather(gated, 'seq', axis=1, tiled=True))  34.5 us
    all_to_all x2, waiting for transfers between devices, mixer_layer(): lax.all_to_all(packed, 'seq', split_axis=0, concat_axis=0, tiled=True)  31.5 us
    dot_general x2, matrix products, mixer_layer(): jnp.dot(gated_parts[half], w_blocks[half].reshape(-1, width), preferred_e...  21.2 us
    unnamed x39, local copies, waits for them, and re-layouts  20 us
    ppermute x5, starting transfers between devices, gather_by_doubling(): other = lax.ppermute(acc, axis, perm=pairs)  14.6 us
    all_to_all x2, starting transfers between devices, mixer_layer(): lax.all_to_all(packed, 'seq', split_axis=0, concat_axis=0, tiled=True)  9.66 us
    ppermute x6, waiting for transfers between devices, gather_by_shifts(): parts.append(lax.ppermute(value, axis, perm=pairs))  8.39 us
    dot_general x1, matrix products, mixer_layer(): jnp.einsum('sthj,hsjo->to', picked, w_blocks, preferred_element_type=jnp....  8.32 us
  transfers between devices with their start and end apart: 16, of which 12 were waited for; matrix products, arithmetic and copies ran while one was open for 39% of the time, Pallas kernels for 0%

profile of v12, /device:TPU:1, one launch (start us, length us, event | category | flops | bytes accessed | tf_op | source)
XLA Modules:
  0.0 227.2 jit_solution(15174913866168755251)
XLA Ops:
  7.2 1.5 copy-done
  8.8 0.9 constant_dynamic-slice_fusion
  9.7 4.1 %copy.413 = bf16[128,8192]{0,1:T(8,128)(2,1)} copy(bf16[128,8192]{1,0:T(8,128)(2,1)} %param.13) | data formatting | bytes 4194304 | tf_op args[0]
  13.8 3.3 %copy.414 = bf16[128,8192]{0,1:T(8,128)(2,1)S(1)} copy(bf16[128,8192]{1,0:T(8,128)(2,1)} %param.15) | data formatting | bytes 4194304 | tf_op args[2]
  17.6 2.9 %fusion.84 = (bf16[4,128,2320]{1,2,0:T(8,128)(2,1)}, bf16[4,128,2320]{1,2,0:T(8,128)(2,1)S(1)}) fusion(bf16[128,2,4,1024]{0,3,2,1:T(8,128)(2,1)} %bitcast.491), kind=kLoop, calls=%fused_computation.122 | loop fusion | bytes 4194304
  20.5 1.4 fusion.83
  21.9 0.7 fusion.178
  22.6 0.7 fusion.177
  23.3 0.6 constant_dynamic-update-slice_fusion.1
  23.9 1.5 copy-done.7
  25.3 5.1 %all-to-all-start = ((bf16[4,128,2320]{1,2,0:T(8,128)(2,1)}), bf16[4,128,2320]{1,2,0:T(8,128)(2,1)}, u32[]{:S(2)}, u32[]{:S(2)}) async-start(bf16[4,128,2320]{1,2,0:T(8,128)(2,1)} %copy-done.7), calls=%async_computation | async-start | bytes 4751360 | tf_op jit(solution)/shard_map/all_to_all | solution.py:165
  30.8 0.6 fusion.321
  34.6 0.7 fusion.319
  35.3 1.8 slice_convert_fusion
  37.4 22.2 %all-to-all-done = bf16[4,128,2320]{1,2,0:T(8,128)(2,1)} async-done(((bf16[4,128,2320]{1,2,0:T(8,128)(2,1)}), bf16[4,128,2320]{1,2,0:T(8,128)(2,1)}, u32[]{:S(2)}, u32[]{:S(2)}) %all-to-all-start) | async-done | bytes 2375712 | tf_op jit(solution)/shard_map/all_to_all | solution.py:165
  59.6 4.5 %all-to-all-start.1 = ((bf16[4,128,2320]{1,2,0:T(8,128)(2,1)}), bf16[4,128,2320]{1,2,0:T(8,128)(2,1)}, u32[]{:S(2)}, u32[]{:S(2)}) async-start(bf16[4,128,2320]{1,2,0:T(8,128)(2,1)} %get-tuple-element.243), calls=%async_computation.1 | async-start | bytes 4751360 | tf_op jit(solution)/shard_map/all_to_all | solution.py:165
  64.1 2.1 copy_bitcast_fusion.1
  66.2 1.4 copy-done.4
  70.0 1.6 subtract_convert_fusion.27
  73.0 0.6 fusion.59
  78.2 0.6 fusion.65
  79.4 0.6 fusion.63
  80.0 0.6 fusion.61
  80.6 0.7 multiply_reduce_fusion.1
  81.3 1.2 multiply_convert_fusion.1
  82.5 9.3 %all-to-all-done.1 = bf16[4,128,2320]{1,2,0:T(8,128)(2,1)} async-done(((bf16[4,128,2320]{1,2,0:T(8,128)(2,1)}), bf16[4,128,2320]{1,2,0:T(8,128)(2,1)}, u32[]{:S(2)}, u32[]{:S(2)}) %all-to-all-start.1) | async-done | bytes 2375712 | tf_op jit(solution)/shard_map/all_to_all | solution.py:165
  91.8 1.8 copy_bitcast_fusion
  93.7 1.5 copy-done.2
  96.8 1.0 fusion.205
  97.7 1.0 fusion.253
  98.7 1.0 fusion.243
  100.0 1.3 fusion.316
  101.9 1.4 subtract_convert_fusion.21
  109.7 0.6 fusion.71
  110.4 0.6 fusion.69
  111.0 0.6 fusion.67
  111.6 0.7 multiply_reduce_fusion
  112.3 1.3 multiply_convert_fusion
  113.6 1.7 fusion.82
  115.8 0.9 collective-permute-start.2
  116.7 1.2 collective-permute-start.1
  117.9 0.9 collective-permute-done.2
  118.8 2.3 %collective-permute-done.1 = bf16[2,2,1024]{2,0,1:T(2,128)(2,1)S(1)} collective-permute-done((bf16[2,2,1024]{2,0,1:T(2,128)(2,1)S(1)}, bf16[2,2,1024]{2,0,1:T(2,128)(2,1)S(1)}, u32[]{:S(2)}, u32[]{:S(2)}) %collective-permute-start.1) | collective-permute-done | bytes 8224 | tf_op jit(solution)/shard_map/ppermute | solution.py:90
  121.1 1.2 collective-permute-done
  122.4 0.6 gather_fusion
  123.0 8.3 %fusion.79 = f32[2,1024]{1,0:T(2,128)S(1)} fusion(bf16[2,4,1024,1024]{3,2,1,0:T(8,128)(2,1)} %bitcast.489, bf16[4,2,2,1024]{3,1,2,0:T(2,128)(2,1)S(1)} %gather_fusion, pred[4]{0:T(512)(128)(4,1)S(1)} %compare_and_fusion), kind=kOutput, calls=%fused_computation.113 | convolution fusion | flops 33574912 | bytes 16818180 | tf_op jit(solution)/shard_map/sthj,hsjo->to/dot_general | solution.py:211
  131.6 0.6 collective-permute-start.5
  133.1 1.6 collective-permute-done.5
  134.7 1.8 collective-permute-done.4
  136.5 0.6 collective-permute-done.3
  137.8 5.3 %collective-permute-start.6 = (bf16[1,2,4096]{2,1,0:T(2,128)(2,1)S(1)}, bf16[1,2,4096]{2,1,0:T(2,128)(2,1)S(1)}, u32[]{:S(2)}, u32[]{:S(2)}) collective-permute-start(bf16[1,2,4096]{2,1,0:T(2,128)(2,1)S(1)} %bitcast.531), channel_id=1, source_target_pairs={{0,4},{4,0},{8,12},{12,8},{16,20},{20,16},{24,28},{28,24},{32,36},... | collective-permute-start | bytes 49160 | tf_op jit(solution)/shard_map/ppermute | solution.py:101
  143.1 0.8 collective-permute-done.6
  144.0 2.0 collective-permute-start.7
  146.0 1.7 collective-permute-done.7
  147.9 3.4 %collective-permute-start.8 = (bf16[4,2,4096]{2,1,0:T(2,128)(2,1)S(1)}, bf16[4,2,4096]{2,1,0:T(2,128)(2,1)S(1)}, u32[]{:S(2)}, u32[]{:S(2)}) collective-permute-start(bf16[4,2,4096]{2,1,0:T(2,128)(2,1)S(1)} %broadcast_select_fusion.3), channel_id=1, source_target_pairs={{0,16},{4,20},{8,24},{12,28},{16,0},{20,4},{24,8},{28,12},{32,48},... | collective-permute-start | bytes 196616 | tf_op jit(solution)/shard_map/ppermute | solution.py:101
  151.3 1.7 collective-permute-done.8
  153.3 1.3 collective-permute-start.9
  154.6 10.6 %fusion.2 = f32[512,1024]{1,0:T(8,128)} fusion(bf16[512,4096]{0,1:T(8,128)(2,1)} %all-gather.4.cloned.1.call-done, bf16[8192,1024]{1,0:T(8,128)(2,1)} %all-gather.6.cloned.1.call-done), kind=kOutput, calls=%fused_computation.4 | convolution fusion | flops 4294967296 | bytes 14680064 | tf_op jit(solution)/shard_map/dot_general | solution.py:224
  165.7 2.5 %collective-permute-start.10 = (bf16[16,2,4096]{2,1,0:T(2,128)(2,1)S(1)}, bf16[16,2,4096]{2,1,0:T(2,128)(2,1)S(1)}, u32[]{:S(2)}, u32[]{:S(2)}) collective-permute-start(bf16[16,2,4096]{2,1,0:T(2,128)(2,1)S(1)} %broadcast_select_fusion.1), channel_id=1, source_target_pairs={{0,64},{4,68},{8,72},{12,76},{16,80},{20,84},{24,88},{28,92},{32,9... | collective-permute-start | bytes 786440 | tf_op jit(solution)/shard_map/ppermute | solution.py:101
  168.2 34.5 %all-gather.8.cloned.1.call-done = bf16[512,4096]{0,1:T(8,128)(2,1)} async-done(((bf16[512,1024]{0,1:T(8,128)(2,1)}), bf16[512,4096]{0,1:T(8,128)(2,1)}) %all-gather.8.cloned.1.call-update) | async-done | bytes 4194320 | tf_op jit(solution)/shard_map/all_gather | solution.py:204
  202.7 10.6 %add_convert_fusion = bf16[512,1024]{1,0:T(8,128)(2,1)} fusion(bf16[512,1024]{1,0:T(8,128)(2,1)S(1)} %copy-done.8, f32[512,1024]{1,0:T(8,128)} %fusion.2, bf16[512,4096]{0,1:T(8,128)(2,1)} %all-gather.8.cloned.1.call-done, bf16[8192,1024]{1,0:T(8,128)(2,1)} %all-gather.6.cloned.1.call-done), kind=kOutput, calls=%fused_computation.20 | convolution fusion | flops 4298113024 | bytes 16777216 | tf_op jit(solution)/shard_map/dot_general | solution.py:224
  213.4 2.3 %multiply_reduce_fusion.2 = (f32[32,2]{1,0:T(8,128)S(1)}, f32[32,2,4096]{2,1,0:T(2,128)}) fusion(bf16[16,2,4096]{2,1,0:T(2,128)(2,1)S(1)} %broadcast_select_fusion.1, bf16[16,2,4096]{2,1,0:T(2,128)(2,1)S(1)} %collective-permute-done.10, pred[]{:T(512)S(6)} %eq.100), kind=kLoop, calls=%fused_computation.128 | loop fusion | flops 1572800 | bytes 1573121 | tf_op jit(solution)/shard_map/reduce_sum | solution.py:218
  215.7 2.1 reshape.943
  217.9 2.7 %fusion.96 = f32[64,256]{1,0:T(8,128)} fusion(bf16[4096,256]{1,0:T(8,128)(2,1)} %param.24, f32[64,4096]{1,0:T(8,128)S(1)} %reshape.943, f32[4096]{0:T(1024)S(1)} %copy-done.11, f32[64]{0:T(128)S(1)} %rsqrt.30), kind=kOutput, calls=%fused_computation.155 | convolution fusion | flops 135004160 | bytes 3227904 | tf_op jit(solution)/shard_map/dot_general | solution.py:220
  (172 shorter events, 22.3 us)
Async XLA Ops:
  7.2 1.6 copy-start
  7.2 115.8 %all-gather.6.cloned.1.call-start = ((), (), s32[]{:S(2)}) async-start(), calls=%async_computation.3 | async-start | bytes 17301504 | tf_op jit(solution)/shard_map/all_gather | solution.py:143
  13.8 3.3 %copy-start.9 = (bf16[128,2048]{1,0:T(8,128)(2,1)S(1)}, bf16[128,2048]{1,0:T(8,128)(2,1)}, u32[]{:S(2)}) copy-start(bf16[128,2048]{1,0:T(8,128)(2,1)} %param.14) | copy-start | bytes 1572868
  13.8 3.7 %copy-start.10 = (bf16[128,128]{1,0:T(8,128)(2,1)S(1)}, bf16[128,128]{1,0:T(8,128)(2,1)}, u32[]{:S(2)}) copy-start(bf16[128,128]{1,0:T(8,128)(2,1)} %param.16) | copy-start | bytes 98308
  23.9 1.5 copy-start.7
  25.3 5.2 %copy-start.15 = (s32[1,2]{1,0:T(1,128)S(1)}, s32[1,2]{1,0:T(1,128)}, u32[]{:S(2)}) copy-start(s32[1,2]{1,0:T(1,128)} %param.25) | copy-start | bytes 28
  25.3 9.1 %copy-start.12 = (f32[128]{0:T(128)S(1)}, f32[128]{0:T(128)}, u32[]{:S(2)}) copy-start(f32[128]{0:T(128)} %param.17) | copy-start | bytes 1540
  25.3 9.2 %copy-start.13 = (f32[128]{0:T(128)S(1)}, f32[128]{0:T(128)}, u32[]{:S(2)}) copy-start(f32[128]{0:T(128)} %param.18) | copy-start | bytes 1540
  25.3 9.2 %copy-start.14 = (f32[128]{0:T(128)S(1)}, f32[128]{0:T(128)}, u32[]{:S(2)}) copy-start(f32[128]{0:T(128)} %param.19) | copy-start | bytes 1540
  25.3 34.2 %all-to-all-start = ((bf16[4,128,2320]{1,2,0:T(8,128)(2,1)}), bf16[4,128,2320]{1,2,0:T(8,128)(2,1)}, u32[]{:S(2)}, u32[]{:S(2)}) async-start(bf16[4,128,2320]{1,2,0:T(8,128)(2,1)} %copy-done.7), calls=%async_computation | async-start | bytes 4751360 | tf_op jit(solution)/shard_map/all_to_all | solution.py:165
  59.6 32.3 %all-to-all-start.1 = ((bf16[4,128,2320]{1,2,0:T(8,128)(2,1)}), bf16[4,128,2320]{1,2,0:T(8,128)(2,1)}, u32[]{:S(2)}, u32[]{:S(2)}) async-start(bf16[4,128,2320]{1,2,0:T(8,128)(2,1)} %get-tuple-element.243), calls=%async_computation.1 | async-start | bytes 4751360 | tf_op jit(solution)/shard_map/all_to_all | solution.py:165
  64.1 90.5 %all-gather.4.cloned.1.call-start = ((), (), s32[]{:S(2)}) async-start(), calls=%async_computation.2 | async-start | bytes 5242880 | tf_op jit(solution)/shard_map/all_gather | solution.py:204
  66.2 1.4 copy-start.4
  69.8 2.2 copy-start.5
  93.7 1.5 copy-start.2
  101.3 101.4 %all-gather.8.cloned.1.call-start = ((), (), s32[]{:S(2)}) async-start(), calls=%async_computation.4 | async-start | bytes 5242880 | tf_op jit(solution)/shard_map/all_gather | solution.py:204
  103.3 1.7 copy-start.3
  112.3 3.1 %copy-start.6 = (bf16[512,1024]{0,1:T(8,128)(2,1)S(1)}, bf16[512,1024]{0,1:T(8,128)(2,1)}, u32[]{:S(2)}) copy-start(bf16[512,1024]{0,1:T(8,128)(2,1)} %multiply_convert_fusion.1) | copy-start | bytes 3145732
  115.8 3.0 %collective-permute-start.2 = (bf16[2,2,1024]{2,0,1:T(2,128)(2,1)S(1)}, bf16[2,2,1024]{2,0,1:T(2,128)(2,1)S(1)}, u32[]{:S(2)}, u32[]{:S(2)}) collective-permute-start(bf16[2,2,1024]{2,0,1:T(2,128)(2,1)S(1)} %pad_maximum_fusion.2), channel_id=1, source_target_pairs={{0,3},{1,0},{2,1},{3,2},{4,7},{5,4},{6,5},{7,6},{8,11},{9,8},{10,9... | collective-permute-start | bytes 24584 | tf_op jit(solution)/shard_map/ppermute | solution.py:90
  116.7 4.4 %collective-permute-start.1 = (bf16[2,2,1024]{2,0,1:T(2,128)(2,1)S(1)}, bf16[2,2,1024]{2,0,1:T(2,128)(2,1)S(1)}, u32[]{:S(2)}, u32[]{:S(2)}) collective-permute-start(bf16[2,2,1024]{2,0,1:T(2,128)(2,1)S(1)} %pad_maximum_fusion.2), channel_id=1, source_target_pairs={{0,2},{1,3},{2,0},{3,1},{4,6},{5,7},{6,4},{7,5},{8,10},{9,11},{10,... | collective-permute-start | bytes 24584 | tf_op jit(solution)/shard_map/ppermute | solution.py:90
  117.9 4.4 %collective-permute-start = (bf16[2,2,1024]{2,0,1:T(2,128)(2,1)S(1)}, bf16[2,2,1024]{2,0,1:T(2,128)(2,1)S(1)}, u32[]{:S(2)}, u32[]{:S(2)}) collective-permute-start(bf16[2,2,1024]{2,0,1:T(2,128)(2,1)S(1)} %pad_maximum_fusion.2), channel_id=1, source_target_pairs={{0,1},{1,2},{2,3},{3,0},{4,5},{5,6},{6,7},{7,4},{8,9},{9,10},{10,1... | collective-permute-start | bytes 24584 | tf_op jit(solution)/shard_map/ppermute | solution.py:90
  123.0 8.3 %copy-start.8 = (bf16[512,1024]{1,0:T(8,128)(2,1)S(1)}, bf16[512,1024]{1,0:T(8,128)(2,1)}, u32[]{:S(2)}) copy-start(bf16[512,1024]{1,0:T(8,128)(2,1)} %param.21) | copy-start | bytes 3145732
  131.6 3.1 %collective-permute-start.5 = (bf16[2,1024]{1,0:T(2,128)(2,1)S(1)}, bf16[2,1024]{1,0:T(2,128)(2,1)S(1)}, u32[]{:S(2)}, u32[]{:S(2)}) collective-permute-start(bf16[2,1024]{1,0:T(2,128)(2,1)S(1)} %fusion.80), channel_id=1, source_target_pairs={{0,3},{1,0},{2,1},{3,2},{4,7},{5,4},{6,5},{7,6},{8,11},{9,8},{10,9... | collective-permute-start | bytes 12296 | tf_op jit(solution)/shard_map/ppermute | solution.py:90
  132.3 4.2 %collective-permute-start.4 = (bf16[2,1024]{1,0:T(2,128)(2,1)S(1)}, bf16[2,1024]{1,0:T(2,128)(2,1)S(1)}, u32[]{:S(2)}, u32[]{:S(2)}) collective-permute-start(bf16[2,1024]{1,0:T(2,128)(2,1)S(1)} %fusion.80), channel_id=1, source_target_pairs={{0,2},{1,3},{2,0},{3,1},{4,6},{5,7},{6,4},{7,5},{8,10},{9,11},{10,... | collective-permute-start | bytes 12296 | tf_op jit(solution)/shard_map/ppermute | solution.py:90
  132.7 4.4 %collective-permute-start.3 = (bf16[2,1024]{1,0:T(2,128)(2,1)S(1)}, bf16[2,1024]{1,0:T(2,128)(2,1)S(1)}, u32[]{:S(2)}, u32[]{:S(2)}) collective-permute-start(bf16[2,1024]{1,0:T(2,128)(2,1)S(1)} %fusion.80), channel_id=1, source_target_pairs={{0,1},{1,2},{2,3},{3,0},{4,5},{5,6},{6,7},{7,4},{8,9},{9,10},{10,1... | collective-permute-start | bytes 12296 | tf_op jit(solution)/shard_map/ppermute | solution.py:90
  137.8 6.1 %collective-permute-start.6 = (bf16[1,2,4096]{2,1,0:T(2,128)(2,1)S(1)}, bf16[1,2,4096]{2,1,0:T(2,128)(2,1)S(1)}, u32[]{:S(2)}, u32[]{:S(2)}) collective-permute-start(bf16[1,2,4096]{2,1,0:T(2,128)(2,1)S(1)} %bitcast.531), channel_id=1, source_target_pairs={{0,4},{4,0},{8,12},{12,8},{16,20},{20,16},{24,28},{28,24},{32,36},... | collective-permute-start | bytes 49160 | tf_op jit(solution)/shard_map/ppermute | solution.py:101
  144.0 3.7 %collective-permute-start.7 = (bf16[2,2,4096]{2,1,0:T(2,128)(2,1)S(1)}, bf16[2,2,4096]{2,1,0:T(2,128)(2,1)S(1)}, u32[]{:S(2)}, u32[]{:S(2)}) collective-permute-start(bf16[2,2,4096]{2,1,0:T(2,128)(2,1)S(1)} %broadcast_select_fusion.5), channel_id=1, source_target_pairs={{0,8},{4,12},{8,0},{12,4},{16,24},{20,28},{24,16},{28,20},{32,40},... | collective-permute-start | bytes 98312 | tf_op jit(solution)/shard_map/ppermute | solution.py:101
  147.9 5.1 %collective-permute-start.8 = (bf16[4,2,4096]{2,1,0:T(2,128)(2,1)S(1)}, bf16[4,2,4096]{2,1,0:T(2,128)(2,1)S(1)}, u32[]{:S(2)}, u32[]{:S(2)}) collective-permute-start(bf16[4,2,4096]{2,1,0:T(2,128)(2,1)S(1)} %broadcast_select_fusion.3), channel_id=1, source_target_pairs={{0,16},{4,20},{8,24},{12,28},{16,0},{20,4},{24,8},{28,12},{32,48},... | collective-permute-start | bytes 196616 | tf_op jit(solution)/shard_map/ppermute | solution.py:101
  153.3 11.9 %collective-permute-start.9 = (bf16[8,2,4096]{2,1,0:T(2,128)(2,1)S(1)}, bf16[8,2,4096]{2,1,0:T(2,128)(2,1)S(1)}, u32[]{:S(2)}, u32[]{:S(2)}) collective-permute-start(bf16[8,2,4096]{2,1,0:T(2,128)(2,1)S(1)} %broadcast_select_fusion.2), channel_id=1, source_target_pairs={{0,32},{4,36},{8,40},{12,44},{16,48},{20,52},{24,56},{28,60},{32,0... | collective-permute-start | bytes 393224 | tf_op jit(solution)/shard_map/ppermute | solution.py:101
  165.7 47.6 %collective-permute-start.10 = (bf16[16,2,4096]{2,1,0:T(2,128)(2,1)S(1)}, bf16[16,2,4096]{2,1,0:T(2,128)(2,1)S(1)}, u32[]{:S(2)}, u32[]{:S(2)}) collective-permute-start(bf16[16,2,4096]{2,1,0:T(2,128)(2,1)S(1)} %broadcast_select_fusion.1), channel_id=1, source_target_pairs={{0,64},{4,68},{8,72},{12,76},{16,80},{20,84},{24,88},{28,92},{32,9... | collective-permute-start | bytes 786440 | tf_op jit(solution)/shard_map/ppermute | solution.py:101
  213.3 4.5 %copy-start.11 = (f32[4096]{0:T(1024)S(1)}, f32[4096]{0:T(1024)}, u32[]{:S(2)}) copy-start(f32[4096]{0:T(1024)} %param.23) | copy-start | bytes 49156
  215.7 5.0 %copy-start.1 = (bf16[256,4096]{1,0:T(8,128)(2,1)S(1)}, bf16[256,4096]{1,0:T(8,128)(2,1)}, u32[]{:S(2)}) copy-start(bf16[256,4096]{1,0:T(8,128)(2,1)} %param.22) | copy-start | bytes 6291460
Sparse Core Ops, SparseCore 0:
  10.2 76.3 all-gather.5
  101.4 50.9 all-gather.3
  154.1 48.5 all-gather.7
